TPU v7x, 32 devices: a whole 2x2x4 slice. The times are simulated.
32 devices in a mesh: region: 4 (over y, x), tile: 8 (over z, core).
Axes of the slice: x: 2, y: 2, z: 4, core: 2. Of those that a mesh axis runs over, the one named last changes fastest.
Arguments:
- estimate: float32 [32, 128, 512], P('region', 'tile'), may hold values from 0.5 to 18
- observed: float32 [32, 16, 32, 512], P('region', 'tile'), may hold values from 0.3 to 3
- tile_offset: int32 [16], P('tile'), may hold values from 0 to 96
- tile_view: int32 [16], P('tile'), may hold values from 0 to 5
- psf_taps: float32 [6, 3, 3, 15], replicated, may hold values from 0.01 to 0.1
- view_weight: float32 [6], replicated, may hold values from 0.5 to 2
Outputs:
- updated: float32 [32, 128, 512], P('region', 'tile')
All inputs are finite; a program needn't handle non-finite values.
Results may differ from a plain program's by a relative error of at most 0.0003.
Values sent between devices are 32-bit elements; how exact they have to be, the bound alone decides.
No kernel may reach another device: no remote copies, remote signals or barrier semaphores. Data moves between devices by JAX's collectives and lax.ppermute only.
A program may use at most 128 MiB of HBM per device.

v0:
```python
import jax
import jax.numpy as jnp
from jax import lax
from jax.sharding import PartitionSpec as P

PRIOR_WEIGHT = 0.25


def with_halo(cells, sides, width):
    for axis, dim in sides:
        count = lax.axis_size(axis)
        ends = count - 1
        head = lax.slice_in_dim(cells, 0, width, axis=dim)
        tail = lax.slice_in_dim(cells, cells.shape[dim] - width, cells.shape[dim], axis=dim)
        cells = jnp.concatenate(
            [
                lax.ppermute(tail, axis, [(i, (i + 1) % count) for i in range(ends)]),
                cells,
                lax.ppermute(head, axis, [((i + 1) % count, i) for i in range(ends)]),
            ],
            axis=dim,
        )
    return cells


def taps_pass(values_in, filters, along, out_length):
    summed = filters[0] * lax.slice_in_dim(values_in, 0, out_length, axis=along)
    for k in range(1, filters.shape[0]):
        summed = summed + filters[k] * lax.slice_in_dim(values_in, k, k + out_length, axis=along)
    return summed


def dense_rows(weighted, weights, tile_offset, block_x, region_rows, depth_cells, tile_rows):
    numerator = jnp.zeros((block_x, region_rows, depth_cells), jnp.float32)
    coverage = jnp.zeros((region_rows,), jnp.float32)
    for j in range(len(weighted)):
        start_row = tile_offset[j]
        current = lax.dynamic_slice_in_dim(numerator, start_row, tile_rows, 1)
        numerator = lax.dynamic_update_slice_in_dim(numerator, current + weighted[j], start_row, 1)
        cover_now = lax.dynamic_slice_in_dim(coverage, start_row, tile_rows, 0)
        coverage = lax.dynamic_update_slice_in_dim(coverage, cover_now + weights[j], start_row, 0)
    return (numerator, coverage)


def on_device(estimate, observed, tile_offset, tile_view, psf_taps, view_weight):
    rim_width = (psf_taps.shape[3] - 1) // 2
    block_x, block_y, depth_cells = estimate.shape
    tile_count = observed.shape[1]
    tile_rows = observed.shape[2]
    view_count = psf_taps.shape[0]
    rank_terms = psf_taps.shape[1]
    group_size = lax.axis_size("tile")
    region_rows = block_y * group_size
    pad_rows = ((0, 0), (rim_width, rim_width), (0, 0))
    rimmed = with_halo(estimate, (("region", 0),), rim_width)
    gathered = lax.all_gather(rimmed, "tile", axis=1, tiled=True)
    gathered = jnp.pad(gathered, pad_rows)
    windows = [
        lax.dynamic_slice_in_dim(gathered, tile_offset[j], tile_rows + 2 * rim_width, 1)
        for j in range(tile_count)
    ]
    view_ids = jnp.arange(view_count, dtype=jnp.int32)
    weighted = []
    weights = []
    for j in range(tile_count):
        selector = (view_ids == tile_view[j]).astype(jnp.float32)
        filters = jnp.sum(selector[:, None, None, None] * psf_taps, 0)
        weight = jnp.sum(selector * view_weight)
        blurred = jnp.zeros((block_x, tile_rows, depth_cells), jnp.float32)
        for q in range(rank_terms):
            partial_value = taps_pass(windows[j], filters[q, 0], 0, block_x)
            partial_value = taps_pass(partial_value, filters[q, 1], 1, tile_rows)
            partial_value = jnp.pad(partial_value, ((0, 0), (0, 0), (rim_width, rim_width)))
            partial_value = taps_pass(partial_value, filters[q, 2], 2, depth_cells)
            blurred = blurred + partial_value
        quotient = observed[:, j] / blurred
        correction = jnp.zeros((block_x, tile_rows, depth_cells), jnp.float32)
        for q in range(rank_terms):
            partial_value = jnp.pad(quotient, ((rim_width, rim_width), (0, 0), (0, 0)))
            partial_value = taps_pass(partial_value, filters[q, 0, ::-1], 0, block_x)
            partial_value = jnp.pad(partial_value, pad_rows)
            partial_value = taps_pass(partial_value, filters[q, 1, ::-1], 1, tile_rows)
            partial_value = jnp.pad(partial_value, ((0, 0), (0, 0), (rim_width, rim_width)))
            partial_value = taps_pass(partial_value, filters[q, 2, ::-1], 2, depth_cells)
            correction = correction + partial_value
        weighted.append(weight * correction)
        weights.append(weight)
    numerator, coverage = dense_rows(
        weighted, weights, tile_offset, block_x, region_rows, depth_cells, tile_rows
    )
    own_numerator, own_coverage = (
        lax.psum_scatter(numerator, "tile", scatter_dimension=1, tiled=True),
        lax.psum_scatter(coverage, "tile", scatter_dimension=0, tiled=True),
    )
    return estimate * (own_numerator + PRIOR_WEIGHT) / (own_coverage[None, :, None] + PRIOR_WEIGHT)


def solution(mesh):
    return jax.shard_map(
        on_device,
        mesh=mesh,
        in_specs=(
            P("region", "tile", None),
            P("region", "tile", None, None),
            P("tile"),
            P("tile"),
            P(),
            P(),
        ),
        out_specs=P("region", "tile", None),
        check_vma=False,
    )
```

profile of v0, /device:TPU:0, one launch (start us, length us, event | category | flops | bytes accessed | tf_op | source)
XLA Modules:
  0.0 553.2 jit_solution(11306587291668121028)
XLA Ops:
  6.5 1.1 fusion.601
  7.6 4.9 collective-permute-start
  12.5 1.3 collective-permute-start.1
  13.8 3.5 collective-permute-done
  17.3 6.9 %collective-permute-done.1 = f32[7,16,512]{2,1,0:T(8,128)S(1)} collective-permute-done((f32[7,16,512]{2,1,0:T(8,128)S(1)}, f32[7,16,512]{2,1,0:T(8,128)S(1)}, u32[]{:S(2)}, u32[]{:S(2)}) %collective-permute-start.1) | collective-permute-done | bytes 229408 | tf_op jit(solution)/shard_map/ppermute | solution.py:19
  24.2 1.9 pad_maximum_fusion
  26.2 1.3 fusion.618
  33.8 1.3 fusion.619
  36.4 2.6 fusion.600
  38.9 0.9 multiply_reduce_fusion
  44.8 0.7 fusion.605
  48.4 0.7 fusion.611
  50.6 36.4 %all-gather.2.cloned.1.call-done = f32[22,128,512]{2,1,0:T(8,128)} async-done(((f32[22,16,512]{2,1,0:T(8,128)}), f32[22,128,512]{2,1,0:T(8,128)}) %all-gather.2.cloned.1.call-update) | async-done | bytes 5767184 | tf_op jit(solution)/shard_map/all_gather | solution.py:56
  86.9 19.1 %multiply_add_fusion.4 = f32[8,46,512]{2,1,0:T(8,128)S(1)} fusion(f32[]{:T(128)} %bitcast.64, f32[]{:T(128)} %bitcast.63, f32[]{:T(128)} %bitcast.62, f32[]{:T(128)} %bitcast.61, f32[]{:T(128)} %bitcast.60, f32[]{:T(128)} %bitcast.59, f32[]{:T(128)} %bitcast.58, f32[]{:T(128)} %bitcast.57, f32[]{:T(128)} %bitcast.56, f32[]{:T(128)} %bitcast.55, ...), kind=kLoop, calls=%fused_computation.314 | loop fusion | flops 5464064 | bytes 6520952 | tf_op jit(solution)/shard_map/add | solution.py:29
  106.0 10.2 %fusion.570 = f32[8,32,512]{2,1,0:T(8,128)S(1)} fusion(f32[8,46,512]{2,1,0:T(8,128)S(1)} %multiply_add_fusion.4, f32[]{:T(128)} %bitcast.78, f32[]{:T(128)} %bitcast.77, f32[]{:T(128)} %bitcast.76, f32[]{:T(128)} %bitcast.75, f32[]{:T(128)} %bitcast.74, f32[]{:T(128)} %bitcast.73, f32[]{:T(128)} %bitcast.72, f32[]{:T(128)} %bitcast.71, f32[]{:T(128)} %bitcast.70, ...), kind=kLoop, calls=%fused_computation.948 | loop fusion | flops 3801088 | bytes 8388668 | tf_op jit(solution)/shard_map/add | solution.py:29
  116.2 12.3 %multiply_add_fusion.3 = f32[8,46,512]{2,1,0:T(8,128)S(1)} fusion(f32[]{:T(128)} %bitcast.109, f32[]{:T(128)} %bitcast.108, f32[]{:T(128)} %bitcast.107, f32[]{:T(128)} %bitcast.106, f32[]{:T(128)} %bitcast.105, f32[]{:T(128)} %bitcast.104, f32[]{:T(128)} %bitcast.103, f32[]{:T(128)} %bitcast.102, f32[]{:T(128)} %bitcast.101, f32[]{:T(128)} %bitcast.100, ...), kind=kLoop, calls=%fused_computation.313 | loop fusion | flops 5464064 | bytes 6520952 | tf_op jit(solution)/shard_map/add | solution.py:29
  128.6 10.1 %fusion.556 = f32[8,32,512]{2,1,0:T(8,128)S(1)} fusion(f32[8,46,512]{2,1,0:T(8,128)S(1)} %multiply_add_fusion.3, f32[]{:T(128)} %bitcast.123, f32[]{:T(128)} %bitcast.122, f32[]{:T(128)} %bitcast.121, f32[]{:T(128)} %bitcast.120, f32[]{:T(128)} %bitcast.119, f32[]{:T(128)} %bitcast.118, f32[]{:T(128)} %bitcast.117, f32[]{:T(128)} %bitcast.116, ...), kind=kLoop, calls=%fused_computation.919 | loop fusion | flops 3801088 | bytes 8388668 | tf_op jit(solution)/shard_map/add | solution.py:29
  138.7 12.5 %multiply_add_fusion.5 = f32[8,46,512]{2,1,0:T(8,128)S(1)} fusion(f32[]{:T(128)} %bitcast.3, f32[]{:T(128)} %bitcast.21, f32[]{:T(128)} %bitcast.20, f32[]{:T(128)} %bitcast.19, f32[]{:T(128)} %bitcast.18, f32[]{:T(128)} %bitcast.17, f32[]{:T(128)} %bitcast.16, f32[]{:T(128)} %bitcast.15, f32[]{:T(128)} %bitcast.14, f32[]{:T(128)} %bitcast.13, f32[]{:T(128)} %bitcast.12, ...), kind=kLoop, calls=%fused_computation.315 | loop fusion | flops 5464064 | bytes 6520952 | tf_op jit(solution)/shard_map/add | solution.py:29
  151.2 10.3 %fusion.584 = f32[8,32,512]{2,1,0:T(8,128)S(1)} fusion(f32[8,46,512]{2,1,0:T(8,128)S(1)} %multiply_add_fusion.5, f32[]{:T(128)} %bitcast.34, f32[]{:T(128)} %bitcast.33, f32[]{:T(128)} %bitcast.32, f32[]{:T(128)} %bitcast.31, f32[]{:T(128)} %bitcast.30, f32[]{:T(128)} %bitcast.29, f32[]{:T(128)} %bitcast.28, f32[]{:T(128)} %bitcast.27, f32[]{:T(128)} %bitcast.26, ...), kind=kLoop, calls=%fused_computation.977 | loop fusion | flops 3801088 | bytes 8388668 | tf_op jit(solution)/shard_map/add | solution.py:29
  161.5 33.7 %fusion.17 = f32[8,32,512]{2,1,0:T(8,128)S(1)} fusion(f32[8,32,512]{2,1,0:T(8,128)S(1)} %fusion.584, f32[8,32,512]{2,1,0:T(8,128)S(1)} %fusion.570, f32[8,32,512]{2,1,0:T(8,128)S(1)} %fusion.556, f32[8,2,32,512]{3,2,1,0:T(8,128)S(1)} %copy-done.2, f32[]{:T(128)} %bitcast.137, f32[]{:T(128)} %bitcast.136, f32[]{:T(128)} %bitcast.135, f32[]{:T(128)} %bitcast.134, ...), kind=kLoop, calls=%fused_computation.334 | loop fusion | flops 11796480 | bytes 2621620 | tf_op jit(solution)/shard_map/div | solution.py:76
  195.1 9.5 %multiply_add_fusion.11 = f32[8,32,512]{2,1,0:T(8,128)S(1)} fusion(f32[8,32,512]{2,1,0:T(8,128)S(1)} %fusion.17, f32[]{:T(128)} %bitcast.50, f32[]{:T(128)} %bitcast.51, f32[]{:T(128)} %bitcast.52, f32[]{:T(128)} %bitcast.53, f32[]{:T(128)} %bitcast.54, f32[]{:T(128)} %bitcast.55, f32[]{:T(128)} %bitcast.56, f32[]{:T(128)} %bitcast.57, f32[]{:T(128)} %bitcast.58, ...), kind=kLoop, calls=%fused_computation.1010 | loop fusion | flops 3801088 | bytes 1048636 | tf_op jit(solution)/shard_map/add | solution.py:29
  204.6 9.5 %multiply_add_fusion.12 = f32[8,32,512]{2,1,0:T(8,128)S(1)} fusion(f32[8,32,512]{2,1,0:T(8,128)S(1)} %fusion.17, f32[]{:T(128)} %bitcast.7, f32[]{:T(128)} %bitcast.9, f32[]{:T(128)} %bitcast.10, f32[]{:T(128)} %bitcast.11, f32[]{:T(128)} %bitcast.12, f32[]{:T(128)} %bitcast.13, f32[]{:T(128)} %bitcast.14, f32[]{:T(128)} %bitcast.15, f32[]{:T(128)} %bitcast.16, ...), kind=kLoop, calls=%fused_computation.1011 | loop fusion | flops 3801088 | bytes 1048636 | tf_op jit(solution)/shard_map/add | solution.py:29
  214.2 9.8 %multiply_add_fusion.10 = f32[8,32,512]{2,1,0:T(8,128)S(1)} fusion(f32[8,32,512]{2,1,0:T(8,128)S(1)} %fusion.17, f32[]{:T(128)} %bitcast.95, f32[]{:T(128)} %bitcast.96, f32[]{:T(128)} %bitcast.97, f32[]{:T(128)} %bitcast.98, f32[]{:T(128)} %bitcast.99, f32[]{:T(128)} %bitcast.100, f32[]{:T(128)} %bitcast.101, f32[]{:T(128)} %bitcast.102, f32[]{:T(128)} %bitcast.103, ...), kind=kLoop, calls=%fused_computation.1009 | loop fusion | flops 3801088 | bytes 1048636 | tf_op jit(solution)/shard_map/add | solution.py:29
  223.9 12.3 %multiply_add_fusion.2 = f32[8,46,512]{2,1,0:T(8,128)S(1)} fusion(f32[]{:T(128)} %bitcast.142, f32[]{:T(128)} %bitcast.159, f32[]{:T(128)} %bitcast.158, f32[]{:T(128)} %bitcast.157, f32[]{:T(128)} %bitcast.156, f32[]{:T(128)} %bitcast.155, f32[]{:T(128)} %bitcast.154, f32[]{:T(128)} %bitcast.153, f32[]{:T(128)} %bitcast.152, f32[]{:T(128)} %bitcast.151, ...), kind=kLoop, calls=%fused_computation.312 | loop fusion | flops 5464064 | bytes 6520952 | tf_op jit(solution)/shard_map/add | solution.py:29
  236.2 10.3 %fusion.542 = f32[8,32,512]{2,1,0:T(8,128)S(1)} fusion(f32[8,46,512]{2,1,0:T(8,128)S(1)} %multiply_add_fusion.2, f32[]{:T(128)} %bitcast.172, f32[]{:T(128)} %bitcast.171, f32[]{:T(128)} %bitcast.170, f32[]{:T(128)} %bitcast.169, f32[]{:T(128)} %bitcast.168, f32[]{:T(128)} %bitcast.167, f32[]{:T(128)} %bitcast.166, f32[]{:T(128)} %bitcast.165, ...), kind=kLoop, calls=%fused_computation.890 | loop fusion | flops 3801088 | bytes 8388668 | tf_op jit(solution)/shard_map/add | solution.py:29
  246.5 12.3 %multiply_add_fusion.1 = f32[8,46,512]{2,1,0:T(8,128)S(1)} fusion(f32[]{:T(128)} %bitcast.202, f32[]{:T(128)} %bitcast.201, f32[]{:T(128)} %bitcast.200, f32[]{:T(128)} %bitcast.199, f32[]{:T(128)} %bitcast.198, f32[]{:T(128)} %bitcast.197, f32[]{:T(128)} %bitcast.196, f32[]{:T(128)} %bitcast.195, f32[]{:T(128)} %bitcast.194, f32[]{:T(128)} %bitcast.193, ...), kind=kLoop, calls=%fused_computation.311 | loop fusion | flops 5464064 | bytes 6520952 | tf_op jit(solution)/shard_map/add | solution.py:29
  258.8 10.4 %fusion.528 = f32[8,32,512]{2,1,0:T(8,128)S(1)} fusion(f32[8,46,512]{2,1,0:T(8,128)S(1)} %multiply_add_fusion.1, f32[]{:T(128)} %bitcast.216, f32[]{:T(128)} %bitcast.215, f32[]{:T(128)} %bitcast.214, f32[]{:T(128)} %bitcast.213, f32[]{:T(128)} %bitcast.212, f32[]{:T(128)} %bitcast.211, f32[]{:T(128)} %bitcast.210, f32[]{:T(128)} %bitcast.209, ...), kind=kLoop, calls=%fused_computation.861 | loop fusion | flops 3801088 | bytes 8388668 | tf_op jit(solution)/shard_map/add | solution.py:29
  269.2 24.3 %multiply_add_fusion = f32[8,46,512]{2,1,0:T(8,128)S(1)} fusion(f32[]{:T(128)} %bitcast.247, f32[]{:T(128)} %bitcast.246, f32[]{:T(128)} %bitcast.245, f32[]{:T(128)} %bitcast.244, f32[]{:T(128)} %bitcast.243, f32[]{:T(128)} %bitcast.242, f32[]{:T(128)} %bitcast.241, f32[]{:T(128)} %bitcast.240, f32[]{:T(128)} %bitcast.239, f32[]{:T(128)} %bitcast.238, ...), kind=kLoop, calls=%fused_computation.310 | loop fusion | flops 5464064 | bytes 6520952 | tf_op jit(solution)/shard_map/add | solution.py:29
  293.5 10.1 %fusion.514 = f32[8,32,512]{2,1,0:T(8,128)S(1)} fusion(f32[8,46,512]{2,1,0:T(8,128)S(1)} %multiply_add_fusion, f32[]{:T(128)} %bitcast.261, f32[]{:T(128)} %bitcast.260, f32[]{:T(128)} %bitcast.259, f32[]{:T(128)} %bitcast.258, f32[]{:T(128)} %bitcast.257, f32[]{:T(128)} %bitcast.256, f32[]{:T(128)} %bitcast.255, f32[]{:T(128)} %bitcast.254, f32[]{:T(128)} %bitcast.253, ...), kind=kLoop, calls=%fused_computation.832 | loop fusion | flops 3801088 | bytes 8388668 | tf_op jit(solution)/shard_map/add | solution.py:29
  303.6 34.0 %fusion.190 = f32[8,32,512]{2,1,0:T(8,128)S(1)} fusion(f32[8,32,512]{2,1,0:T(8,128)S(1)} %fusion.542, f32[8,32,512]{2,1,0:T(8,128)S(1)} %fusion.528, f32[8,32,512]{2,1,0:T(8,128)S(1)} %fusion.514, f32[8,2,32,512]{3,2,1,0:T(8,128)S(1)} %copy-done.2, f32[]{:T(128)} %bitcast.275, f32[]{:T(128)} %bitcast.274, f32[]{:T(128)} %bitcast.273, f32[]{:T(128)} %bitcast.272, ...), kind=kLoop, calls=%fused_computation.507 | loop fusion | flops 11796480 | bytes 2621620 | tf_op jit(solution)/shard_map/div | solution.py:76
  337.6 9.8 %multiply_add_fusion.8 = f32[8,32,512]{2,1,0:T(8,128)S(1)} fusion(f32[8,32,512]{2,1,0:T(8,128)S(1)} %fusion.190, f32[]{:T(128)} %bitcast.188, f32[]{:T(128)} %bitcast.189, f32[]{:T(128)} %bitcast.190, f32[]{:T(128)} %bitcast.191, f32[]{:T(128)} %bitcast.192, f32[]{:T(128)} %bitcast.193, f32[]{:T(128)} %bitcast.194, f32[]{:T(128)} %bitcast.195, ...), kind=kLoop, calls=%fused_computation.1007 | loop fusion | flops 3801088 | bytes 1048636 | tf_op jit(solution)/shard_map/add | solution.py:29
  347.4 9.7 %multiply_add_fusion.9 = f32[8,32,512]{2,1,0:T(8,128)S(1)} fusion(f32[8,32,512]{2,1,0:T(8,128)S(1)} %fusion.190, f32[]{:T(128)} %bitcast.146, f32[]{:T(128)} %bitcast.147, f32[]{:T(128)} %bitcast.148, f32[]{:T(128)} %bitcast.149, f32[]{:T(128)} %bitcast.150, f32[]{:T(128)} %bitcast.151, f32[]{:T(128)} %bitcast.152, f32[]{:T(128)} %bitcast.153, ...), kind=kLoop, calls=%fused_computation.1008 | loop fusion | flops 3801088 | bytes 1048636 | tf_op jit(solution)/shard_map/add | solution.py:29
  357.1 10.0 %multiply_add_fusion.7 = f32[8,32,512]{2,1,0:T(8,128)S(1)} fusion(f32[8,32,512]{2,1,0:T(8,128)S(1)} %fusion.190, f32[]{:T(128)} %bitcast.233, f32[]{:T(128)} %bitcast.234, f32[]{:T(128)} %bitcast.235, f32[]{:T(128)} %bitcast.236, f32[]{:T(128)} %bitcast.237, f32[]{:T(128)} %bitcast.238, f32[]{:T(128)} %bitcast.239, f32[]{:T(128)} %bitcast.240, ...), kind=kLoop, calls=%fused_computation.1006 | loop fusion | flops 3801088 | bytes 1048636 | tf_op jit(solution)/shard_map/add | solution.py:29
  367.1 10.1 %fusion.388 = f32[8,32,512]{2,1,0:T(8,128)S(1)} fusion(f32[8,32,512]{2,1,0:T(8,128)S(1)} %multiply_add_fusion.11, f32[]{:T(128)} %bitcast.78, f32[]{:T(128)} %bitcast.77, f32[]{:T(128)} %bitcast.76, f32[]{:T(128)} %bitcast.75, f32[]{:T(128)} %bitcast.74, f32[]{:T(128)} %bitcast.73, f32[]{:T(128)} %bitcast.72, f32[]{:T(128)} %bitcast.71, f32[]{:T(128)} %bitcast.70, ...), kind=kLoop, calls=%fused_computation.705 | loop fusion | flops 3801088 | bytes 1048636 | tf_op jit(solution)/shard_map/add | solution.py:29
  377.2 10.2 %fusion.416 = f32[8,32,512]{2,1,0:T(8,128)S(1)} fusion(f32[8,32,512]{2,1,0:T(8,128)S(1)} %multiply_add_fusion.10, f32[]{:T(128)} %bitcast.123, f32[]{:T(128)} %bitcast.122, f32[]{:T(128)} %bitcast.121, f32[]{:T(128)} %bitcast.120, f32[]{:T(128)} %bitcast.119, f32[]{:T(128)} %bitcast.118, f32[]{:T(128)} %bitcast.117, f32[]{:T(128)} %bitcast.116, ...), kind=kLoop, calls=%fused_computation.733 | loop fusion | flops 3801088 | bytes 1048636 | tf_op jit(solution)/shard_map/add | solution.py:29
  387.4 10.2 %fusion.360 = f32[8,32,512]{2,1,0:T(8,128)S(1)} fusion(f32[8,32,512]{2,1,0:T(8,128)S(1)} %multiply_add_fusion.12, f32[]{:T(128)} %bitcast.34, f32[]{:T(128)} %bitcast.33, f32[]{:T(128)} %bitcast.32, f32[]{:T(128)} %bitcast.31, f32[]{:T(128)} %bitcast.30, f32[]{:T(128)} %bitcast.29, f32[]{:T(128)} %bitcast.28, f32[]{:T(128)} %bitcast.27, f32[]{:T(128)} %bitcast.26, ...), kind=kLoop, calls=%fused_computation.677 | loop fusion | flops 3801088 | bytes 1048636 | tf_op jit(solution)/shard_map/add | solution.py:29
  397.6 10.4 %fusion.472 = f32[8,32,512]{2,1,0:T(8,128)S(1)} fusion(f32[8,32,512]{2,1,0:T(8,128)S(1)} %multiply_add_fusion.8, f32[]{:T(128)} %bitcast.216, f32[]{:T(128)} %bitcast.215, f32[]{:T(128)} %bitcast.214, f32[]{:T(128)} %bitcast.213, f32[]{:T(128)} %bitcast.212, f32[]{:T(128)} %bitcast.211, f32[]{:T(128)} %bitcast.210, f32[]{:T(128)} %bitcast.209, ...), kind=kLoop, calls=%fused_computation.789 | loop fusion | flops 3801088 | bytes 1048636 | tf_op jit(solution)/shard_map/add | solution.py:29
  408.0 10.9 %fusion.500 = f32[8,32,512]{2,1,0:T(8,128)} fusion(f32[8,32,512]{2,1,0:T(8,128)S(1)} %multiply_add_fusion.7, f32[]{:T(128)} %bitcast.261, f32[]{:T(128)} %bitcast.260, f32[]{:T(128)} %bitcast.259, f32[]{:T(128)} %bitcast.258, f32[]{:T(128)} %bitcast.257, f32[]{:T(128)} %bitcast.256, f32[]{:T(128)} %bitcast.255, f32[]{:T(128)} %bitcast.254, f32[]{:T(128)} %bitcast.253, ...), kind=kLoop, calls=%fused_computation.817 | loop fusion | flops 3801088 | bytes 1048636 | tf_op jit(solution)/shard_map/add | solution.py:29
  419.0 11.1 %fusion.444 = f32[8,32,512]{2,1,0:T(8,128)} fusion(f32[8,32,512]{2,1,0:T(8,128)S(1)} %multiply_add_fusion.9, f32[]{:T(128)} %bitcast.172, f32[]{:T(128)} %bitcast.171, f32[]{:T(128)} %bitcast.170, f32[]{:T(128)} %bitcast.169, f32[]{:T(128)} %bitcast.168, f32[]{:T(128)} %bitcast.167, f32[]{:T(128)} %bitcast.166, f32[]{:T(128)} %bitcast.165, f32[]{:T(128)} %bitcast.164, ...), kind=kLoop, calls=%fused_computation.761 | loop fusion | flops 3801088 | bytes 1048636 | tf_op jit(solution)/shard_map/add | solution.py:29
  430.1 34.4 %fusion.598 = f32[8,32,512]{2,1,0:T(8,128)S(1)} fusion(f32[8,32,512]{2,1,0:T(8,128)S(1)} %fusion.416, f32[8,32,512]{2,1,0:T(8,128)S(1)} %fusion.388, f32[8,32,512]{2,1,0:T(8,128)S(1)} %fusion.360, f32[]{:T(128)} %bitcast.137, f32[]{:T(128)} %bitcast.136, f32[]{:T(128)} %bitcast.135, f32[]{:T(128)} %bitcast.134, f32[]{:T(128)} %bitcast.133, f32[]{:T(128)} %bitcast.132, ...), kind=kLoop, calls=%fused_computation.1012 | loop fusion | flops 11796480 | bytes 2097336 | tf_op jit(solution)/shard_map/mul | solution.py:86
  464.7 0.8 dynamic_update_slice.12
  465.5 41.8 %multiply_add_fusion.6 = f32[8,32,512]{2,1,0:T(8,128)S(1)} fusion(f32[8,128,512]{2,1,0:T(8,128)S(1)} %dynamic_update_slice.12, s32[]{:T(128)S(6)} %select_n.18, f32[8,32,512]{2,1,0:T(8,128)} %fusion.500, f32[8,32,512]{2,1,0:T(8,128)S(1)} %fusion.472, f32[8,32,512]{2,1,0:T(8,128)} %fusion.444, f32[]{:T(128)} %bitcast.275, f32[]{:T(128)} %bitcast.274, ...), kind=kLoop, calls=%fused_computation.1005 | loop fusion | flops 11927552 | bytes 2621628 | tf_op jit(solution)/shard_map/add | solution.py:39
  507.3 0.8 dynamic_update_slice.13
  508.0 1.3 copy-done
  511.4 0.8 add_dynamic-update-slice_fusion
  512.2 14.0 %all-reduce.21 = f32[128]{0:T(128)S(1)} all-reduce(f32[128]{0:T(128)S(1)} %add_dynamic-update-slice_fusion), channel_id=3, replica_groups=mesh['region'=4,'tile'=8] {'tile'}, use_global_device_ids=true, to_apply=%region_5.6.clone | all-reduce | flops 128 | bytes 1024
  526.2 18.1 %reduce-scatter.2.cloned.1.call-done = f32[8,16,512]{2,1,0:T(8,128)} async-done(((f32[8,128,512]{2,1,0:T(8,128)}), f32[8,16,512]{2,1,0:T(8,128)}) %reduce-scatter.2.cloned.1.call-update) | async-done | bytes 262160 | tf_op jit(solution)/shard_map/reduce_scatter | solution.py:92
  544.4 1.7 multiply_divide_fusion
  (36 shorter events, 12.2 us)
Async XLA Ops:
  6.5 80.4 %all-gather.2.cloned.1.call-start = ((), (), s32[]{:S(2)}) async-start(), calls=%async_computation.1 | async-start | bytes 6488064 | tf_op jit(solution)/shard_map/all_gather | solution.py:56
  7.6 9.7 %collective-permute-start = (f32[7,16,512]{2,1,0:T(8,128)S(1)}, f32[7,16,512]{2,1,0:T(8,128)S(1)}, u32[]{:S(2)}, u32[]{:S(2)}) collective-permute-start(f32[7,16,512]{2,1,0:T(8,128)S(1)} %get-tuple-element.9), channel_id=1, source_target_pairs={{0,8},{8,16},{16,24},{1,9},{9,17},{17,25},{2,10},{10,18},{18,26},{... | collective-permute-start | bytes 688136 | tf_op jit(solution)/shard_map/ppermute | solution.py:17
  12.5 11.7 %collective-permute-start.1 = (f32[7,16,512]{2,1,0:T(8,128)S(1)}, f32[7,16,512]{2,1,0:T(8,128)S(1)}, u32[]{:S(2)}, u32[]{:S(2)}) collective-permute-start(f32[7,16,512]{2,1,0:T(8,128)S(1)} %get-tuple-element.10), channel_id=1, source_target_pairs={{8,0},{16,8},{24,16},{9,1},{17,9},{25,17},{10,2},{18,10},{26,18},{... | collective-permute-start | bytes 688136 | tf_op jit(solution)/shard_map/ppermute | solution.py:19
  26.1 518.2 %reduce-scatter.2.cloned.1.call-start = ((), (), s32[]{:S(2)}) async-start(), calls=%async_computation.2 | async-start | bytes 2359296 | tf_op jit(solution)/shard_map/reduce_scatter | solution.py:92
  86.9 29.3 %slice-start = ((s8[5767168]{0:T(1024)(128)(4,1)}), s8[4194304]{0:T(1024)(128)(4,1)S(1)}, s32[]{:S(2)}) async-start(s8[5767168]{0:T(1024)(128)(4,1)} %bitcast.283), calls=%async_computation.3 | async-start | bytes 8388608
  106.0 10.2 %slice-start.1 = ((s8[5767168]{0:T(1024)(128)(4,1)}), s8[1572864]{0:T(1024)(128)(4,1)S(1)}, s32[]{:S(2)}) async-start(s8[5767168]{0:T(1024)(128)(4,1)} %bitcast.283), calls=%async_computation.4 | async-start | bytes 3145728
  151.2 10.3 %copy-start.2 = (f32[8,2,32,512]{3,2,1,0:T(8,128)S(1)}, f32[8,2,32,512]{3,2,1,0:T(8,128)}, u32[]{:S(2)}) copy-start(f32[8,2,32,512]{3,2,1,0:T(8,128)} %param.7) | copy-start | bytes 3145732
  430.1 79.3 %copy-start.3 = (u32[32]{0:T(128)S(1)}, u32[32]{0:T(128)}, u32[]{:S(2)}) copy-start(u32[32]{0:T(128)} %constant.63) | copy-start | bytes 388
  430.1 114.3 %copy-start.1 = (f32[8,16,512]{2,1,0:T(8,128)S(1)}, f32[8,16,512]{2,1,0:T(8,128)}, u32[]{:S(2)}) copy-start(f32[8,16,512]{2,1,0:T(8,128)} %param.6) | copy-start | bytes 786436
  508.0 1.3 copy-start
Sparse Core Ops, SparseCore 0:
  26.2 60.6 all-gather.1
  509.5 34.7 reduce-scatter.1
where the time goes:
time: 561 us; the launch traced here: 553 us
  other arithmetic  428 us (76%)
  waiting for transfers between devices  64.9 us (12%)
  between operations  20.9 us (4%)
  local copies, waits for them, and re-layouts  18.9 us (3%)
  blocking collectives  14 us (2%)
  starting transfers between devices  6.19 us (1%)
    add x24, other arithmetic, taps_pass(): summed + filters[k] * lax.slice_in_dim(values_in, k, k + out_length, axis...  275 us
    div x2, other arithmetic, on_device(): quotient = observed[:, j] / blurred  67.7 us
    add x1, other arithmetic, dense_rows(): current + weighted[j]  41.8 us
    all_gather x1, waiting for transfers between devices, on_device(): gathered = lax.all_gather(rimmed, 'tile', axis=1, tiled=True)  36.4 us
    mul x1, other arithmetic, on_device(): weighted.append(weight * correction)  34.4 us
    reduce_scatter x1, waiting for transfers between devices, on_device(): lax.psum_scatter(numerator, 'tile', scatter_dimension=1, tiled=True)  18.1 us
    unnamed x1, blocking collectives  14 us
  transfers between devices with their start and end apart: 4, of which 4 were waited for; matrix products, arithmetic and copies ran while one was open for 4% of the time, Pallas kernels for 0%

commit v1 on v0

v1 whole, which is shorter than its diff:
```python
import jax
import jax.numpy as jnp
from jax import lax
from jax.sharding import PartitionSpec as P

PRIOR_WEIGHT = 0.25
MATMUL_PRECISION = lax.Precision.HIGH


def with_halo(cells, sides, width):
    for axis, dim in sides:
        count = lax.axis_size(axis)
        ends = count - 1
        head = lax.slice_in_dim(cells, 0, width, axis=dim)
        tail = lax.slice_in_dim(cells, cells.shape[dim] - width, cells.shape[dim], axis=dim)
        cells = jnp.concatenate(
            [
                lax.ppermute(tail, axis, [(i, (i + 1) % count) for i in range(ends)]),
                cells,
                lax.ppermute(head, axis, [((i + 1) % count, i) for i in range(ends)]),
            ],
            axis=dim,
        )
    return cells


def band(taps, rows, cols, shift):
    kt = taps.shape[-1]
    i = lax.broadcasted_iota(jnp.int32, (rows, cols), 0)
    j = lax.broadcasted_iota(jnp.int32, (rows, cols), 1)
    d = j - i - jnp.asarray(shift, jnp.int32)[..., None, None]
    out = jnp.zeros(d.shape[:-2] + (rows, cols), jnp.float32)
    out = jnp.broadcast_to(out, taps.shape[:-1] + (rows, cols))
    for k in range(kt):
        out = jnp.where(d == k, taps[..., k, None, None], out)
    return out


def depth_band(taps, depth, block):
    kt = taps.shape[-1]
    half = (kt - 1) // 2
    i = lax.broadcasted_iota(jnp.int32, (3 * block, block), 0)
    j = lax.broadcasted_iota(jnp.int32, (3 * block, block), 1)
    d = i - block - j + half
    strip = jnp.zeros(taps.shape[:-1] + (3 * block, block), jnp.float32)
    for k in range(kt):
        strip = jnp.where(d == k, taps[..., k, None, None], strip)
    nb = depth // block
    lead = taps.shape[:-1]
    cols = []
    for b in range(nb):
        col = jnp.pad(strip, [(0, 0)] * len(lead) + [(b * block, (nb - 1 - b) * block), (0, 0)])
        cols.append(col[..., block : block + depth, :])
    return jnp.concatenate(cols, axis=-1)


def on_device(estimate, observed, tile_offset, tile_view, psf_taps, view_weight):
    kt = psf_taps.shape[3]
    rim = (kt - 1) // 2
    block_x, block_y, depth = estimate.shape
    tile_count = observed.shape[1]
    tile_rows = observed.shape[2]
    rank_terms = psf_taps.shape[1]
    group_size = lax.axis_size("tile")
    region_rows = block_y * group_size
    win_rows = -(-(tile_rows + 2 * rim) // 8) * 8
    win_x = block_x + 2 * rim

    all_offset = lax.all_gather(tile_offset, "tile", tiled=True)
    all_view = lax.all_gather(tile_view, "tile", tiled=True)

    rimmed = with_halo(estimate, (("region", 0),), rim)
    gathered = lax.all_gather(rimmed, "tile", axis=1, tiled=True)

    filters = psf_taps[tile_view]
    weight = view_weight[tile_view]
    ax = filters[:, :, 0]
    ay = filters[:, :, 1]
    az = filters[:, :, 2]

    starts = jnp.clip(tile_offset - rim, 0, region_rows - win_rows)
    shifts = tile_offset - rim - starts
    windows = jnp.stack(
        [lax.dynamic_slice_in_dim(gathered, starts[j], win_rows, 1) for j in range(tile_count)]
    ).reshape(tile_count, win_x * win_rows, depth)

    tx = band(ax, block_x, win_x, 0)
    ty = band(ay, tile_rows, win_rows, shifts[:, None])
    kxy = (tx[:, :, :, None, :, None] * ty[:, :, None, :, None, :]).reshape(
        tile_count, rank_terms * block_x * tile_rows, win_x * win_rows
    )
    tz = depth_band(az, depth, 128)

    cells = block_x * tile_rows
    part = jnp.einsum("tmk,tkz->tmz", kxy, windows, precision=MATMUL_PRECISION)
    part = part.reshape(tile_count, rank_terms, cells, depth)
    blurred = jnp.einsum("tqmz,tqzn->tmn", part, tz, precision=MATMUL_PRECISION)

    quotient = observed.transpose(1, 0, 2, 3).reshape(tile_count, cells, depth) / blurred

    fx = band(ax[..., ::-1], block_x, block_x, -rim)
    fy = band(ay[..., ::-1], tile_rows, tile_rows, -rim)
    fxy = (fx[:, :, :, None, :, None] * fy[:, :, None, :, None, :]).reshape(
        tile_count, rank_terms * cells, cells
    )
    part = jnp.einsum("tmk,tkz->tmz", fxy, quotient, precision=MATMUL_PRECISION)
    part = part.reshape(tile_count, rank_terms, cells, depth)
    correction = jnp.einsum("tqmz,tqnz->tmn", part, tz, precision=MATMUL_PRECISION)
    weighted = (weight[:, None, None] * correction).reshape(tile_count, block_x, tile_rows, depth)

    numerator = jnp.zeros((block_x, region_rows, depth), jnp.float32)
    for j in range(tile_count):
        current = lax.dynamic_slice_in_dim(numerator, tile_offset[j], tile_rows, 1)
        numerator = lax.dynamic_update_slice_in_dim(numerator, current + weighted[j], tile_offset[j], 1)
    own_numerator = lax.psum_scatter(numerator, "tile", scatter_dimension=1, tiled=True)

    me = lax.axis_index("tile")
    rows = me * block_y + jnp.arange(block_y, dtype=jnp.int32)
    inside = (rows[None, :] >= all_offset[:, None]) & (rows[None, :] < all_offset[:, None] + tile_rows)
    own_coverage = jnp.sum(jnp.where(inside, view_weight[all_view][:, None], 0.0), axis=0)
    return estimate * (own_numerator + PRIOR_WEIGHT) / (own_coverage[None, :, None] + PRIOR_WEIGHT)


def solution(mesh):
    return jax.shard_map(
        on_device,
        mesh=mesh,
        in_specs=(
            P("region", "tile", None),
            P("region", "tile", None, None),
            P("tile"),
            P("tile"),
            P(),
            P(),
        ),
        out_specs=P("region", "tile", None),
        check_vma=False,
    )
```

time: 561 us -> 154 us (0.27); the launches traced: 553 us -> 154 us
  other arithmetic: 428 us -> 20 us
  waiting for transfers between devices: 64.9 us -> 41.7 us
  local copies, waits for them, and re-layouts: 18.9 us -> 39.9 us
  matrix products: 0 us -> 17 us
  blocking collectives: 14 us -> 6.99 us
    add x25 -> x2, other arithmetic: 317 us -> 0.12 us  [the longest x1 0.11 us: on_device(): current + weighted[j]]
    div x2 -> x0, other arithmetic: 67.7 us -> none  [on_device(): quotient = observed[:, j] / blurred]
    all_gather x1, waiting for transfers between devices: 36.4 us -> 6.23 us  [on_device(): gathered = lax.all_gather(rimmed, 'tile', axis=1, tiled=True)]
    mul x1 -> x2, other arithmetic: 34.4 us -> 12.7 us  [the longest x1 9.3 us: on_device(): tx[:, :, :, None, :, None] * ty[:, :, None, :, None, :]]
    mul x0 -> x2, local copies, waits for them, and re-layouts: none -> 20.4 us  [the longest x1 15 us: on_device(): tx[:, :, :, None, :, None] * ty[:, :, None, :, None, :]]
    dot_general x0 -> x4, matrix products: none -> 17 us  [the longest x1 8.93 us: on_device(): part = jnp.einsum('tmk,tkz->tmz', kxy, windows, precision=MATMUL_PRECISION)]
    unnamed x1, blocking collectives: 14 us -> 6.99 us
    reduce_scatter x1, waiting for transfers between devices: 18.1 us -> 25 us  [on_device(): lax.psum_scatter(numerator, 'tile', scatter_dimension=1, tiled=True)]
  transfers between devices with their start and end apart: 4 -> 4, of which waited for: 4 -> 4; matrix products, arithmetic and copies ran while one was open for 4% -> 32% of each run, Pallas kernels for 0% -> 0%
where the time goes in v1:
time: 154 us
  waiting for transfers between devices  41.7 us (27%)
  local copies, waits for them, and re-layouts  39.9 us (26%)
  between operations  21.9 us (14%)
  other arithmetic  20 us (13%)
  matrix products  17 us (11%)
  blocking collectives  6.99 us (5%)
  starting transfers between devices  6.19 us (4%)
    reduce_scatter x1, waiting for transfers between devices, on_device(): lax.psum_scatter(numerator, 'tile', scatter_dimension=1, tiled=True)  25 us
    mul x1, local copies, waits for them, and re-layouts, on_device(): tx[:, :, :, None, :, None] * ty[:, :, None, :, None, :]  15 us
    mul x1, other arithmetic, on_device(): tx[:, :, :, None, :, None] * ty[:, :, None, :, None, :]  9.3 us
    dot_general x1, matrix products, on_device(): part = jnp.einsum('tmk,tkz->tmz', kxy, windows, precision=MATMUL_PRECISION)  8.93 us
    unnamed x1, blocking collectives  6.99 us
    ppermute x1, waiting for transfers between devices, with_halo(): lax.ppermute(head, axis, [((i + 1) % count, i) for i in range(ends)])  6.86 us
    all_gather x1, waiting for transfers between devices, on_device(): gathered = lax.all_gather(rimmed, 'tile', axis=1, tiled=True)  6.23 us
    mul x1, local copies, waits for them, and re-layouts, on_device(): fx[:, :, :, None, :, None] * fy[:, :, None, :, None, :]  5.4 us
  transfers between devices with their start and end apart: 4, of which 4 were waited for; matrix products, arithmetic and copies ran while one was open for 32% of the time, Pallas kernels for 0%

profile of v1, /device:TPU:0, one launch (start us, length us, event | category | flops | bytes accessed | tf_op | source)
XLA Modules:
  0.0 153.7 jit_solution(13385739109346607121)
XLA Ops:
  6.5 1.1 fusion.73
  7.7 4.9 %collective-permute-start = (f32[7,16,512]{2,1,0:T(8,128)S(1)}, f32[7,16,512]{2,1,0:T(8,128)S(1)}, u32[]{:S(2)}, u32[]{:S(2)}) collective-permute-start(f32[7,16,512]{2,1,0:T(8,128)S(1)} %get-tuple-element.15), channel_id=1, source_target_pairs={{0,8},{8,16},{16,24},{1,9},{9,17},{17,25},{2,10},{10,18},{18,26},{... | collective-permute-start | bytes 688136 | tf_op jit(solution)/shard_map/ppermute | solution.py:18
  12.5 1.3 collective-permute-start.1
  13.8 3.5 %collective-permute-done = f32[7,16,512]{2,1,0:T(8,128)S(1)} collective-permute-done((f32[7,16,512]{2,1,0:T(8,128)S(1)}, f32[7,16,512]{2,1,0:T(8,128)S(1)}, u32[]{:S(2)}, u32[]{:S(2)}) %collective-permute-start) | collective-permute-done | bytes 229408 | tf_op jit(solution)/shard_map/ppermute | solution.py:18
  17.4 6.9 %collective-permute-done.1 = f32[7,16,512]{2,1,0:T(8,128)S(1)} collective-permute-done((f32[7,16,512]{2,1,0:T(8,128)S(1)}, f32[7,16,512]{2,1,0:T(8,128)S(1)}, u32[]{:S(2)}, u32[]{:S(2)}) %collective-permute-start.1) | collective-permute-done | bytes 229408 | tf_op jit(solution)/shard_map/ppermute | solution.py:20
  24.2 2.0 %pad_maximum_fusion.11 = f32[22,16,512]{2,1,0:T(8,128)} fusion(f32[7,16,512]{2,1,0:T(8,128)S(1)} %collective-permute-done.1, f32[8,16,512]{2,1,0:T(8,128)} %param.6, f32[7,16,512]{2,1,0:T(8,128)S(1)} %collective-permute-done), kind=kLoop, calls=%fused_computation.21 | loop fusion | flops 360448 | bytes 1441792 | tf_op jit(solution)/shard_map/concatenate | solution.py:16
  26.3 0.6 gather_fusion.1
  26.9 0.1 fusion.77
  27.0 0.1 copy.122
  27.1 0.1 copy.123
  27.5 0.1 copy.127
  28.5 0.1 fusion.76
  30.2 0.2 select_select_fusion.3
  30.4 0.1 subtract_compare_fusion.14
  30.5 0.3 select_select_fusion.1
  30.8 9.3 %broadcast_multiply_fusion = f32[2,3,8,32,22,48]{5,4,3,2,1,0:T(8,128)} fusion(f32[2,3,32,48]{3,2,1,0:T(8,128)S(1)} %select_select_fusion.1, f32[2,3,8,22]{3,2,1,0:T(8,128)S(1)} %select_select_fusion.3), kind=kLoop, calls=%fused_computation.3 | loop fusion | flops 1622016 | bytes 6529152 | tf_op jit(solution)/shard_map/mul | solution.py:89
  40.1 15.0 %mul.56 = f32[2,768,1056]{2,1,0:T(8,128)} reshape(f32[2,3,8,32,22,48]{5,4,3,2,1,0:T(8,128)} %broadcast_multiply_fusion) | data formatting | bytes 12976128 | tf_op jit(solution)/shard_map/mul | solution.py:89
  55.1 0.6 fusion.79
  58.3 0.1 fusion.75
  58.4 0.1 copy.140
  59.9 1.2 copy.137
  61.3 0.2 select_select_fusion.4
  61.5 0.2 select_select_fusion.2
  61.8 3.4 %broadcast_multiply_fusion.1 = f32[2,3,8,32,8,32]{5,4,3,2,1,0:T(8,128)} fusion(f32[2,3,32,32]{3,2,1,0:T(8,128)S(1)} %select_select_fusion.2, f32[2,3,8,8]{3,2,1,0:T(8,128)S(1)} %select_select_fusion.4), kind=kLoop, calls=%fused_computation.11 | loop fusion | flops 393216 | bytes 1598976 | tf_op jit(solution)/shard_map/mul | solution.py:103
  65.2 5.4 %mul.52 = f32[2,768,256]{2,1,0:T(8,128)} reshape(f32[2,3,8,32,8,32]{5,4,3,2,1,0:T(8,128)} %broadcast_multiply_fusion.1) | data formatting | bytes 3145728 | tf_op jit(solution)/shard_map/mul | solution.py:103
  70.6 0.6 gather_fusion
  71.2 0.6 fusion.78
  76.6 0.6 fusion.23
  77.2 1.5 select_select_fusion
  78.7 2.1 %pad_slice_fusion.3 = (f32[2,3,512,128]{3,2,1,0:T(8,128)S(1)}, f32[2,3,512,128]{3,2,1,0:T(8,128)S(1)}, f32[2,3,512,128]{3,2,1,0:T(8,128)}, f32[2,3,512,128]{3,2,1,0:T(8,128)}) fusion(f32[2,3,384,128]{3,2,1,0:T(8,128)S(1)} %select_select_fusion), kind=kLoop, calls=%fused_computation.15 | loop fusion | bytes 7471104 | tf_op jit(solution)/shard_map/slice | solution.py:53
  80.8 6.2 %all-gather.2.cloned.1.call-done = f32[22,128,512]{2,1,0:T(8,128)} async-done(((f32[22,16,512]{2,1,0:T(8,128)}), f32[22,128,512]{2,1,0:T(8,128)}) %all-gather.2.cloned.1.call-update) | async-done | bytes 5767184 | tf_op jit(solution)/shard_map/all_gather | solution.py:73
  87.0 3.1 %constant_dynamic-slice_fusion.1 = (f32[22,48,512]{2,1,0:T(8,128)S(1)}, f32[22,48,512]{2,1,0:T(8,128)S(1)}) fusion(f32[22,128,512]{2,1,0:T(8,128)} %all-gather.2.cloned.1.call-done, s32[]{:T(128)S(6)} %select_n.555, s32[]{:T(128)S(6)} %select_n.556), kind=kLoop, calls=%fused_computation.118 | loop fusion | bytes 8650760 | tf_op jit(solution)/shard_map/dynamic_slice | solution.py:84
  90.2 8.9 %fusion = f32[2,768,512]{2,1,0:T(8,128)S(1)} fusion(f32[2,768,1056]{2,1,0:T(8,128)} %mul.56, f32[1,1056,512]{2,1,0:T(8,128)S(1)} %bitcast.88, f32[1,1056,512]{2,1,0:T(8,128)S(1)} %bitcast.87), kind=kOutput, calls=%fused_computation.5 | convolution fusion | flops 4983914496 | bytes 13959168 | tf_op jit(solution)/shard_map/tmk,tkz->tmz/dot_general | solution.py:95
  99.2 3.5 %bitcast_divide_fusion = f32[2,256,512]{2,1,0:T(8,128)S(1)} fusion(f32[8,2,32,512]{3,2,0,1:T(8,128)S(1)} %copy-done.9, f32[2,3,256,512]{3,2,1,0:T(8,128)S(1)} %bitcast.89, f32[2,3,512,128]{3,2,1,0:T(8,128)S(1)} %get-tuple-element.10, f32[2,3,512,128]{3,2,1,0:T(8,128)S(1)} %copy-done.4, f32[2,3,512,128]{3,2,1,0:T(8,128)S(1)} %copy-done.5, ...), kind=kOutput, calls=%fused_computation.20 | convolution fusion | flops 2420899840 | bytes 11534336 | tf_op jit(solution)/shard_map/tqmz,tqzn->tmn/dot_general | solution.py:97
  102.6 1.5 fusion.80
  104.1 3.1 %fusion.8 = f32[2,256,512]{2,1,0:T(8,128)S(1)} fusion(f32[2,3,256,512]{3,2,1,0:T(8,128)S(1)} %bitcast.86, f32[2,3,512,128]{3,2,1,0:T(8,128)S(1)} %get-tuple-element.10, f32[2,3,512,128]{3,2,1,0:T(8,128)S(1)} %copy-done.4, f32[2,3,512,128]{3,2,1,0:T(8,128)S(1)} %copy-done.5, f32[2,3,512,128]{3,2,1,0:T(8,128)S(1)} %get-tuple-element.9, f32[2]{0:T(128)S(1)} %gather_fusion), kind=kOutput, calls=%fused_computation.18 | convolution fusion | flops 2420899840 | bytes 10485768 | tf_op jit(solution)/shard_map/tqmz,tqnz->tmn/dot_general | solution.py:108
  107.3 0.2 broadcast_in_dim.779
  107.6 0.7 dynamic_update_slice.6
  108.3 0.1 dynamic-slice_add_fusion
  108.5 0.7 dynamic_update_slice.7
  109.2 1.3 copy-done.3
  110.6 0.6 dynamic-slice
  111.8 0.2 dynamic-update-slice
  112.1 0.2 dynamic-update-slice.1
  112.3 7.0 %all-reduce.6 = (s32[16]{0:T(128)S(1)}, s32[16]{0:T(128)S(1)}) all-reduce(s32[16]{0:T(128)S(1)} %dynamic-update-slice.1, s32[16]{0:T(128)S(1)} %dynamic-update-slice), channel_id=1, replica_groups=mesh['region'=4,'tile'=8] {'tile'}, use_global_device_ids=true, to_apply=%add.5 | all-reduce | flops 32 | bytes 256
  119.3 0.7 gather_fusion.2
  120.1 25.0 %reduce-scatter.2.cloned.1.call-done = f32[8,16,512]{2,1,0:T(8,128)} async-done(((f32[8,128,512]{2,1,0:T(8,128)}), f32[8,16,512]{2,1,0:T(8,128)}) %reduce-scatter.2.cloned.1.call-update) | async-done | bytes 262160 | tf_op jit(solution)/shard_map/reduce_scatter | solution.py:115
  145.1 1.8 %multiply_divide_fusion = f32[8,16,512]{2,1,0:T(8,128)} fusion(f32[8,16,512]{2,1,0:T(8,128)S(1)} %copy-done.7, f32[8,16,512]{2,1,0:T(8,128)} %reduce-scatter.2.cloned.1.call-done, f32[16]{0:T(128)S(1)} %broadcast_add_fusion), kind=kLoop, calls=%fused_computation.23 | loop fusion | flops 196608 | bytes 786496 | tf_op jit(solution)/shard_map/div | solution.py:121
  (110 shorter events, 4.6 us)
Async XLA Ops:
  6.5 19.8 %copy-start = (f32[6,3,3,15]{3,2,1,0:T(4,128)S(1)}, f32[6,3,3,15]{3,2,1,0:T(4,128)}, u32[]{:S(2)}) copy-start(f32[6,3,3,15]{3,2,1,0:T(4,128)} %param.10) | copy-start | bytes 9724
  6.5 19.7 %copy-start.10 = (s32[2]{0:T(128)S(1)}, s32[2]{0:T(128)}, u32[]{:S(2)}) copy-start(s32[2]{0:T(128)} %param.8) | copy-start | bytes 28
  6.5 19.7 %copy-start.11 = (s32[2]{0:T(128)S(1)}, s32[2]{0:T(128)}, u32[]{:S(2)}) copy-start(s32[2]{0:T(128)} %param.9) | copy-start | bytes 28
  6.5 80.5 %all-gather.2.cloned.1.call-start = ((), (), s32[]{:S(2)}) async-start(), calls=%async_computation.1 | async-start | bytes 6488064 | tf_op jit(solution)/shard_map/all_gather | solution.py:73
  7.7 9.7 %collective-permute-start = (f32[7,16,512]{2,1,0:T(8,128)S(1)}, f32[7,16,512]{2,1,0:T(8,128)S(1)}, u32[]{:S(2)}, u32[]{:S(2)}) collective-permute-start(f32[7,16,512]{2,1,0:T(8,128)S(1)} %get-tuple-element.15), channel_id=1, source_target_pairs={{0,8},{8,16},{16,24},{1,9},{9,17},{17,25},{2,10},{10,18},{18,26},{... | collective-permute-start | bytes 688136 | tf_op jit(solution)/shard_map/ppermute | solution.py:18
  12.5 11.7 %collective-permute-start.1 = (f32[7,16,512]{2,1,0:T(8,128)S(1)}, f32[7,16,512]{2,1,0:T(8,128)S(1)}, u32[]{:S(2)}, u32[]{:S(2)}) collective-permute-start(f32[7,16,512]{2,1,0:T(8,128)S(1)} %get-tuple-element.16), channel_id=1, source_target_pairs={{8,0},{16,8},{24,16},{9,1},{17,9},{25,17},{10,2},{18,10},{26,18},{... | collective-permute-start | bytes 688136 | tf_op jit(solution)/shard_map/ppermute | solution.py:20
  26.2 118.9 %reduce-scatter.2.cloned.1.call-start = ((), (), s32[]{:S(2)}) async-start(), calls=%async_computation.2 | async-start | bytes 2359296 | tf_op jit(solution)/shard_map/reduce_scatter | solution.py:115
  40.1 19.8 %copy-start.8 = (f32[8,2,32,512]{3,2,1,0:T(8,128)S(1)}, f32[8,2,32,512]{3,2,1,0:T(8,128)}, u32[]{:S(2)}) copy-start(f32[8,2,32,512]{3,2,1,0:T(8,128)} %param.7) | copy-start | bytes 3145732
  65.2 5.4 %copy-start.2 = (f32[6]{0:T(128)S(1)}, f32[6]{0:T(128)}, u32[]{:S(2)}) copy-start(f32[6]{0:T(128)} %param.11) | copy-start | bytes 76
  90.1 9.0 %copy-start.4 = (f32[2,3,512,128]{3,2,1,0:T(8,128)S(1)}, f32[2,3,512,128]{3,2,1,0:T(8,128)}, u32[]{:S(2)}) copy-start(f32[2,3,512,128]{3,2,1,0:T(8,128)} %get-tuple-element.11) | copy-start | bytes 4718596
  90.1 9.0 %copy-start.5 = (f32[2,3,512,128]{3,2,1,0:T(8,128)S(1)}, f32[2,3,512,128]{3,2,1,0:T(8,128)}, u32[]{:S(2)}) copy-start(f32[2,3,512,128]{3,2,1,0:T(8,128)} %get-tuple-element.12) | copy-start | bytes 4718596
  90.2 9.0 %copy-start.9 = (f32[8,2,32,512]{3,2,0,1:T(8,128)S(1)}, f32[8,2,32,512]{3,2,0,1:T(8,128)}, u32[]{:S(2)}) copy-start(f32[8,2,32,512]{3,2,0,1:T(8,128)} %copy.137) | copy-start | bytes 3145732
  99.1 3.5 %copy-start.6 = (f32[2,768,256]{2,1,0:T(8,128)S(1)}, f32[2,768,256]{2,1,0:T(8,128)}, u32[]{:S(2)}) copy-start(f32[2,768,256]{2,1,0:T(8,128)} %mul.52) | copy-start | bytes 4718596
  108.4 2.1 %copy-start.12 = (u32[32]{0:T(128)S(1)}, u32[32]{0:T(128)}, u32[]{:S(2)}) copy-start(u32[32]{0:T(128)} %constant.19) | copy-start | bytes 388
  109.2 1.3 copy-start.3
  109.2 35.9 %copy-start.7 = (f32[8,16,512]{2,1,0:T(8,128)S(1)}, f32[8,16,512]{2,1,0:T(8,128)}, u32[]{:S(2)}) copy-start(f32[8,16,512]{2,1,0:T(8,128)} %param.6) | copy-start | bytes 786436
  109.2 37.6 %copy-start.1 = (f32[6,3,3,15]{3,2,1,0:T(4,128)S(1)}, f32[6,3,3,15]{3,2,1,0:T(4,128)}, u32[]{:S(2)}) copy-start(f32[6,3,3,15]{3,2,1,0:T(4,128)} %param.10) | copy-start | bytes 9724
Sparse Core Ops, SparseCore 0:
  26.3 60.6 all-gather.1
  110.7 34.3 reduce-scatter.1

commit v2 on v1

--- a/solution.py
+++ b/solution.py
@@ -36,6 +36,23 @@
     return out
 
 
+def kron_band(taps_a, taps_b, rows_a, rows_b, span_b, cols, shift_a, shift_b):
+    kt = taps_a.shape[-1]
+    lead = taps_a.shape[:-1]
+    ia = lax.broadcasted_iota(jnp.int32, (rows_a, cols), 0)
+    ca = lax.broadcasted_iota(jnp.int32, (rows_a, cols), 1) // span_b
+    ib = lax.broadcasted_iota(jnp.int32, (rows_b, cols), 0)
+    cb = lax.broadcasted_iota(jnp.int32, (rows_b, cols), 1) % span_b
+    da = ca - ia - jnp.asarray(shift_a, jnp.int32)[..., None, None]
+    db = cb - ib - jnp.asarray(shift_b, jnp.int32)[..., None, None]
+    ea = jnp.zeros(lead + (rows_a, cols), jnp.float32)
+    eb = jnp.zeros(lead + (rows_b, cols), jnp.float32)
+    for k in range(kt):
+        ea = jnp.where(da == k, taps_a[..., k, None, None], ea)
+        eb = jnp.where(db == k, taps_b[..., k, None, None], eb)
+    return ea[..., :, None, :] * eb[..., None, :, :]
+
+
 def depth_band(taps, depth, block):
     kt = taps.shape[-1]
     half = (kt - 1) // 2
@@ -66,11 +83,17 @@
     win_rows = -(-(tile_rows + 2 * rim) // 8) * 8
     win_x = block_x + 2 * rim
 
-    all_offset = lax.all_gather(tile_offset, "tile", tiled=True)
-    all_view = lax.all_gather(tile_view, "tile", tiled=True)
+    tile_info = jnp.stack([tile_offset.astype(jnp.float32), view_weight[tile_view]], axis=1)
+    all_info = lax.all_gather(tile_info, "tile", tiled=True)
+    all_offset = all_info[:, 0].astype(jnp.int32)
+    all_weight = all_info[:, 1]
 
-    rimmed = with_halo(estimate, (("region", 0),), rim)
-    gathered = lax.all_gather(rimmed, "tile", axis=1, tiled=True)
+    core = lax.all_gather(estimate, "tile", axis=1, tiled=True)
+    count = lax.axis_size("region")
+    lower = lax.ppermute(estimate[block_x - rim :], "region", [(i, i + 1) for i in range(count - 1)])
+    upper = lax.ppermute(estimate[:rim], "region", [(i + 1, i) for i in range(count - 1)])
+    rims = lax.all_gather(jnp.concatenate([lower, upper], axis=0), "tile", axis=1, tiled=True)
+    gathered = jnp.concatenate([rims[:rim], core, rims[rim:]], axis=0)
 
     filters = psf_taps[tile_view]
     weight = view_weight[tile_view]
@@ -84,9 +107,7 @@
         [lax.dynamic_slice_in_dim(gathered, starts[j], win_rows, 1) for j in range(tile_count)]
     ).reshape(tile_count, win_x * win_rows, depth)
 
-    tx = band(ax, block_x, win_x, 0)
-    ty = band(ay, tile_rows, win_rows, shifts[:, None])
-    kxy = (tx[:, :, :, None, :, None] * ty[:, :, None, :, None, :]).reshape(
+    kxy = kron_band(ax, ay, block_x, tile_rows, win_rows, win_x * win_rows, 0, shifts[:, None]).reshape(
         tile_count, rank_terms * block_x * tile_rows, win_x * win_rows
     )
     tz = depth_band(az, depth, 128)
@@ -98,9 +119,7 @@
 
     quotient = observed.transpose(1, 0, 2, 3).reshape(tile_count, cells, depth) / blurred
 
-    fx = band(ax[..., ::-1], block_x, block_x, -rim)
-    fy = band(ay[..., ::-1], tile_rows, tile_rows, -rim)
-    fxy = (fx[:, :, :, None, :, None] * fy[:, :, None, :, None, :]).reshape(
+    fxy = kron_band(ax[..., ::-1], ay[..., ::-1], block_x, tile_rows, tile_rows, cells, -rim, -rim).reshape(
         tile_count, rank_terms * cells, cells
     )
     part = jnp.einsum("tmk,tkz->tmz", fxy, quotient, precision=MATMUL_PRECISION)
@@ -117,7 +136,7 @@
     me = lax.axis_index("tile")
     rows = me * block_y + jnp.arange(block_y, dtype=jnp.int32)
     inside = (rows[None, :] >= all_offset[:, None]) & (rows[None, :] < all_offset[:, None] + tile_rows)
-    own_coverage = jnp.sum(jnp.where(inside, view_weight[all_view][:, None], 0.0), axis=0)
+    own_coverage = jnp.sum(jnp.where(inside, all_weight[:, None], 0.0), axis=0)
     return estimate * (own_numerator + PRIOR_WEIGHT) / (own_coverage[None, :, None] + PRIOR_WEIGHT)
 
 

time: 154 us -> 164 us (1.065)
  waiting for transfers between devices: 41.7 us -> 75.4 us
  local copies, waits for them, and re-layouts: 39.9 us -> 20.8 us
  other arithmetic: 20 us -> 15 us
  blocking collectives: 6.99 us -> 10.4 us
  matrix products: 17 us -> 14.4 us
    all_gather x1 -> x2, waiting for transfers between devices: 6.23 us -> 39.8 us  [the longest x1 25.8 us: on_device(): core = lax.all_gather(estimate, 'tile', axis=1, tiled=True)]
    mul x2 -> x0, local copies, waits for them, and re-layouts: 20.4 us -> none  [the longest x1 15 us: on_device(): tx[:, :, :, None, :, None] * ty[:, :, None, :, None, :]]
    all_gather x0 -> x1, blocking collectives: none -> 10.4 us  [on_device(): all_info = lax.all_gather(tile_info, 'tile', tiled=True)]
    mul x2, other arithmetic: 12.7 us -> 3.9 us  [kron_band(): return ea[..., :, None, :] * eb[..., None, :, :]]
    unnamed x1 -> x0, blocking collectives: 6.99 us -> none
    slice x33 -> x35, local copies, waits for them, and re-layouts: 4.27 us -> 8.13 us  [the longest x1 3.8 us: on_device(): gathered = jnp.concatenate([rims[:rim], core, rims[rim:]], axis=0)]
    dot_general x1, matrix products: 8.93 us -> 6.62 us  [on_device(): part = jnp.einsum('tmk,tkz->tmz', kxy, windows, precision=MATMUL_PRECISION)]
    dynamic_slice x1, local copies, waits for them, and re-layouts: 3.09 us -> 0.79 us  [on_device(): lax.dynamic_slice_in_dim(gathered, starts[j], win_rows, 1)]
  transfers between devices with their start and end apart: 4 -> 5, of which waited for: 4 -> 5; matrix products, arithmetic and copies ran while one was open for 32% -> 15% of each run, Pallas kernels for 0% -> 0%
where the time goes in v2:
time: 164 us
  waiting for transfers between devices  75.4 us (46%)
  between operations  21.2 us (13%)
  local copies, waits for them, and re-layouts  20.8 us (13%)
  other arithmetic  15 us (9%)
  matrix products  14.4 us (9%)
  blocking collectives  10.4 us (6%)
  starting transfers between devices  6.23 us (4%)
    all_gather x1, waiting for transfers between devices, on_device(): core = lax.all_gather(estimate, 'tile', axis=1, tiled=True)  25.8 us
    reduce_scatter x1, waiting for transfers between devices, on_device(): lax.psum_scatter(numerator, 'tile', scatter_dimension=1, tiled=True)  24.5 us
    all_gather x1, waiting for transfers between devices, on_device(): lax.all_gather(jnp.concatenate([lower, upper], axis=0), 'tile', axis=1, t...  13.9 us
    all_gather x1, blocking collectives, on_device(): all_info = lax.all_gather(tile_info, 'tile', tiled=True)  10.4 us
    ppermute x1, waiting for transfers between devices, on_device(): lax.ppermute(estimate[:rim], 'region', [(i + 1, i) for i in range(count -...  6.86 us
    dot_general x1, matrix products, on_device(): part = jnp.einsum('tmk,tkz->tmz', kxy, windows, precision=MATMUL_PRECISION)  6.62 us
    ppermute x1, starting transfers between devices, on_device(): lax.ppermute(estimate[block_x - rim:], 'region', [(i, i + 1) for i in ran...  4.86 us
    mul x2, other arithmetic, kron_band(): return ea[..., :, None, :] * eb[..., None, :, :]  3.9 us
  transfers between devices with their start and end apart: 5, of which 5 were waited for; matrix products, arithmetic and copies ran while one was open for 15% of the time, Pallas kernels for 0%

profile of v2, /device:TPU:0, one launch (start us, length us, event | category | flops | bytes accessed | tf_op | source)
XLA Modules:
  0.0 163.5 jit_solution(2711943102630633958)
XLA Ops:
  6.5 1.1 fusion.82
  7.7 4.9 %collective-permute-start = (f32[7,16,512]{2,1,0:T(8,128)S(1)}, f32[7,16,512]{2,1,0:T(8,128)S(1)}, u32[]{:S(2)}, u32[]{:S(2)}) collective-permute-start(f32[7,16,512]{2,1,0:T(8,128)S(1)} %get-tuple-element.15), channel_id=1, source_target_pairs={{0,8},{8,16},{16,24},{1,9},{9,17},{17,25},{2,10},{10,18},{18,26},{... | collective-permute-start | bytes 688136 | tf_op jit(solution)/shard_map/ppermute | solution.py:93
  12.5 1.3 collective-permute-start.1
  13.8 3.5 %collective-permute-done = f32[7,16,512]{2,1,0:T(8,128)S(1)} collective-permute-done((f32[7,16,512]{2,1,0:T(8,128)S(1)}, f32[7,16,512]{2,1,0:T(8,128)S(1)}, u32[]{:S(2)}, u32[]{:S(2)}) %collective-permute-start) | collective-permute-done | bytes 229408 | tf_op jit(solution)/shard_map/ppermute | solution.py:93
  17.4 6.9 %collective-permute-done.1 = f32[7,16,512]{2,1,0:T(8,128)S(1)} collective-permute-done((f32[7,16,512]{2,1,0:T(8,128)S(1)}, f32[7,16,512]{2,1,0:T(8,128)S(1)}, u32[]{:S(2)}, u32[]{:S(2)}) %collective-permute-start.1) | collective-permute-done | bytes 229408 | tf_op jit(solution)/shard_map/ppermute | solution.py:94
  24.2 0.8 pad_maximum_fusion.12
  25.1 0.7 all-gather.6.cloned.1.call-update
  25.9 0.7 fusion.89
  29.3 0.6 fusion.88
  32.3 0.6 gather_fusion.1
  32.9 0.1 fusion.87
  33.0 0.1 copy.178
  33.1 0.1 copy.179
  33.2 0.1 copy.180
  34.5 0.1 fusion.86
  34.6 0.1 copy.162
  36.1 0.1 fusion.85
  36.2 0.1 copy.196
  37.7 0.6 fusion.23
  38.3 1.5 select_select_fusion
  39.8 2.9 %pad_slice_fusion.3 = (f32[2,3,512,128]{3,2,1,0:T(8,128)}, f32[2,3,512,128]{3,2,1,0:T(8,128)}, f32[2,3,512,128]{3,2,1,0:T(8,128)}, f32[2,3,512,128]{3,2,1,0:T(8,128)}) fusion(f32[2,3,384,128]{3,2,1,0:T(8,128)S(1)} %select_select_fusion), kind=kLoop, calls=%fused_computation.14 | loop fusion | bytes 7471104 | tf_op jit(solution)/shard_map/slice | solution.py:70
  42.7 1.1 copy.193
  43.8 0.6 gather_fusion
  45.9 0.4 select_select_fusion.3
  46.2 0.2 select_select_fusion.4
  46.4 0.2 broadcast_multiply_fusion.1
  47.9 0.4 select_select_fusion.2
  48.3 0.7 subtract_compare_fusion.14
  49.0 1.4 select_select_fusion.1
  50.4 3.7 %broadcast_multiply_fusion = f32[2,3,8,32,1056]{4,3,2,1,0:T(8,128)} fusion(f32[2,3,32,1056]{3,2,1,0:T(8,128)S(1)} %select_select_fusion.1, f32[2,3,8,1056]{3,2,1,0:T(8,128)S(1)} %select_select_fusion.2), kind=kLoop, calls=%fused_computation.10 | loop fusion | flops 1622016 | bytes 7501824 | tf_op jit(solution)/shard_map/mul | solution.py:53
  54.1 13.9 %all-gather.4.cloned.1.call-done = f32[14,128,512]{2,1,0:T(8,128)} async-done(((f32[14,16,512]{2,1,0:T(8,128)}), f32[14,128,512]{2,1,0:T(8,128)}) %all-gather.4.cloned.1.call-update) | async-done | bytes 3670032 | tf_op jit(solution)/shard_map/all_gather | solution.py:95
  68.1 3.8 %fusion.80 = (f32[7,128,512]{2,1,0:T(8,128)S(1)}, f32[7,128,512]{2,1,0:T(8,128)}) fusion(f32[14,128,512]{2,1,0:T(8,128)} %all-gather.4.cloned.1.call-done), kind=kLoop, calls=%fused_computation.146 | loop fusion | bytes 7340032 | tf_op jit(solution)/shard_map/slice | solution.py:96
  71.9 25.8 %all-gather.6.cloned.1.call-done = f32[8,128,512]{2,1,0:T(8,128)} async-done(((f32[8,16,512]{2,1,0:T(8,128)}), f32[8,128,512]{2,1,0:T(8,128)}) %all-gather.6.cloned.1.call-update) | async-done | bytes 2097168 | tf_op jit(solution)/shard_map/all_gather | solution.py:91
  97.7 3.0 %pad_maximum_fusion.1 = f32[22,128,512]{2,1,0:T(8,128)S(1)} fusion(f32[7,128,512]{2,1,0:T(8,128)} %get-tuple-element.8, f32[8,128,512]{2,1,0:T(8,128)} %all-gather.6.cloned.1.call-done, f32[7,128,512]{2,1,0:T(8,128)S(1)} %get-tuple-element.7), kind=kLoop, calls=%fused_computation.3 | loop fusion | flops 2883584 | bytes 11534336 | tf_op jit(solution)/shard_map/concatenate | solution.py:96
  100.7 0.8 constant_dynamic-slice_fusion.1
  101.5 0.5 slice-done.1
  102.0 6.6 %fusion = f32[2,768,512]{2,1,0:T(8,128)S(1)} fusion(f32[2,768,1056]{2,1,0:T(8,128)S(1)} %bitcast.97, f32[1,1056,512]{2,1,0:T(8,128)S(1)} %bitcast.100, f32[1,1056,512]{2,1,0:T(8,128)S(1)} %bitcast.99), kind=kOutput, calls=%fused_computation.4 | convolution fusion | flops 4983914496 | bytes 13959168 | tf_op jit(solution)/shard_map/tmk,tkz->tmz/dot_general | solution.py:116
  108.7 3.3 %bitcast_divide_fusion = f32[2,256,512]{2,1,0:T(8,128)S(1)} fusion(f32[8,2,32,512]{3,2,0,1:T(8,128)S(1)} %copy-done.9, f32[2,3,256,512]{3,2,1,0:T(8,128)S(1)} %bitcast.102, f32[2,3,512,128]{3,2,1,0:T(8,128)S(1)} %copy-done.4, f32[2,3,512,128]{3,2,1,0:T(8,128)S(1)} %copy-done.5, f32[2,3,512,128]{3,2,1,0:T(8,128)S(1)} %copy-done.6, ...), kind=kOutput, calls=%fused_computation.34 | convolution fusion | flops 2420899840 | bytes 11534336 | tf_op jit(solution)/shard_map/tqmz,tqzn->tmn/dot_general | solution.py:118
  112.0 1.5 fusion.90
  113.5 3.0 %fusion.8 = f32[2,256,512]{2,1,0:T(8,128)S(1)} fusion(f32[2,3,256,512]{3,2,1,0:T(8,128)S(1)} %bitcast.98, f32[2,3,512,128]{3,2,1,0:T(8,128)S(1)} %copy-done.4, f32[2,3,512,128]{3,2,1,0:T(8,128)S(1)} %copy-done.5, f32[2,3,512,128]{3,2,1,0:T(8,128)S(1)} %copy-done.6, f32[2,3,512,128]{3,2,1,0:T(8,128)S(1)} %copy-done.3, f32[2]{0:T(128)S(1)} %gather_fusion), kind=kOutput, calls=%fused_computation.32 | convolution fusion | flops 2420899840 | bytes 10485768 | tf_op jit(solution)/shard_map/tqmz,tqnz->tmn/dot_general | solution.py:127
  116.6 0.2 broadcast_in_dim.790
  116.9 0.7 dynamic_update_slice.6
  117.6 0.1 dynamic-slice_add_fusion
  117.7 0.7 dynamic_update_slice.7
  118.5 1.3 copy-done.2
  120.0 10.4 %all-gather = f32[8,2,2]{2,1,0:T(2,128)S(1)} all-gather(f32[1,2,2]{2,1,0:T(2,128)S(1)} %bitcast.185), channel_id=1, replica_groups=mesh['region'=4,'tile'=8] {'tile'}, dimensions={0}, use_global_device_ids=true | all-gather | bytes 144 | tf_op jit(solution)/shard_map/all_gather | solution.py:87
  130.7 24.5 %reduce-scatter.2.cloned.1.call-done = f32[8,16,512]{2,1,0:T(8,128)} async-done(((f32[8,128,512]{2,1,0:T(8,128)}), f32[8,16,512]{2,1,0:T(8,128)}) %reduce-scatter.2.cloned.1.call-update) | async-done | bytes 262160 | tf_op jit(solution)/shard_map/reduce_scatter | solution.py:134
  155.2 1.8 %multiply_divide_fusion = f32[8,16,512]{2,1,0:T(8,128)} fusion(f32[8,16,512]{2,1,0:T(8,128)S(1)} %copy-done.7, f32[8,16,512]{2,1,0:T(8,128)} %reduce-scatter.2.cloned.1.call-done, f32[16]{0:T(128)S(1)} %broadcast_add_fusion.2), kind=kLoop, calls=%fused_computation.39 | loop fusion | flops 196608 | bytes 786496 | tf_op jit(solution)/shard_map/div | solution.py:140
  (101 shorter events, 4.9 us)
Async XLA Ops:
  6.5 25.8 %copy-start = (f32[6,3,3,15]{3,2,1,0:T(4,128)S(1)}, f32[6,3,3,15]{3,2,1,0:T(4,128)}, u32[]{:S(2)}) copy-start(f32[6,3,3,15]{3,2,1,0:T(4,128)} %param.10) | copy-start | bytes 9724
  6.5 19.4 %copy-start.10 = (s32[2]{0:T(128)S(1)}, s32[2]{0:T(128)}, u32[]{:S(2)}) copy-start(s32[2]{0:T(128)} %param.8) | copy-start | bytes 28
  6.5 19.4 %copy-start.11 = (s32[2]{0:T(128)S(1)}, s32[2]{0:T(128)}, u32[]{:S(2)}) copy-start(s32[2]{0:T(128)} %param.9) | copy-start | bytes 28
  6.5 61.6 %all-gather.4.cloned.1.call-start = ((), (), s32[]{:S(2)}) async-start(), calls=%async_computation.1 | async-start | bytes 4128768 | tf_op jit(solution)/shard_map/all_gather | solution.py:95
  7.7 9.7 %collective-permute-start = (f32[7,16,512]{2,1,0:T(8,128)S(1)}, f32[7,16,512]{2,1,0:T(8,128)S(1)}, u32[]{:S(2)}, u32[]{:S(2)}) collective-permute-start(f32[7,16,512]{2,1,0:T(8,128)S(1)} %get-tuple-element.15), channel_id=1, source_target_pairs={{0,8},{8,16},{16,24},{1,9},{9,17},{17,25},{2,10},{10,18},{18,26},{... | collective-permute-start | bytes 688136 | tf_op jit(solution)/shard_map/ppermute | solution.py:93
  12.5 11.7 %collective-permute-start.1 = (f32[7,16,512]{2,1,0:T(8,128)S(1)}, f32[7,16,512]{2,1,0:T(8,128)S(1)}, u32[]{:S(2)}, u32[]{:S(2)}) collective-permute-start(f32[7,16,512]{2,1,0:T(8,128)S(1)} %get-tuple-element.16), channel_id=1, source_target_pairs={{8,0},{16,8},{24,16},{9,1},{17,9},{25,17},{10,2},{18,10},{26,18},{... | collective-permute-start | bytes 688136 | tf_op jit(solution)/shard_map/ppermute | solution.py:94
  25.0 72.7 %all-gather.6.cloned.1.call-start = ((), (), s32[]{:S(2)}) async-start(), calls=%async_computation.2 | async-start | bytes 2359296 | tf_op jit(solution)/shard_map/all_gather | solution.py:91
  25.8 129.4 %reduce-scatter.2.cloned.1.call-start = ((), (), s32[]{:S(2)}) async-start(), calls=%async_computation.3 | async-start | bytes 2359296 | tf_op jit(solution)/shard_map/reduce_scatter | solution.py:134
  39.8 2.9 %copy-start.8 = (f32[8,2,32,512]{3,2,1,0:T(8,128)S(1)}, f32[8,2,32,512]{3,2,1,0:T(8,128)}, u32[]{:S(2)}) copy-start(f32[8,2,32,512]{3,2,1,0:T(8,128)} %param.7) | copy-start | bytes 3145732
  42.7 1.1 copy-start.1
  97.7 3.8 %slice-start = ((s8[7077888]{0:T(1024)(128)(4,1)}), s8[4194304]{0:T(1024)(128)(4,1)S(1)}, s32[]{:S(2)}) async-start(s8[7077888]{0:T(1024)(128)(4,1)} %bitcast.95), calls=%async_computation.4 | async-start | bytes 8388608
  97.7 4.3 %slice-start.1 = ((s8[7077888]{0:T(1024)(128)(4,1)}), s8[2883584]{0:T(1024)(128)(4,1)S(1)}, s32[]{:S(2)}) async-start(s8[7077888]{0:T(1024)(128)(4,1)} %bitcast.95), calls=%async_computation.5 | async-start | bytes 5767168
  102.0 6.6 %copy-start.3 = (f32[2,3,512,128]{3,2,1,0:T(8,128)S(1)}, f32[2,3,512,128]{3,2,1,0:T(8,128)}, u32[]{:S(2)}) copy-start(f32[2,3,512,128]{3,2,1,0:T(8,128)} %get-tuple-element.9) | copy-start | bytes 4718596
  102.0 6.7 %copy-start.4 = (f32[2,3,512,128]{3,2,1,0:T(8,128)S(1)}, f32[2,3,512,128]{3,2,1,0:T(8,128)}, u32[]{:S(2)}) copy-start(f32[2,3,512,128]{3,2,1,0:T(8,128)} %get-tuple-element.10) | copy-start | bytes 4718596
  102.0 6.7 %copy-start.5 = (f32[2,3,512,128]{3,2,1,0:T(8,128)S(1)}, f32[2,3,512,128]{3,2,1,0:T(8,128)}, u32[]{:S(2)}) copy-start(f32[2,3,512,128]{3,2,1,0:T(8,128)} %get-tuple-element.11) | copy-start | bytes 4718596
  102.0 6.7 %copy-start.6 = (f32[2,3,512,128]{3,2,1,0:T(8,128)S(1)}, f32[2,3,512,128]{3,2,1,0:T(8,128)}, u32[]{:S(2)}) copy-start(f32[2,3,512,128]{3,2,1,0:T(8,128)} %get-tuple-element.12) | copy-start | bytes 4718596
  102.0 6.7 %copy-start.9 = (f32[8,2,32,512]{3,2,0,1:T(8,128)S(1)}, f32[8,2,32,512]{3,2,0,1:T(8,128)}, u32[]{:S(2)}) copy-start(f32[8,2,32,512]{3,2,0,1:T(8,128)} %copy.193) | copy-start | bytes 3145732
  117.7 37.5 %copy-start.7 = (f32[8,16,512]{2,1,0:T(8,128)S(1)}, f32[8,16,512]{2,1,0:T(8,128)}, u32[]{:S(2)}) copy-start(f32[8,16,512]{2,1,0:T(8,128)} %param.6) | copy-start | bytes 786436
  118.5 1.4 copy-start.2
Sparse Core Ops, SparseCore 0:
  25.2 42.8 all-gather.3
  69.7 27.9 all-gather.5
  120.0 35.2 reduce-scatter.1

commit v3 on v2

--- a/solution.py
+++ b/solution.py
@@ -22,18 +22,6 @@
             axis=dim,
         )
     return cells
-
-
-def band(taps, rows, cols, shift):
-    kt = taps.shape[-1]
-    i = lax.broadcasted_iota(jnp.int32, (rows, cols), 0)
-    j = lax.broadcasted_iota(jnp.int32, (rows, cols), 1)
-    d = j - i - jnp.asarray(shift, jnp.int32)[..., None, None]
-    out = jnp.zeros(d.shape[:-2] + (rows, cols), jnp.float32)
-    out = jnp.broadcast_to(out, taps.shape[:-1] + (rows, cols))
-    for k in range(kt):
-        out = jnp.where(d == k, taps[..., k, None, None], out)
-    return out
 
 
 def kron_band(taps_a, taps_b, rows_a, rows_b, span_b, cols, shift_a, shift_b):
@@ -88,12 +76,8 @@
     all_offset = all_info[:, 0].astype(jnp.int32)
     all_weight = all_info[:, 1]
 
-    core = lax.all_gather(estimate, "tile", axis=1, tiled=True)
-    count = lax.axis_size("region")
-    lower = lax.ppermute(estimate[block_x - rim :], "region", [(i, i + 1) for i in range(count - 1)])
-    upper = lax.ppermute(estimate[:rim], "region", [(i + 1, i) for i in range(count - 1)])
-    rims = lax.all_gather(jnp.concatenate([lower, upper], axis=0), "tile", axis=1, tiled=True)
-    gathered = jnp.concatenate([rims[:rim], core, rims[rim:]], axis=0)
+    rimmed = with_halo(estimate, (("region", 0),), rim)
+    gathered = lax.all_gather(rimmed, "tile", axis=1, tiled=True)
 
     filters = psf_taps[tile_view]
     weight = view_weight[tile_view]

time: 164 us -> 153 us (0.933)
  waiting for transfers between devices: 75.4 us -> 68.3 us
  other arithmetic: 15 us -> 13.2 us
    all_gather x2 -> x1, waiting for transfers between devices: 39.8 us -> 33.1 us  [on_device(): gathered = lax.all_gather(rimmed, 'tile', axis=1, tiled=True)]
    slice x2 -> x1, local copies, waits for them, and re-layouts: 4.9 us -> 1.11 us  [with_halo(): lax.slice_in_dim(cells, cells.shape[dim] - width, cells.shape[dim], axis=...]
    dynamic_slice x1, local copies, waits for them, and re-layouts: 0.79 us -> 3.18 us  [on_device(): lax.dynamic_slice_in_dim(gathered, starts[j], win_rows, 1)]
    concatenate x2 -> x1, other arithmetic: 3.79 us -> 1.94 us  [with_halo(): jnp.concatenate([lax.ppermute(tail, axis, [(i, (i + 1) % count) for i in...]
    unnamed x31 -> x27, local copies, waits for them, and re-layouts: 3.1 us -> 3.85 us
  transfers between devices with their start and end apart: 5 -> 4, of which waited for: 5 -> 4; matrix products, arithmetic and copies ran while one was open for 15% -> 13% of each run, Pallas kernels for 0% -> 0%
where the time goes in v3:
time: 153 us
  waiting for transfers between devices  68.3 us (45%)
  between operations  21.3 us (14%)
  local copies, waits for them, and re-layouts  19.6 us (13%)
  matrix products  14.7 us (10%)
  other arithmetic  13.2 us (9%)
  blocking collectives  9.38 us (6%)
  starting transfers between devices  6.32 us (4%)
    all_gather x1, waiting for transfers between devices, on_device(): gathered = lax.all_gather(rimmed, 'tile', axis=1, tiled=True)  33.1 us
    reduce_scatter x1, waiting for transfers between devices, on_device(): lax.psum_scatter(numerator, 'tile', scatter_dimension=1, tiled=True)  24.8 us
    all_gather x1, blocking collectives, on_device(): all_info = lax.all_gather(tile_info, 'tile', tiled=True)  9.38 us
    ppermute x1, waiting for transfers between devices, with_halo(): lax.ppermute(head, axis, [((i + 1) % count, i) for i in range(ends)])  6.86 us
    dot_general x1, matrix products, on_device(): part = jnp.einsum('tmk,tkz->tmz', kxy, windows, precision=MATMUL_PRECISION)  6.72 us
    ppermute x1, starting transfers between devices, with_halo(): lax.ppermute(tail, axis, [(i, (i + 1) % count) for i in range(ends)])  4.99 us
    mul x2, other arithmetic, kron_band(): return ea[..., :, None, :] * eb[..., None, :, :]  3.92 us
    unnamed x27, local copies, waits for them, and re-layouts  3.85 us
  transfers between devices with their start and end apart: 4, of which 4 were waited for; matrix products, arithmetic and copies ran while one was open for 13% of the time, Pallas kernels for 0%

profile of v3, /device:TPU:0, one launch (start us, length us, event | category | flops | bytes accessed | tf_op | source)
XLA Modules:
  0.0 152.8 jit_solution(11709061538156455320)
XLA Ops:
  6.5 1.1 fusion.81
  7.7 5.0 %collective-permute-start = (f32[7,16,512]{2,1,0:T(8,128)S(1)}, f32[7,16,512]{2,1,0:T(8,128)S(1)}, u32[]{:S(2)}, u32[]{:S(2)}) collective-permute-start(f32[7,16,512]{2,1,0:T(8,128)S(1)} %get-tuple-element.13), channel_id=1, source_target_pairs={{0,8},{8,16},{16,24},{1,9},{9,17},{17,25},{2,10},{10,18},{18,26},{... | collective-permute-start | bytes 688136 | tf_op jit(solution)/shard_map/ppermute | solution.py:18
  12.7 1.3 collective-permute-start.1
  14.0 3.5 %collective-permute-done = f32[7,16,512]{2,1,0:T(8,128)S(1)} collective-permute-done((f32[7,16,512]{2,1,0:T(8,128)S(1)}, f32[7,16,512]{2,1,0:T(8,128)S(1)}, u32[]{:S(2)}, u32[]{:S(2)}) %collective-permute-start) | collective-permute-done | bytes 229408 | tf_op jit(solution)/shard_map/ppermute | solution.py:18
  17.5 6.9 %collective-permute-done.1 = f32[7,16,512]{2,1,0:T(8,128)S(1)} collective-permute-done((f32[7,16,512]{2,1,0:T(8,128)S(1)}, f32[7,16,512]{2,1,0:T(8,128)S(1)}, u32[]{:S(2)}, u32[]{:S(2)}) %collective-permute-start.1) | collective-permute-done | bytes 229408 | tf_op jit(solution)/shard_map/ppermute | solution.py:20
  24.4 1.9 %pad_maximum_fusion.11 = f32[22,16,512]{2,1,0:T(8,128)} fusion(f32[7,16,512]{2,1,0:T(8,128)S(1)} %collective-permute-done.1, f32[8,16,512]{2,1,0:T(8,128)} %param.6, f32[7,16,512]{2,1,0:T(8,128)S(1)} %collective-permute-done), kind=kLoop, calls=%fused_computation.36 | loop fusion | flops 360448 | bytes 1441792 | tf_op jit(solution)/shard_map/concatenate | solution.py:16
  26.4 0.6 fusion.88
  29.7 0.6 fusion.87
  32.7 0.6 gather_fusion.1
  33.3 0.1 fusion.86
  33.4 0.1 copy.178
  33.5 0.1 copy.179
  33.6 0.1 copy.180
  33.7 0.1 copy.181
  33.8 0.1 copy.182
  33.9 0.1 copy.183
  34.0 0.1 copy.184
  34.9 0.1 fusion.85
  35.0 0.1 copy.162
  36.5 0.1 fusion.84
  36.6 0.1 copy.196
  38.1 1.1 copy.193
  39.2 0.6 gather_fusion
  42.4 0.2 select_select_fusion.4
  42.7 0.4 select_select_fusion.3
  43.1 0.6 fusion.23
  43.7 0.2 broadcast_multiply_fusion.1
  43.8 1.5 select_select_fusion
  45.3 2.4 %pad_slice_fusion.3 = (f32[2,3,512,128]{3,2,1,0:T(8,128)S(1)}, f32[2,3,512,128]{3,2,1,0:T(8,128)}, f32[2,3,512,128]{3,2,1,0:T(8,128)}, f32[2,3,512,128]{3,2,1,0:T(8,128)}) fusion(f32[2,3,384,128]{3,2,1,0:T(8,128)S(1)} %select_select_fusion), kind=kLoop, calls=%fused_computation.13 | loop fusion | bytes 7471104 | tf_op jit(solution)/shard_map/slice | solution.py:58
  47.9 0.4 select_select_fusion.2
  48.2 0.7 subtract_compare_fusion.14
  48.9 1.4 select_select_fusion.1
  50.3 3.7 %broadcast_multiply_fusion = f32[2,3,8,32,1056]{4,3,2,1,0:T(8,128)} fusion(f32[2,3,32,1056]{3,2,1,0:T(8,128)S(1)} %select_select_fusion.1, f32[2,3,8,1056]{3,2,1,0:T(8,128)S(1)} %select_select_fusion.2), kind=kLoop, calls=%fused_computation.9 | loop fusion | flops 1622016 | bytes 7501824 | tf_op jit(solution)/shard_map/mul | solution.py:41
  54.1 33.1 %all-gather.3.cloned.1.call-done = f32[22,128,512]{2,1,0:T(8,128)} async-done(((f32[22,16,512]{2,1,0:T(8,128)}), f32[22,128,512]{2,1,0:T(8,128)}) %all-gather.3.cloned.1.call-update) | async-done | bytes 5767184 | tf_op jit(solution)/shard_map/all_gather | solution.py:80
  87.2 3.2 %constant_dynamic-slice_fusion.1 = (f32[22,48,512]{2,1,0:T(8,128)S(1)}, f32[22,48,512]{2,1,0:T(8,128)S(1)}) fusion(f32[22,128,512]{2,1,0:T(8,128)} %all-gather.3.cloned.1.call-done, s32[]{:T(128)S(6)} %select_n.668, s32[]{:T(128)S(6)} %select_n.669), kind=kLoop, calls=%fused_computation.133 | loop fusion | bytes 8650760 | tf_op jit(solution)/shard_map/dynamic_slice | solution.py:91
  90.4 1.2 copy-done.2
  91.6 6.7 %fusion = f32[2,768,512]{2,1,0:T(8,128)S(1)} fusion(f32[2,768,1056]{2,1,0:T(8,128)S(1)} %bitcast.95, f32[1,1056,512]{2,1,0:T(8,128)S(1)} %bitcast.98, f32[1,1056,512]{2,1,0:T(8,128)S(1)} %bitcast.97), kind=kOutput, calls=%fused_computation.3 | convolution fusion | flops 4983914496 | bytes 13959168 | tf_op jit(solution)/shard_map/tmk,tkz->tmz/dot_general | solution.py:100
  98.4 3.4 %bitcast_divide_fusion = f32[2,256,512]{2,1,0:T(8,128)S(1)} fusion(f32[8,2,32,512]{3,2,0,1:T(8,128)S(1)} %copy-done.9, f32[2,3,256,512]{3,2,1,0:T(8,128)S(1)} %bitcast.100, f32[2,3,512,128]{3,2,1,0:T(8,128)S(1)} %copy-done.4, f32[2,3,512,128]{3,2,1,0:T(8,128)S(1)} %copy-done.5, f32[2,3,512,128]{3,2,1,0:T(8,128)S(1)} %copy-done.6, ...), kind=kOutput, calls=%fused_computation.33 | convolution fusion | flops 2420899840 | bytes 11534336 | tf_op jit(solution)/shard_map/tqmz,tqzn->tmn/dot_general | solution.py:102
  101.8 1.5 fusion.89
  103.3 3.1 %fusion.8 = f32[2,256,512]{2,1,0:T(8,128)S(1)} fusion(f32[2,3,256,512]{3,2,1,0:T(8,128)S(1)} %bitcast.96, f32[2,3,512,128]{3,2,1,0:T(8,128)S(1)} %copy-done.4, f32[2,3,512,128]{3,2,1,0:T(8,128)S(1)} %copy-done.5, f32[2,3,512,128]{3,2,1,0:T(8,128)S(1)} %copy-done.6, f32[2,3,512,128]{3,2,1,0:T(8,128)S(1)} %get-tuple-element.7, f32[2]{0:T(128)S(1)} %gather_fusion), kind=kOutput, calls=%fused_computation.31 | convolution fusion | flops 2420899840 | bytes 10485768 | tf_op jit(solution)/shard_map/tqmz,tqnz->tmn/dot_general | solution.py:111
  106.5 0.2 broadcast_in_dim.790
  106.7 0.7 dynamic_update_slice.6
  107.5 0.1 dynamic-slice_add_fusion
  107.6 0.6 dynamic_update_slice.7
  108.3 1.3 copy-done.3
  109.7 9.4 %all-gather = f32[8,2,2]{2,1,0:T(2,128)S(1)} all-gather(f32[1,2,2]{2,1,0:T(2,128)S(1)} %bitcast.183), channel_id=1, replica_groups=mesh['region'=4,'tile'=8] {'tile'}, dimensions={0}, use_global_device_ids=true | all-gather | bytes 144 | tf_op jit(solution)/shard_map/all_gather | solution.py:75
  119.5 24.8 %reduce-scatter.2.cloned.1.call-done = f32[8,16,512]{2,1,0:T(8,128)} async-done(((f32[8,128,512]{2,1,0:T(8,128)}), f32[8,16,512]{2,1,0:T(8,128)}) %reduce-scatter.2.cloned.1.call-update) | async-done | bytes 262160 | tf_op jit(solution)/shard_map/reduce_scatter | solution.py:118
  144.2 1.8 %multiply_divide_fusion = f32[8,16,512]{2,1,0:T(8,128)} fusion(f32[8,16,512]{2,1,0:T(8,128)S(1)} %copy-done.7, f32[8,16,512]{2,1,0:T(8,128)} %reduce-scatter.2.cloned.1.call-done, f32[16]{0:T(128)S(1)} %broadcast_add_fusion.2), kind=kLoop, calls=%fused_computation.38 | loop fusion | flops 196608 | bytes 786496 | tf_op jit(solution)/shard_map/div | solution.py:124
  (91 shorter events, 4.5 us)
Async XLA Ops:
  6.5 26.2 %copy-start = (f32[6,3,3,15]{3,2,1,0:T(4,128)S(1)}, f32[6,3,3,15]{3,2,1,0:T(4,128)}, u32[]{:S(2)}) copy-start(f32[6,3,3,15]{3,2,1,0:T(4,128)} %param.10) | copy-start | bytes 9724
  6.5 19.8 %copy-start.10 = (s32[2]{0:T(128)S(1)}, s32[2]{0:T(128)}, u32[]{:S(2)}) copy-start(s32[2]{0:T(128)} %param.8) | copy-start | bytes 28
  6.5 19.8 %copy-start.11 = (s32[2]{0:T(128)S(1)}, s32[2]{0:T(128)}, u32[]{:S(2)}) copy-start(s32[2]{0:T(128)} %param.9) | copy-start | bytes 28
  6.5 80.6 %all-gather.3.cloned.1.call-start = ((), (), s32[]{:S(2)}) async-start(), calls=%async_computation.1 | async-start | bytes 6488064 | tf_op jit(solution)/shard_map/all_gather | solution.py:80
  7.7 30.4 %copy-start.8 = (f32[8,2,32,512]{3,2,1,0:T(8,128)S(1)}, f32[8,2,32,512]{3,2,1,0:T(8,128)}, u32[]{:S(2)}) copy-start(f32[8,2,32,512]{3,2,1,0:T(8,128)} %param.7) | copy-start | bytes 3145732
  7.7 9.8 %collective-permute-start = (f32[7,16,512]{2,1,0:T(8,128)S(1)}, f32[7,16,512]{2,1,0:T(8,128)S(1)}, u32[]{:S(2)}, u32[]{:S(2)}) collective-permute-start(f32[7,16,512]{2,1,0:T(8,128)S(1)} %get-tuple-element.13), channel_id=1, source_target_pairs={{0,8},{8,16},{16,24},{1,9},{9,17},{17,25},{2,10},{10,18},{18,26},{... | collective-permute-start | bytes 688136 | tf_op jit(solution)/shard_map/ppermute | solution.py:18
  12.7 11.7 %collective-permute-start.1 = (f32[7,16,512]{2,1,0:T(8,128)S(1)}, f32[7,16,512]{2,1,0:T(8,128)S(1)}, u32[]{:S(2)}, u32[]{:S(2)}) collective-permute-start(f32[7,16,512]{2,1,0:T(8,128)S(1)} %get-tuple-element.14), channel_id=1, source_target_pairs={{8,0},{16,8},{24,16},{9,1},{17,9},{25,17},{10,2},{18,10},{26,18},{... | collective-permute-start | bytes 688136 | tf_op jit(solution)/shard_map/ppermute | solution.py:20
  26.3 12.9 %copy-start.1 = (f32[6]{0:T(128)S(1)}, f32[6]{0:T(128)}, u32[]{:S(2)}) copy-start(f32[6]{0:T(128)} %param.11) | copy-start | bytes 76
  26.3 117.9 %reduce-scatter.2.cloned.1.call-start = ((), (), s32[]{:S(2)}) async-start(), calls=%async_computation.2 | async-start | bytes 2359296 | tf_op jit(solution)/shard_map/reduce_scatter | solution.py:118
  87.2 4.4 %copy-start.2 = (f32[2,3,8,32,1056]{4,3,2,1,0:T(8,128)S(1)}, f32[2,3,8,32,1056]{4,3,2,1,0:T(8,128)}, u32[]{:S(2)}) copy-start(f32[2,3,8,32,1056]{4,3,2,1,0:T(8,128)} %broadcast_multiply_fusion) | copy-start | bytes 19464196
  91.6 6.7 %copy-start.4 = (f32[2,3,512,128]{3,2,1,0:T(8,128)S(1)}, f32[2,3,512,128]{3,2,1,0:T(8,128)}, u32[]{:S(2)}) copy-start(f32[2,3,512,128]{3,2,1,0:T(8,128)} %get-tuple-element.8) | copy-start | bytes 4718596
  91.6 6.8 %copy-start.5 = (f32[2,3,512,128]{3,2,1,0:T(8,128)S(1)}, f32[2,3,512,128]{3,2,1,0:T(8,128)}, u32[]{:S(2)}) copy-start(f32[2,3,512,128]{3,2,1,0:T(8,128)} %get-tuple-element.9) | copy-start | bytes 4718596
  91.6 6.8 %copy-start.6 = (f32[2,3,512,128]{3,2,1,0:T(8,128)S(1)}, f32[2,3,512,128]{3,2,1,0:T(8,128)}, u32[]{:S(2)}) copy-start(f32[2,3,512,128]{3,2,1,0:T(8,128)} %get-tuple-element.10) | copy-start | bytes 4718596
  91.6 6.8 %copy-start.9 = (f32[8,2,32,512]{3,2,0,1:T(8,128)S(1)}, f32[8,2,32,512]{3,2,0,1:T(8,128)}, u32[]{:S(2)}) copy-start(f32[8,2,32,512]{3,2,0,1:T(8,128)} %copy.193) | copy-start | bytes 3145732
  107.6 36.6 %copy-start.7 = (f32[8,16,512]{2,1,0:T(8,128)S(1)}, f32[8,16,512]{2,1,0:T(8,128)}, u32[]{:S(2)}) copy-start(f32[8,16,512]{2,1,0:T(8,128)} %param.6) | copy-start | bytes 786436
  108.3 1.3 copy-start.3
Sparse Core Ops, SparseCore 0:
  26.4 60.6 all-gather.2
  109.7 34.4 reduce-scatter.1

commit v4 on v3

--- a/solution.py
+++ b/solution.py
@@ -76,8 +76,25 @@
     all_offset = all_info[:, 0].astype(jnp.int32)
     all_weight = all_info[:, 1]
 
-    rimmed = with_halo(estimate, (("region", 0),), rim)
-    gathered = lax.all_gather(rimmed, "tile", axis=1, tiled=True)
+    core = lax.all_gather(estimate, "tile", axis=1, tiled=True)
+    count = lax.axis_size("region")
+    half_rows = region_rows // 2
+    side = lax.axis_index("tile") % 2
+    mine = side * half_rows
+    lower = lax.ppermute(
+        lax.dynamic_slice_in_dim(core[block_x - rim :], mine, half_rows, 1),
+        "region", [(i, i + 1) for i in range(count - 1)],
+    )
+    upper = lax.ppermute(
+        lax.dynamic_slice_in_dim(core[:rim], mine, half_rows, 1),
+        "region", [(i + 1, i) for i in range(count - 1)],
+    )
+    fetched = jnp.concatenate([lower, upper], axis=0)
+    swapped = lax.ppermute(
+        fetched, "tile", [(i, i ^ 1) for i in range(group_size)]
+    )
+    rims = jnp.where(side == 0, jnp.concatenate([fetched, swapped], axis=1), jnp.concatenate([swapped, fetched], axis=1))
+    gathered = jnp.concatenate([rims[:rim], core, rims[rim:]], axis=0)
 
     filters = psf_taps[tile_view]
     weight = view_weight[tile_view]

time: 153 us -> 157 us (1.026)
  waiting for transfers between devices: 68.3 us -> 73.5 us
  other arithmetic: 13.2 us -> 10.6 us
    ppermute x2 -> x3, waiting for transfers between devices: 10.4 us -> 40.2 us  [the longest x1 21.6 us: on_device(): lax.ppermute(lax.dynamic_slice_in_dim(core[:rim], mine, half_rows, 1), 'r...]
    all_gather x1, waiting for transfers between devices: 33.1 us -> 8.96 us  [on_device(): core = lax.all_gather(estimate, 'tile', axis=1, tiled=True)]
    mul x2, other arithmetic: 3.92 us -> 1.03 us  [kron_band(): return ea[..., :, None, :] * eb[..., None, :, :]]
    dynamic_slice x1, local copies, waits for them, and re-layouts: 3.18 us -> 0.63 us  [on_device(): lax.dynamic_slice_in_dim(gathered, starts[j], win_rows, 1)]
    slice x1 -> x2, local copies, waits for them, and re-layouts: 1.11 us -> 2.84 us  [the longest x1 2.45 us: on_device(): core[:rim]]
    ppermute x2 -> x3, starting transfers between devices: 6.28 us -> 4.93 us  [the longest x1 3.39 us: on_device(): lax.ppermute(lax.dynamic_slice_in_dim(core[block_x - rim:], mine, half_ro...]
    unnamed x27 -> x22, local copies, waits for them, and re-layouts: 3.85 us -> 5.11 us
  transfers between devices with their start and end apart: 4 -> 5, of which waited for: 4 -> 5; matrix products, arithmetic and copies ran while one was open for 13% -> 13% of each run, Pallas kernels for 0% -> 0%
where the time goes in v4:
time: 157 us
  waiting for transfers between devices  73.5 us (47%)
  between operations  21.9 us (14%)
  local copies, waits for them, and re-layouts  21.1 us (13%)
  matrix products  14.3 us (9%)
  other arithmetic  10.6 us (7%)
  blocking collectives  10.3 us (7%)
  starting transfers between devices  4.97 us (3%)
    reduce_scatter x1, waiting for transfers between devices, on_device(): lax.psum_scatter(numerator, 'tile', scatter_dimension=1, tiled=True)  23.6 us
    ppermute x1, waiting for transfers between devices, on_device(): lax.ppermute(lax.dynamic_slice_in_dim(core[:rim], mine, half_rows, 1), 'r...  21.6 us
    ppermute x1, waiting for transfers between devices, on_device(): lax.ppermute(lax.dynamic_slice_in_dim(core[block_x - rim:], mine, half_ro...  17.5 us
    all_gather x1, blocking collectives, on_device(): all_info = lax.all_gather(tile_info, 'tile', tiled=True)  10.3 us
    all_gather x1, waiting for transfers between devices, on_device(): core = lax.all_gather(estimate, 'tile', axis=1, tiled=True)  8.96 us
    dot_general x1, matrix products, on_device(): part = jnp.einsum('tmk,tkz->tmz', kxy, windows, precision=MATMUL_PRECISION)  6.47 us
    unnamed x22, local copies, waits for them, and re-layouts  5.11 us
    dot_general x1, matrix products, on_device(): blurred = jnp.einsum('tqmz,tqzn->tmn', part, tz, precision=MATMUL_PRECISION)  3.45 us
  transfers between devices with their start and end apart: 5, of which 5 were waited for; matrix products, arithmetic and copies ran while one was open for 13% of the time, Pallas kernels for 0%

profile of v4, /device:TPU:0, one launch (start us, length us, event | category | flops | bytes accessed | tf_op | source)
XLA Modules:
  0.0 156.7 jit_solution(13943756855415800847)
XLA Ops:
  6.5 0.7 all-gather.3.cloned.1.call-update
  7.3 1.4 fusion.88
  8.7 0.7 convert_bitcast_fusion.1
  9.5 0.6 gather_fusion.1
  10.1 0.1 fusion.87
  10.2 0.1 fusion.86
  10.3 0.1 fusion.85
  10.4 0.7 fusion.89
  16.4 0.1 copy.178
  16.5 0.1 copy.179
  17.1 0.1 copy.185
  17.2 0.1 copy.186
  20.8 2.3 %copy.193 = f32[8,2,32,512]{3,2,0,1:T(8,128)} copy(f32[8,2,32,512]{3,2,1,0:T(8,128)} %param.7) | data formatting | bytes 2097152 | tf_op args[1]
  23.1 0.6 gather_fusion
  26.6 0.2 select_select_fusion.4
  26.9 0.4 select_select_fusion.3
  27.2 0.6 fusion.23
  27.8 1.5 select_select_fusion
  29.3 2.4 %pad_slice_fusion.3 = (f32[2,3,512,128]{3,2,1,0:T(8,128)S(1)}, f32[2,3,512,128]{3,2,1,0:T(8,128)}, f32[2,3,512,128]{3,2,1,0:T(8,128)}, f32[2,3,512,128]{3,2,1,0:T(8,128)}) fusion(f32[2,3,384,128]{3,2,1,0:T(8,128)S(1)} %select_select_fusion), kind=kLoop, calls=%fused_computation.15 | loop fusion | bytes 7471104 | tf_op jit(solution)/shard_map/slice | solution.py:58
  31.9 9.0 %all-gather.3.cloned.1.call-done = f32[8,128,512]{2,1,0:T(8,128)} async-done(((f32[8,16,512]{2,1,0:T(8,128)}), f32[8,128,512]{2,1,0:T(8,128)}) %all-gather.3.cloned.1.call-update) | async-done | bytes 2097168 | tf_op jit(solution)/shard_map/all_gather | solution.py:79
  40.8 2.4 %fusion.81 = (f32[7,128,512]{2,1,0:T(8,128)S(1)}, f32[7,128,512]{2,1,0:T(8,128)S(1)}) fusion(f32[8,128,512]{2,1,0:T(8,128)} %all-gather.3.cloned.1.call-done), kind=kLoop, calls=%fused_computation.151 | loop fusion | bytes 7340032 | tf_op jit(solution)/shard_map/slice | solution.py:89
  43.3 3.4 %collective-permute-start = (f32[7,64,512]{2,1,0:T(8,128)S(1)}, f32[7,64,512]{2,1,0:T(8,128)S(1)}, u32[]{:S(2)}, u32[]{:S(2)}) collective-permute-start(f32[7,64,512]{2,1,0:T(8,128)S(1)} %constant_dynamic-slice_fusion.3), channel_id=1, source_target_pairs={{0,8},{8,16},{16,24},{1,9},{9,17},{17,25},{2,10},{10,18},{18,26},{... | collective-permute-start | bytes 2752520 | tf_op jit(solution)/shard_map/ppermute | solution.py:84
  46.8 1.5 collective-permute-start.1
  48.3 0.2 broadcast_multiply_fusion.1
  48.5 0.7 subtract_compare_fusion.14
  49.2 17.5 %collective-permute-done = f32[7,64,512]{2,1,0:T(8,128)S(1)} collective-permute-done((f32[7,64,512]{2,1,0:T(8,128)S(1)}, f32[7,64,512]{2,1,0:T(8,128)S(1)}, u32[]{:S(2)}, u32[]{:S(2)}) %collective-permute-start) | collective-permute-done | bytes 917536 | tf_op jit(solution)/shard_map/ppermute | solution.py:84
  66.8 21.6 %collective-permute-done.1 = f32[7,64,512]{2,1,0:T(8,128)S(1)} collective-permute-done((f32[7,64,512]{2,1,0:T(8,128)S(1)}, f32[7,64,512]{2,1,0:T(8,128)S(1)}, u32[]{:S(2)}, u32[]{:S(2)}) %collective-permute-start.1) | collective-permute-done | bytes 917536 | tf_op jit(solution)/shard_map/ppermute | solution.py:88
  88.5 0.4 select_select_fusion.2
  88.9 1.5 select_select_fusion.1
  90.4 0.8 broadcast_multiply_fusion
  91.3 1.0 collective-permute-done.2
  92.3 0.4 maximum_select_fusion
  92.8 0.4 fusion.80
  93.2 1.2 copy-done.2
  94.4 1.0 pad_maximum_fusion.1
  95.4 0.6 constant_dynamic-slice_fusion.1
  96.0 6.5 %fusion = f32[2,768,512]{2,1,0:T(8,128)S(1)} fusion(f32[2,768,1056]{2,1,0:T(8,128)S(1)} %bitcast.95, f32[1,1056,512]{2,1,0:T(8,128)S(1)} %bitcast.98, f32[1,1056,512]{2,1,0:T(8,128)S(1)} %bitcast.97), kind=kOutput, calls=%fused_computation.4 | convolution fusion | flops 4983914496 | bytes 13959168 | tf_op jit(solution)/shard_map/tmk,tkz->tmz/dot_general | solution.py:117
  102.5 3.5 %bitcast_divide_fusion = f32[2,256,512]{2,1,0:T(8,128)S(1)} fusion(f32[8,2,32,512]{3,2,0,1:T(8,128)S(1)} %copy-done.7, f32[2,3,256,512]{3,2,1,0:T(8,128)S(1)} %bitcast.100, f32[2,3,512,128]{3,2,1,0:T(8,128)S(1)} %copy-done.4, f32[2,3,512,128]{3,2,1,0:T(8,128)S(1)} %copy-done.5, f32[2,3,512,128]{3,2,1,0:T(8,128)S(1)} %copy-done.6, ...), kind=kOutput, calls=%fused_computation.35 | convolution fusion | flops 2420899840 | bytes 11534336 | tf_op jit(solution)/shard_map/tqmz,tqzn->tmn/dot_general | solution.py:119
  106.0 1.4 fusion.90
  107.4 2.9 %fusion.8 = f32[2,256,512]{2,1,0:T(8,128)S(1)} fusion(f32[2,3,256,512]{3,2,1,0:T(8,128)S(1)} %bitcast.96, f32[2,3,512,128]{3,2,1,0:T(8,128)S(1)} %copy-done.4, f32[2,3,512,128]{3,2,1,0:T(8,128)S(1)} %copy-done.5, f32[2,3,512,128]{3,2,1,0:T(8,128)S(1)} %copy-done.6, f32[2,3,512,128]{3,2,1,0:T(8,128)S(1)} %get-tuple-element.11, f32[2]{0:T(128)S(1)} %gather_fusion), kind=kOutput, calls=%fused_computation.33 | convolution fusion | flops 2420899840 | bytes 10485768 | tf_op jit(solution)/shard_map/tqmz,tqnz->tmn/dot_general | solution.py:128
  110.4 0.2 broadcast_in_dim.790
  110.7 0.7 dynamic_update_slice.6
  111.4 0.1 dynamic-slice_add_fusion
  111.5 0.7 dynamic_update_slice.7
  112.3 1.3 copy-done.3
  113.8 10.3 %all-gather = f32[8,2,2]{2,1,0:T(2,128)S(1)} all-gather(f32[1,2,2]{2,1,0:T(2,128)S(1)} %bitcast.183), channel_id=1, replica_groups=mesh['region'=4,'tile'=8] {'tile'}, dimensions={0}, use_global_device_ids=true | all-gather | bytes 144 | tf_op jit(solution)/shard_map/all_gather | solution.py:75
  124.5 23.6 %reduce-scatter.2.cloned.1.call-done = f32[8,16,512]{2,1,0:T(8,128)} async-done(((f32[8,128,512]{2,1,0:T(8,128)}), f32[8,16,512]{2,1,0:T(8,128)}) %reduce-scatter.2.cloned.1.call-update) | async-done | bytes 262160 | tf_op jit(solution)/shard_map/reduce_scatter | solution.py:135
  148.1 1.8 %multiply_divide_fusion = f32[8,16,512]{2,1,0:T(8,128)} fusion(f32[8,16,512]{2,1,0:T(8,128)S(1)} %copy-done.8, f32[8,16,512]{2,1,0:T(8,128)} %reduce-scatter.2.cloned.1.call-done, f32[16]{0:T(128)S(1)} %broadcast_add_fusion.2), kind=kLoop, calls=%fused_computation.39 | loop fusion | flops 196608 | bytes 786496 | tf_op jit(solution)/shard_map/div | solution.py:141
  (93 shorter events, 5.3 us)
Async XLA Ops:
  6.5 2.9 %copy-start = (f32[6,3,3,15]{3,2,1,0:T(4,128)S(1)}, f32[6,3,3,15]{3,2,1,0:T(4,128)}, u32[]{:S(2)}) copy-start(f32[6,3,3,15]{3,2,1,0:T(4,128)} %param.10) | copy-start | bytes 9724
  6.5 16.6 %copy-start.1 = (f32[6]{0:T(128)S(1)}, f32[6]{0:T(128)}, u32[]{:S(2)}) copy-start(f32[6]{0:T(128)} %param.11) | copy-start | bytes 76
  6.5 34.3 %all-gather.3.cloned.1.call-start = ((), (), s32[]{:S(2)}) async-start(), calls=%async_computation.1 | async-start | bytes 2359296 | tf_op jit(solution)/shard_map/all_gather | solution.py:79
  7.3 140.9 %reduce-scatter.2.cloned.1.call-start = ((), (), s32[]{:S(2)}) async-start(), calls=%async_computation.2 | async-start | bytes 2359296 | tf_op jit(solution)/shard_map/reduce_scatter | solution.py:135
  43.3 23.3 %collective-permute-start = (f32[7,64,512]{2,1,0:T(8,128)S(1)}, f32[7,64,512]{2,1,0:T(8,128)S(1)}, u32[]{:S(2)}, u32[]{:S(2)}) collective-permute-start(f32[7,64,512]{2,1,0:T(8,128)S(1)} %constant_dynamic-slice_fusion.3), channel_id=1, source_target_pairs={{0,8},{8,16},{16,24},{1,9},{9,17},{17,25},{2,10},{10,18},{18,26},{... | collective-permute-start | bytes 2752520 | tf_op jit(solution)/shard_map/ppermute | solution.py:84
  46.8 41.6 %collective-permute-start.1 = (f32[7,64,512]{2,1,0:T(8,128)S(1)}, f32[7,64,512]{2,1,0:T(8,128)S(1)}, u32[]{:S(2)}, u32[]{:S(2)}) collective-permute-start(f32[7,64,512]{2,1,0:T(8,128)S(1)} %constant_dynamic-slice_fusion.2), channel_id=1, source_target_pairs={{8,0},{16,8},{24,16},{9,1},{17,9},{25,17},{10,2},{18,10},{26,18},{... | collective-permute-start | bytes 2752520 | tf_op jit(solution)/shard_map/ppermute | solution.py:88
  88.5 3.9 %collective-permute-start.2 = (f32[14,64,512]{2,1,0:T(8,128)S(1)}, f32[14,64,512]{2,1,0:T(8,128)S(1)}, u32[]{:S(2)}, u32[]{:S(2)}) collective-permute-start(f32[14,64,512]{2,1,0:T(8,128)S(1)} %constant_dynamic-update-slice_fusion), channel_id=1, source_target_pairs={{0,1},{1,0},{2,3},{3,2},{4,5},{5,4},{6,7},{7,6},{8,9},{9,8},{10,11... | collective-permute-start | bytes 5505032 | tf_op jit(solution)/shard_map/ppermute | solution.py:93
  92.8 1.6 %copy-start.2 = (f32[8,128,512]{2,1,0:T(8,128)S(1)}, f32[8,128,512]{2,1,0:T(8,128)}, u32[]{:S(2)}) copy-start(f32[8,128,512]{2,1,0:T(8,128)} %all-gather.3.cloned.1.call-done) | copy-start | bytes 6291460
  96.0 6.5 %copy-start.4 = (f32[2,3,512,128]{3,2,1,0:T(8,128)S(1)}, f32[2,3,512,128]{3,2,1,0:T(8,128)}, u32[]{:S(2)}) copy-start(f32[2,3,512,128]{3,2,1,0:T(8,128)} %get-tuple-element.12) | copy-start | bytes 4718596
  96.0 6.5 %copy-start.5 = (f32[2,3,512,128]{3,2,1,0:T(8,128)S(1)}, f32[2,3,512,128]{3,2,1,0:T(8,128)}, u32[]{:S(2)}) copy-start(f32[2,3,512,128]{3,2,1,0:T(8,128)} %get-tuple-element.13) | copy-start | bytes 4718596
  96.0 6.5 %copy-start.6 = (f32[2,3,512,128]{3,2,1,0:T(8,128)S(1)}, f32[2,3,512,128]{3,2,1,0:T(8,128)}, u32[]{:S(2)}) copy-start(f32[2,3,512,128]{3,2,1,0:T(8,128)} %get-tuple-element.14) | copy-start | bytes 4718596
  96.0 6.5 %copy-start.7 = (f32[8,2,32,512]{3,2,0,1:T(8,128)S(1)}, f32[8,2,32,512]{3,2,0,1:T(8,128)}, u32[]{:S(2)}) copy-start(f32[8,2,32,512]{3,2,0,1:T(8,128)} %copy.193) | copy-start | bytes 3145732
  111.5 36.6 %copy-start.8 = (f32[8,16,512]{2,1,0:T(8,128)S(1)}, f32[8,16,512]{2,1,0:T(8,128)}, u32[]{:S(2)}) copy-start(f32[8,16,512]{2,1,0:T(8,128)} %param.6) | copy-start | bytes 786436
  112.3 1.3 copy-start.3
Sparse Core Ops, SparseCore 0:
  9.0 31.7 all-gather.2
  113.8 34.2 reduce-scatter.1

commit v5 on v3

--- a/solution.py
+++ b/solution.py
@@ -87,29 +87,43 @@
 
     starts = jnp.clip(tile_offset - rim, 0, region_rows - win_rows)
     shifts = tile_offset - rim - starts
-    windows = jnp.stack(
-        [lax.dynamic_slice_in_dim(gathered, starts[j], win_rows, 1) for j in range(tile_count)]
-    ).reshape(tile_count, win_x * win_rows, depth)
 
     kxy = kron_band(ax, ay, block_x, tile_rows, win_rows, win_x * win_rows, 0, shifts[:, None]).reshape(
         tile_count, rank_terms * block_x * tile_rows, win_x * win_rows
     )
+    fxy = kron_band(ax[..., ::-1], ay[..., ::-1], block_x, tile_rows, tile_rows, block_x * tile_rows, -rim, -rim)
     tz = depth_band(az, depth, 128)
 
     cells = block_x * tile_rows
-    part = jnp.einsum("tmk,tkz->tmz", kxy, windows, precision=MATMUL_PRECISION)
-    part = part.reshape(tile_count, rank_terms, cells, depth)
-    blurred = jnp.einsum("tqmz,tqzn->tmn", part, tz, precision=MATMUL_PRECISION)
+    fxy = fxy.reshape(tile_count, rank_terms * cells, cells)
+    obs = observed.transpose(1, 0, 2, 3).reshape(tile_count, cells, depth)
 
-    quotient = observed.transpose(1, 0, 2, 3).reshape(tile_count, cells, depth) / blurred
+    out_block = 256 if depth % 256 == 0 else depth
+    reach = 128
 
-    fxy = kron_band(ax[..., ::-1], ay[..., ::-1], block_x, tile_rows, tile_rows, cells, -rim, -rim).reshape(
-        tile_count, rank_terms * cells, cells
-    )
-    part = jnp.einsum("tmk,tkz->tmz", fxy, quotient, precision=MATMUL_PRECISION)
-    part = part.reshape(tile_count, rank_terms, cells, depth)
-    correction = jnp.einsum("tqmz,tqnz->tmn", part, tz, precision=MATMUL_PRECISION)
-    weighted = (weight[:, None, None] * correction).reshape(tile_count, block_x, tile_rows, depth)
+    def along_depth(part, mats, flipped):
+        pieces = []
+        for b in range(depth // out_block):
+            lo = max(b * out_block - reach, 0)
+            hi = min((b + 1) * out_block + reach, depth)
+            cols = slice(b * out_block, (b + 1) * out_block)
+            if flipped:
+                m = mats[:, cols, lo:hi]
+                pieces.append(jnp.einsum("qmz,qnz->mn", part[:, :, lo:hi], m, precision=MATMUL_PRECISION))
+            else:
+                m = mats[:, lo:hi, cols]
+                pieces.append(jnp.einsum("qmz,qzn->mn", part[:, :, lo:hi], m, precision=MATMUL_PRECISION))
+        return jnp.concatenate(pieces, axis=-1)
+
+    weighted = []
+    for j in range(tile_count):
+        window = lax.dynamic_slice_in_dim(gathered, starts[j], win_rows, 1).reshape(win_x * win_rows, depth)
+        part = jnp.dot(kxy[j], window, precision=MATMUL_PRECISION).reshape(rank_terms, cells, depth)
+        blurred = along_depth(part, tz[j], False)
+        quotient = obs[j] / blurred
+        part = jnp.dot(fxy[j], quotient, precision=MATMUL_PRECISION).reshape(rank_terms, cells, depth)
+        correction = along_depth(part, tz[j], True)
+        weighted.append((weight[j] * correction).reshape(block_x, tile_rows, depth))
 
     numerator = jnp.zeros((block_x, region_rows, depth), jnp.float32)
     for j in range(tile_count):

time: 153 us -> 156 us (1.020)
  local copies, waits for them, and re-layouts: 19.6 us -> 25.4 us
  waiting for transfers between devices: 68.3 us -> 65.5 us
    slice x1 -> x3, local copies, waits for them, and re-layouts: 0.07 us -> 5.43 us  [the longest x1 3.48 us: on_device(): kxy[j]]
    all_gather x1, waiting for transfers between devices: 33.1 us -> 30.2 us  [on_device(): gathered = lax.all_gather(rimmed, 'tile', axis=1, tiled=True)]
    mul x2, other arithmetic: 3.92 us -> 1.1 us  [kron_band(): return ea[..., :, None, :] * eb[..., None, :, :]]
    squeeze x0 -> x1, local copies, waits for them, and re-layouts: none -> 2.36 us  [on_device(): blurred = along_depth(part, tz[j], False)]
    slice x1, local copies, waits for them, and re-layouts: 2.4 us -> 0.56 us  [depth_band(): cols.append(col[..., block:block + depth, :])]
    dot_general x4 -> x12, matrix products: 14.7 us -> 15.5 us  [the longest x2 6.67 us: on_device(): jnp.dot(kxy[j], window, precision=MATMUL_PRECISION)]
    unnamed x27 -> x30, local copies, waits for them, and re-layouts: 3.85 us -> 3.4 us
  transfers between devices with their start and end apart: 4 -> 4, of which waited for: 4 -> 4; matrix products, arithmetic and copies ran while one was open for 13% -> 15% of each run, Pallas kernels for 0% -> 0%
where the time goes in v5:
time: 156 us
  waiting for transfers between devices  65.5 us (42%)
  local copies, waits for them, and re-layouts  25.4 us (16%)
  between operations  21.6 us (14%)
  matrix products  15.5 us (10%)
  other arithmetic  12.5 us (8%)
  blocking collectives  9.18 us (6%)
  starting transfers between devices  6.19 us (4%)
    all_gather x1, waiting for transfers between devices, on_device(): gathered = lax.all_gather(rimmed, 'tile', axis=1, tiled=True)  30.2 us
    reduce_scatter x1, waiting for transfers between devices, on_device(): lax.psum_scatter(numerator, 'tile', scatter_dimension=1, tiled=True)  24.9 us
    all_gather x1, blocking collectives, on_device(): all_info = lax.all_gather(tile_info, 'tile', tiled=True)  9.18 us
    ppermute x1, waiting for transfers between devices, with_halo(): lax.ppermute(head, axis, [((i + 1) % count, i) for i in range(ends)])  6.86 us
    dot_general x2, matrix products, on_device(): jnp.dot(kxy[j], window, precision=MATMUL_PRECISION)  6.67 us
    ppermute x1, starting transfers between devices, with_halo(): lax.ppermute(tail, axis, [(i, (i + 1) % count) for i in range(ends)])  4.86 us
    dot_general x4, matrix products, along_depth(): jnp.einsum('qmz,qnz->mn', part[:, :, lo:hi], m, precision=MATMUL_PRECISION)  3.9 us
    ppermute x1, waiting for transfers between devices, with_halo(): lax.ppermute(tail, axis, [(i, (i + 1) % count) for i in range(ends)])  3.53 us
  transfers between devices with their start and end apart: 4, of which 4 were waited for; matrix products, arithmetic and copies ran while one was open for 15% of the time, Pallas kernels for 0%

profile of v5, /device:TPU:0, one launch (start us, length us, event | category | flops | bytes accessed | tf_op | source)
XLA Modules:
  0.0 155.9 jit_solution(2771991538121517087)
XLA Ops:
  6.5 1.1 fusion.95
  7.7 4.9 %collective-permute-start = (f32[7,16,512]{2,1,0:T(8,128)S(1)}, f32[7,16,512]{2,1,0:T(8,128)S(1)}, u32[]{:S(2)}, u32[]{:S(2)}) collective-permute-start(f32[7,16,512]{2,1,0:T(8,128)S(1)} %get-tuple-element.19), channel_id=1, source_target_pairs={{0,8},{8,16},{16,24},{1,9},{9,17},{17,25},{2,10},{10,18},{18,26},{... | collective-permute-start | bytes 688136 | tf_op jit(solution)/shard_map/ppermute | solution.py:18
  12.5 1.3 collective-permute-start.1
  13.8 3.5 %collective-permute-done = f32[7,16,512]{2,1,0:T(8,128)S(1)} collective-permute-done((f32[7,16,512]{2,1,0:T(8,128)S(1)}, f32[7,16,512]{2,1,0:T(8,128)S(1)}, u32[]{:S(2)}, u32[]{:S(2)}) %collective-permute-start) | collective-permute-done | bytes 229408 | tf_op jit(solution)/shard_map/ppermute | solution.py:18
  17.4 6.9 %collective-permute-done.1 = f32[7,16,512]{2,1,0:T(8,128)S(1)} collective-permute-done((f32[7,16,512]{2,1,0:T(8,128)S(1)}, f32[7,16,512]{2,1,0:T(8,128)S(1)}, u32[]{:S(2)}, u32[]{:S(2)}) %collective-permute-start.1) | collective-permute-done | bytes 229408 | tf_op jit(solution)/shard_map/ppermute | solution.py:20
  24.2 2.0 %pad_maximum_fusion.1 = f32[22,16,512]{2,1,0:T(8,128)} fusion(f32[7,16,512]{2,1,0:T(8,128)S(1)} %collective-permute-done.1, f32[8,16,512]{2,1,0:T(8,128)} %param.6, f32[7,16,512]{2,1,0:T(8,128)S(1)} %collective-permute-done), kind=kLoop, calls=%fused_computation.52 | loop fusion | flops 360448 | bytes 1441792 | tf_op jit(solution)/shard_map/concatenate | solution.py:16
  26.3 0.6 fusion.103
  29.4 0.7 fusion.102
  32.7 0.6 gather_fusion.1
  38.0 0.6 gather_fusion
  41.3 0.6 fusion.101
  42.2 0.4 select_select_fusion.3
  42.6 0.6 fusion.39
  43.4 1.5 select_select_fusion
  44.9 0.6 pad_slice_fusion.3
  45.4 0.6 pad_maximum_fusion
  46.1 1.4 fusion.94
  47.5 2.4 %slice_bitcast_fusion = (f32[3,512,512]{2,1,0:T(8,128)}, f32[3,512,512]{2,1,0:T(8,128)S(1)}) fusion(f32[2,3,512,512]{3,2,1,0:T(8,128)S(1)} %pad_maximum_fusion), kind=kLoop, calls=%fused_computation.4 | loop fusion | bytes 12582912 | tf_op jit(solution)/shard_map/squeeze | solution.py:122
  49.9 0.4 select_select_fusion.2
  50.3 0.7 subtract_compare_fusion.14
  50.9 1.5 select_select_fusion.1
  52.4 0.9 broadcast_multiply_fusion
  53.3 3.5 %fusion.93 = (f32[1,3,8,32,1056]{4,3,2,1,0:T(8,128)}, f32[1,3,8,32,1056]{4,3,2,1,0:T(8,128)}) fusion(f32[2,3,8,32,1056]{4,3,2,1,0:T(8,128)S(1)} %broadcast_multiply_fusion), kind=kLoop, calls=%fused_computation.162 | loop fusion | bytes 12976128 | tf_op jit(solution)/shard_map/slice | solution.py:121
  56.8 30.2 %all-gather.3.cloned.1.call-done = f32[22,128,512]{2,1,0:T(8,128)} async-done(((f32[22,16,512]{2,1,0:T(8,128)}), f32[22,128,512]{2,1,0:T(8,128)}) %all-gather.3.cloned.1.call-update) | async-done | bytes 5767184 | tf_op jit(solution)/shard_map/all_gather | solution.py:80
  87.1 3.5 %constant_dynamic-slice_fusion = (f32[22,48,512]{2,1,0:T(8,128)S(1)}, f32[22,48,512]{2,1,0:T(8,128)S(1)}) fusion(f32[22,128,512]{2,1,0:T(8,128)} %all-gather.3.cloned.1.call-done, s32[]{:T(128)S(6)} %select_n.686, s32[]{:T(128)S(6)} %select_n.668), kind=kLoop, calls=%fused_computation.152 | loop fusion | bytes 8650760 | tf_op jit(solution)/shard_map/dynamic_slice | solution.py:120
  90.6 3.3 %fusion.104 = f32[3,256,512]{2,1,0:T(8,128)S(1)} fusion(f32[3,256,1056]{2,1,0:T(8,128)S(1)} %bitcast.132, f32[1056,512,1]{1,0,2:T(8,128)S(1)} %bitcast.134), kind=kOutput, calls=%fused_computation.173 | convolution fusion | flops 2491416576 | bytes 6979584 | tf_op jit(solution)/shard_map/dot_general | solution.py:121
  93.9 0.8 fusion.21
  94.7 0.8 fusion.18
  95.5 0.4 copy-done.4
  95.9 3.3 %fusion.106 = f32[3,256,512]{2,1,0:T(8,128)S(1)} fusion(f32[3,256,1056]{2,1,0:T(8,128)S(1)} %bitcast.131, f32[1056,512,1]{1,0,2:T(8,128)S(1)} %bitcast.133), kind=kOutput, calls=%fused_computation.175 | convolution fusion | flops 2491416576 | bytes 6979584 | tf_op jit(solution)/shard_map/dot_general | solution.py:121
  99.3 1.0 fusion.9
  100.3 0.8 fusion.6
  101.1 0.5 copy-done.10
  101.7 0.9 copy-done.9
  102.6 0.8 fusion.107
  103.4 0.8 fusion.3
  104.3 1.5 fusion
  105.8 0.8 fusion.105
  106.6 0.8 fusion.15
  107.4 0.8 fusion.12
  108.2 0.7 maximum_multiply_fusion
  109.2 0.7 dynamic_update_slice.6
  109.9 0.6 fusion.24
  110.6 0.7 dynamic_update_slice.7
  111.4 1.4 copy-done.6
  112.9 9.2 %all-gather = f32[8,2,2]{2,1,0:T(2,128)S(1)} all-gather(f32[1,2,2]{2,1,0:T(2,128)S(1)} %bitcast.228), channel_id=1, replica_groups=mesh['region'=4,'tile'=8] {'tile'}, dimensions={0}, use_global_device_ids=true | all-gather | bytes 144 | tf_op jit(solution)/shard_map/all_gather | solution.py:75
  122.4 24.9 %reduce-scatter.2.cloned.1.call-done = f32[8,16,512]{2,1,0:T(8,128)} async-done(((f32[8,128,512]{2,1,0:T(8,128)}), f32[8,16,512]{2,1,0:T(8,128)}) %reduce-scatter.2.cloned.1.call-update) | async-done | bytes 262160 | tf_op jit(solution)/shard_map/reduce_scatter | solution.py:132
  147.3 1.8 %multiply_divide_fusion = f32[8,16,512]{2,1,0:T(8,128)} fusion(f32[8,16,512]{2,1,0:T(8,128)S(1)} %copy-done.7, f32[8,16,512]{2,1,0:T(8,128)} %reduce-scatter.2.cloned.1.call-done, f32[16]{0:T(128)S(1)} %broadcast_add_fusion.2), kind=kLoop, calls=%fused_computation.58 | loop fusion | flops 196608 | bytes 786496 | tf_op jit(solution)/shard_map/div | solution.py:138
  (108 shorter events, 6.5 us)
Async XLA Ops:
  6.5 26.1 %copy-start = (f32[6,3,3,15]{3,2,1,0:T(4,128)S(1)}, f32[6,3,3,15]{3,2,1,0:T(4,128)}, u32[]{:S(2)}) copy-start(f32[6,3,3,15]{3,2,1,0:T(4,128)} %param.10) | copy-start | bytes 9724
  6.5 19.7 %copy-start.12 = (s32[2]{0:T(128)S(1)}, s32[2]{0:T(128)}, u32[]{:S(2)}) copy-start(s32[2]{0:T(128)} %param.8) | copy-start | bytes 28
  6.5 19.7 %copy-start.13 = (s32[2]{0:T(128)S(1)}, s32[2]{0:T(128)}, u32[]{:S(2)}) copy-start(s32[2]{0:T(128)} %param.9) | copy-start | bytes 28
  6.5 80.5 %all-gather.3.cloned.1.call-start = ((), (), s32[]{:S(2)}) async-start(), calls=%async_computation.1 | async-start | bytes 6488064 | tf_op jit(solution)/shard_map/all_gather | solution.py:80
  7.7 30.4 %copy-start.2 = (f32[6]{0:T(128)S(1)}, f32[6]{0:T(128)}, u32[]{:S(2)}) copy-start(f32[6]{0:T(128)} %param.11) | copy-start | bytes 76
  7.7 9.7 %collective-permute-start = (f32[7,16,512]{2,1,0:T(8,128)S(1)}, f32[7,16,512]{2,1,0:T(8,128)S(1)}, u32[]{:S(2)}, u32[]{:S(2)}) collective-permute-start(f32[7,16,512]{2,1,0:T(8,128)S(1)} %get-tuple-element.19), channel_id=1, source_target_pairs={{0,8},{8,16},{16,24},{1,9},{9,17},{17,25},{2,10},{10,18},{18,26},{... | collective-permute-start | bytes 688136 | tf_op jit(solution)/shard_map/ppermute | solution.py:18
  12.5 11.7 %collective-permute-start.1 = (f32[7,16,512]{2,1,0:T(8,128)S(1)}, f32[7,16,512]{2,1,0:T(8,128)S(1)}, u32[]{:S(2)}, u32[]{:S(2)}) collective-permute-start(f32[7,16,512]{2,1,0:T(8,128)S(1)} %get-tuple-element.20), channel_id=1, source_target_pairs={{8,0},{16,8},{24,16},{9,1},{17,9},{25,17},{10,2},{18,10},{26,18},{... | collective-permute-start | bytes 688136 | tf_op jit(solution)/shard_map/ppermute | solution.py:20
  26.2 121.0 %reduce-scatter.2.cloned.1.call-start = ((), (), s32[]{:S(2)}) async-start(), calls=%async_computation.2 | async-start | bytes 2359296 | tf_op jit(solution)/shard_map/reduce_scatter | solution.py:132
  87.0 3.5 %copy-start.5 = (f32[1,3,8,32,1056]{4,3,2,1,0:T(8,128)S(1)}, f32[1,3,8,32,1056]{4,3,2,1,0:T(8,128)}, u32[]{:S(2)}) copy-start(f32[1,3,8,32,1056]{4,3,2,1,0:T(8,128)} %get-tuple-element.6) | copy-start | bytes 9732100
  93.9 2.0 %copy-start.4 = (f32[1,3,8,32,1056]{4,3,2,1,0:T(8,128)S(1)}, f32[1,3,8,32,1056]{4,3,2,1,0:T(8,128)}, u32[]{:S(2)}) copy-start(f32[1,3,8,32,1056]{4,3,2,1,0:T(8,128)} %get-tuple-element.5) | copy-start | bytes 9732100
  95.9 3.3 %copy-start.3 = (f32[3,512,512]{2,1,0:T(8,128)S(1)}, f32[3,512,512]{2,1,0:T(8,128)}, u32[]{:S(2)}) copy-start(f32[3,512,512]{2,1,0:T(8,128)} %get-tuple-element.7) | copy-start | bytes 9437188
  100.3 1.2 copy-start.10
  101.5 1.1 copy-start.9
  104.2 1.5 copy-start.8
  108.9 1.0 copy-start.11
  110.6 36.7 %copy-start.7 = (f32[8,16,512]{2,1,0:T(8,128)S(1)}, f32[8,16,512]{2,1,0:T(8,128)}, u32[]{:S(2)}) copy-start(f32[8,16,512]{2,1,0:T(8,128)} %param.6) | copy-start | bytes 786436
  110.6 38.4 %copy-start.1 = (f32[6,3,3,15]{3,2,1,0:T(4,128)S(1)}, f32[6,3,3,15]{3,2,1,0:T(4,128)}, u32[]{:S(2)}) copy-start(f32[6,3,3,15]{3,2,1,0:T(4,128)} %param.10) | copy-start | bytes 9724
  111.4 1.4 copy-start.6
Sparse Core Ops, SparseCore 0:
  26.3 60.6 all-gather.2
  112.9 34.3 reduce-scatter.1

commit v6 on v3

--- a/solution.py
+++ b/solution.py
@@ -22,6 +22,21 @@
             axis=dim,
         )
     return cells
+
+
+def split_bf16(values):
+    high = values.astype(jnp.bfloat16)
+    return high, (values - high.astype(jnp.float32)).astype(jnp.bfloat16)
+
+
+def dot_rounded_data(spec, data, taps, data_first):
+    data_high = data.astype(jnp.bfloat16)
+    taps_high, taps_low = split_bf16(taps)
+    if data_first:
+        terms = [(data_high, taps_high), (data_high, taps_low)]
+    else:
+        terms = [(taps_high, data_high), (taps_low, data_high)]
+    return sum(jnp.einsum(spec, a, b, preferred_element_type=jnp.float32) for a, b in terms)
 
 
 def kron_band(taps_a, taps_b, rows_a, rows_b, span_b, cols, shift_a, shift_b):
@@ -99,14 +114,14 @@
     cells = block_x * tile_rows
     part = jnp.einsum("tmk,tkz->tmz", kxy, windows, precision=MATMUL_PRECISION)
     part = part.reshape(tile_count, rank_terms, cells, depth)
-    blurred = jnp.einsum("tqmz,tqzn->tmn", part, tz, precision=MATMUL_PRECISION)
+    blurred = dot_rounded_data("tqmz,tqzn->tmn", part, tz, True)
 
     quotient = observed.transpose(1, 0, 2, 3).reshape(tile_count, cells, depth) / blurred
 
     fxy = kron_band(ax[..., ::-1], ay[..., ::-1], block_x, tile_rows, tile_rows, cells, -rim, -rim).reshape(
         tile_count, rank_terms * cells, cells
     )
-    part = jnp.einsum("tmk,tkz->tmz", fxy, quotient, precision=MATMUL_PRECISION)
+    part = dot_rounded_data("tmk,tkz->tmz", quotient, fxy, False)
     part = part.reshape(tile_count, rank_terms, cells, depth)
     correction = jnp.einsum("tqmz,tqnz->tmn", part, tz, precision=MATMUL_PRECISION)
     weighted = (weight[:, None, None] * correction).reshape(tile_count, block_x, tile_rows, depth)

time: 153 us -> 152 us (level)
    dot_general x2 -> x4, matrix products: 4.9 us -> 3.53 us  [dot_rounded_data(): jnp.einsum(spec, a, b, preferred_element_type=jnp.float32)]
    unnamed x27 -> x28, local copies, waits for them, and re-layouts: 3.85 us -> 3.18 us
  transfers between devices with their start and end apart: 4 -> 4, of which waited for: 4 -> 4; matrix products, arithmetic and copies ran while one was open for 13% -> 14% of each run, Pallas kernels for 0% -> 0%
where the time goes in v6:
time: 152 us
  waiting for transfers between devices  67.1 us (44%)
  between operations  21.6 us (14%)
  local copies, waits for them, and re-layouts  20.2 us (13%)
  other arithmetic  14.5 us (10%)
  matrix products  13.2 us (9%)
  blocking collectives  9.18 us (6%)
  starting transfers between devices  6.32 us (4%)
    all_gather x1, waiting for transfers between devices, on_device(): gathered = lax.all_gather(rimmed, 'tile', axis=1, tiled=True)  31.8 us
    reduce_scatter x1, waiting for transfers between devices, on_device(): lax.psum_scatter(numerator, 'tile', scatter_dimension=1, tiled=True)  24.8 us
    all_gather x1, blocking collectives, on_device(): all_info = lax.all_gather(tile_info, 'tile', tiled=True)  9.18 us
    ppermute x1, waiting for transfers between devices, with_halo(): lax.ppermute(head, axis, [((i + 1) % count, i) for i in range(ends)])  6.86 us
    dot_general x1, matrix products, on_device(): part = jnp.einsum('tmk,tkz->tmz', kxy, windows, precision=MATMUL_PRECISION)  6.71 us
    ppermute x1, starting transfers between devices, with_halo(): lax.ppermute(tail, axis, [(i, (i + 1) % count) for i in range(ends)])  4.99 us
    mul x2, other arithmetic, kron_band(): return ea[..., :, None, :] * eb[..., None, :, :]  3.93 us
    dot_general x4, matrix products, dot_rounded_data(): jnp.einsum(spec, a, b, preferred_element_type=jnp.float32)  3.53 us
  transfers between devices with their start and end apart: 4, of which 4 were waited for; matrix products, arithmetic and copies ran while one was open for 14% of the time, Pallas kernels for 0%

profile of v6, /device:TPU:0, one launch (start us, length us, event | category | flops | bytes accessed | tf_op | source)
XLA Modules:
  0.0 152.0 jit_solution(15761517896845455169)
XLA Ops:
  6.5 1.1 fusion.93
  7.7 5.0 %collective-permute-start = (f32[7,16,512]{2,1,0:T(8,128)S(1)}, f32[7,16,512]{2,1,0:T(8,128)S(1)}, u32[]{:S(2)}, u32[]{:S(2)}) collective-permute-start(f32[7,16,512]{2,1,0:T(8,128)S(1)} %get-tuple-element.15), channel_id=1, source_target_pairs={{0,8},{8,16},{16,24},{1,9},{9,17},{17,25},{2,10},{10,18},{18,26},{... | collective-permute-start | bytes 688136 | tf_op jit(solution)/shard_map/ppermute | solution.py:18
  12.7 1.3 collective-permute-start.1
  14.0 3.5 %collective-permute-done = f32[7,16,512]{2,1,0:T(8,128)S(1)} collective-permute-done((f32[7,16,512]{2,1,0:T(8,128)S(1)}, f32[7,16,512]{2,1,0:T(8,128)S(1)}, u32[]{:S(2)}, u32[]{:S(2)}) %collective-permute-start) | collective-permute-done | bytes 229408 | tf_op jit(solution)/shard_map/ppermute | solution.py:18
  17.5 6.9 %collective-permute-done.1 = f32[7,16,512]{2,1,0:T(8,128)S(1)} collective-permute-done((f32[7,16,512]{2,1,0:T(8,128)S(1)}, f32[7,16,512]{2,1,0:T(8,128)S(1)}, u32[]{:S(2)}, u32[]{:S(2)}) %collective-permute-start.1) | collective-permute-done | bytes 229408 | tf_op jit(solution)/shard_map/ppermute | solution.py:20
  24.4 1.9 %pad_maximum_fusion.4 = f32[22,16,512]{2,1,0:T(8,128)} fusion(f32[7,16,512]{2,1,0:T(8,128)S(1)} %collective-permute-done.1, f32[8,16,512]{2,1,0:T(8,128)} %param.6, f32[7,16,512]{2,1,0:T(8,128)S(1)} %collective-permute-done), kind=kLoop, calls=%fused_computation.47 | loop fusion | flops 360448 | bytes 1441792 | tf_op jit(solution)/shard_map/concatenate | solution.py:16
  26.4 0.6 fusion.100
  29.4 0.6 fusion.99
  32.8 0.6 gather_fusion.1
  33.4 0.1 fusion.98
  33.5 0.1 copy.179
  33.6 0.1 copy.180
  33.7 0.1 copy.181
  35.0 0.1 fusion.97
  35.1 0.1 copy.163
  36.6 0.1 fusion.96
  36.7 0.1 copy.197
  38.2 1.1 copy.194
  39.3 0.6 gather_fusion
  42.6 0.2 select_select_fusion.4
  42.9 0.4 select_select_fusion.3
  43.3 0.6 fusion.34
  43.8 0.2 broadcast_multiply_fusion.1
  44.1 1.5 select_select_fusion
  45.5 2.2 %pad_slice_fusion.3 = (f32[2,3,512,128]{3,2,1,0:T(8,128)S(1)}, f32[2,3,512,128]{3,2,1,0:T(8,128)S(1)}, f32[2,3,512,128]{3,2,1,0:T(8,128)}, f32[2,3,512,128]{3,2,1,0:T(8,128)}) fusion(f32[2,3,384,128]{3,2,1,0:T(8,128)S(1)} %select_select_fusion), kind=kLoop, calls=%fused_computation.13 | loop fusion | bytes 7471104 | tf_op jit(solution)/shard_map/slice | solution.py:73
  47.7 1.3 fusion.8
  49.1 0.4 select_select_fusion.2
  49.5 0.7 subtract_compare_fusion.14
  50.2 1.4 select_select_fusion.1
  51.6 3.7 %broadcast_multiply_fusion = f32[2,3,8,32,1056]{4,3,2,1,0:T(8,128)} fusion(f32[2,3,32,1056]{3,2,1,0:T(8,128)S(1)} %select_select_fusion.1, f32[2,3,8,1056]{3,2,1,0:T(8,128)S(1)} %select_select_fusion.2), kind=kLoop, calls=%fused_computation.8 | loop fusion | flops 1622016 | bytes 7501824 | tf_op jit(solution)/shard_map/mul | solution.py:56
  55.4 31.8 %all-gather.3.cloned.1.call-done = f32[22,128,512]{2,1,0:T(8,128)} async-done(((f32[22,16,512]{2,1,0:T(8,128)}), f32[22,128,512]{2,1,0:T(8,128)}) %all-gather.3.cloned.1.call-update) | async-done | bytes 5767184 | tf_op jit(solution)/shard_map/all_gather | solution.py:95
  87.2 3.5 %constant_dynamic-slice_fusion.1 = (f32[22,48,512]{2,1,0:T(8,128)S(1)}, f32[22,48,512]{2,1,0:T(8,128)S(1)}) fusion(f32[22,128,512]{2,1,0:T(8,128)} %all-gather.3.cloned.1.call-done, s32[]{:T(128)S(6)} %select_n.668, s32[]{:T(128)S(6)} %select_n.669), kind=kLoop, calls=%fused_computation.144 | loop fusion | bytes 8650760 | tf_op jit(solution)/shard_map/dynamic_slice | solution.py:106
  90.7 1.0 copy-done.2
  91.7 6.7 %fusion.5 = bf16[2,768,512]{2,1,0:T(8,128)(2,1)S(1)} fusion(f32[2,768,1056]{2,1,0:T(8,128)S(1)} %bitcast.108, f32[1,1056,512]{2,1,0:T(8,128)S(1)} %bitcast.111, f32[1,1056,512]{2,1,0:T(8,128)S(1)} %bitcast.110), kind=kOutput, calls=%fused_computation.30 | convolution fusion | flops 4984700928 | bytes 12386304 | tf_op jit(solution)/shard_map/tmk,tkz->tmz/dot_general | solution.py:115
  98.4 1.2 fusion.12
  99.7 1.2 fusion.19
  100.9 0.6 fusion.101
  101.5 0.6 copy-done.7
  102.0 0.6 convolution_add_fusion
  102.6 3.0 %fusion.16 = f32[2,256,512]{2,1,0:T(8,128)S(1)} fusion(f32[2,3,256,512]{3,2,1,0:T(8,128)S(1)} %bitcast.109, f32[2,3,512,128]{3,2,1,0:T(8,128)S(1)} %get-tuple-element.10, f32[2,3,512,128]{3,2,1,0:T(8,128)S(1)} %copy-done.4, f32[2,3,512,128]{3,2,1,0:T(8,128)S(1)} %copy-done.5, f32[2,3,512,128]{3,2,1,0:T(8,128)S(1)} %get-tuple-element.9, f32[2]{0:T(128)S(1)} %gather_fusion), kind=kOutput, calls=%fused_computation.40 | convolution fusion | flops 2420899840 | bytes 10485768 | tf_op jit(solution)/shard_map/tqmz,tqnz->tmn/dot_general | solution.py:126
  105.7 0.2 broadcast_in_dim.790
  105.9 0.7 dynamic_update_slice.6
  106.7 0.1 dynamic-slice_add_fusion
  106.8 0.7 dynamic_update_slice.7
  107.6 1.4 copy-done.3
  109.1 9.2 %all-gather = f32[8,2,2]{2,1,0:T(2,128)S(1)} all-gather(f32[1,2,2]{2,1,0:T(2,128)S(1)} %bitcast.198), channel_id=1, replica_groups=mesh['region'=4,'tile'=8] {'tile'}, dimensions={0}, use_global_device_ids=true | all-gather | bytes 144 | tf_op jit(solution)/shard_map/all_gather | solution.py:90
  118.6 24.8 %reduce-scatter.2.cloned.1.call-done = f32[8,16,512]{2,1,0:T(8,128)} async-done(((f32[8,128,512]{2,1,0:T(8,128)}), f32[8,16,512]{2,1,0:T(8,128)}) %reduce-scatter.2.cloned.1.call-update) | async-done | bytes 262160 | tf_op jit(solution)/shard_map/reduce_scatter | solution.py:133
  143.4 1.8 %multiply_divide_fusion = f32[8,16,512]{2,1,0:T(8,128)} fusion(f32[8,16,512]{2,1,0:T(8,128)S(1)} %copy-done.6, f32[8,16,512]{2,1,0:T(8,128)} %reduce-scatter.2.cloned.1.call-done, f32[16]{0:T(128)S(1)} %broadcast_add_fusion.2), kind=kLoop, calls=%fused_computation.49 | loop fusion | flops 196608 | bytes 786496 | tf_op jit(solution)/shard_map/div | solution.py:139
  (96 shorter events, 4.9 us)
Async XLA Ops:
  6.5 26.3 %copy-start = (f32[6,3,3,15]{3,2,1,0:T(4,128)S(1)}, f32[6,3,3,15]{3,2,1,0:T(4,128)}, u32[]{:S(2)}) copy-start(f32[6,3,3,15]{3,2,1,0:T(4,128)} %param.10) | copy-start | bytes 9724
  6.5 19.8 %copy-start.11 = (s32[2]{0:T(128)S(1)}, s32[2]{0:T(128)}, u32[]{:S(2)}) copy-start(s32[2]{0:T(128)} %param.8) | copy-start | bytes 28
  6.5 19.8 %copy-start.12 = (s32[2]{0:T(128)S(1)}, s32[2]{0:T(128)}, u32[]{:S(2)}) copy-start(s32[2]{0:T(128)} %param.9) | copy-start | bytes 28
  6.5 80.6 %all-gather.3.cloned.1.call-start = ((), (), s32[]{:S(2)}) async-start(), calls=%async_computation.1 | async-start | bytes 6488064 | tf_op jit(solution)/shard_map/all_gather | solution.py:95
  7.7 30.5 %copy-start.9 = (f32[8,2,32,512]{3,2,1,0:T(8,128)S(1)}, f32[8,2,32,512]{3,2,1,0:T(8,128)}, u32[]{:S(2)}) copy-start(f32[8,2,32,512]{3,2,1,0:T(8,128)} %param.7) | copy-start | bytes 3145732
  7.7 9.8 %collective-permute-start = (f32[7,16,512]{2,1,0:T(8,128)S(1)}, f32[7,16,512]{2,1,0:T(8,128)S(1)}, u32[]{:S(2)}, u32[]{:S(2)}) collective-permute-start(f32[7,16,512]{2,1,0:T(8,128)S(1)} %get-tuple-element.15), channel_id=1, source_target_pairs={{0,8},{8,16},{16,24},{1,9},{9,17},{17,25},{2,10},{10,18},{18,26},{... | collective-permute-start | bytes 688136 | tf_op jit(solution)/shard_map/ppermute | solution.py:18
  12.7 11.7 %collective-permute-start.1 = (f32[7,16,512]{2,1,0:T(8,128)S(1)}, f32[7,16,512]{2,1,0:T(8,128)S(1)}, u32[]{:S(2)}, u32[]{:S(2)}) collective-permute-start(f32[7,16,512]{2,1,0:T(8,128)S(1)} %get-tuple-element.16), channel_id=1, source_target_pairs={{8,0},{16,8},{24,16},{9,1},{17,9},{25,17},{10,2},{18,10},{26,18},{... | collective-permute-start | bytes 688136 | tf_op jit(solution)/shard_map/ppermute | solution.py:20
  26.3 13.0 %copy-start.1 = (f32[6]{0:T(128)S(1)}, f32[6]{0:T(128)}, u32[]{:S(2)}) copy-start(f32[6]{0:T(128)} %param.11) | copy-start | bytes 76
  26.3 117.1 %reduce-scatter.2.cloned.1.call-start = ((), (), s32[]{:S(2)}) async-start(), calls=%async_computation.2 | async-start | bytes 2359296 | tf_op jit(solution)/shard_map/reduce_scatter | solution.py:133
  87.2 4.5 %copy-start.2 = (f32[2,3,8,32,1056]{4,3,2,1,0:T(8,128)S(1)}, f32[2,3,8,32,1056]{4,3,2,1,0:T(8,128)}, u32[]{:S(2)}) copy-start(f32[2,3,8,32,1056]{4,3,2,1,0:T(8,128)} %broadcast_multiply_fusion) | copy-start | bytes 19464196
  91.7 6.7 %copy-start.4 = (f32[2,3,512,128]{3,2,1,0:T(8,128)S(1)}, f32[2,3,512,128]{3,2,1,0:T(8,128)}, u32[]{:S(2)}) copy-start(f32[2,3,512,128]{3,2,1,0:T(8,128)} %get-tuple-element.11) | copy-start | bytes 4718596
  91.7 6.7 %copy-start.5 = (f32[2,3,512,128]{3,2,1,0:T(8,128)S(1)}, f32[2,3,512,128]{3,2,1,0:T(8,128)}, u32[]{:S(2)}) copy-start(f32[2,3,512,128]{3,2,1,0:T(8,128)} %get-tuple-element.12) | copy-start | bytes 4718596
  98.4 1.2 copy-start.10
  99.7 1.2 copy-start.8
  100.9 1.1 copy-start.7
  106.8 36.6 %copy-start.6 = (f32[8,16,512]{2,1,0:T(8,128)S(1)}, f32[8,16,512]{2,1,0:T(8,128)}, u32[]{:S(2)}) copy-start(f32[8,16,512]{2,1,0:T(8,128)} %param.6) | copy-start | bytes 786436
  107.6 1.4 copy-start.3
Sparse Core Ops, SparseCore 0:
  26.4 60.6 all-gather.2
  109.1 34.3 reduce-scatter.1

commit v7 on v6

--- a/solution.py
+++ b/solution.py
@@ -25,8 +25,8 @@
 
 
 def split_bf16(values):
-    high = values.astype(jnp.bfloat16)
-    return high, (values - high.astype(jnp.float32)).astype(jnp.bfloat16)
+    high = lax.reduce_precision(values, exponent_bits=8, mantissa_bits=7)
+    return high.astype(jnp.bfloat16), (values - high).astype(jnp.bfloat16)
 
 
 def dot_rounded_data(spec, data, taps, data_first):

time: 152 us -> 153 us (level)
  no operation moved by 1% of the time
where the time goes in v7:
time: 153 us; the launch traced here: 152 us
  waiting for transfers between devices  67.1 us (44%)
  between operations  21.6 us (14%)
  local copies, waits for them, and re-layouts  20 us (13%)
  other arithmetic  14.6 us (10%)
  matrix products  13.2 us (9%)
  blocking collectives  9.38 us (6%)
  starting transfers between devices  6.32 us (4%)
    all_gather x1, waiting for transfers between devices, on_device(): gathered = lax.all_gather(rimmed, 'tile', axis=1, tiled=True)  31.7 us
    reduce_scatter x1, waiting for transfers between devices, on_device(): lax.psum_scatter(numerator, 'tile', scatter_dimension=1, tiled=True)  24.9 us
    all_gather x1, blocking collectives, on_device(): all_info = lax.all_gather(tile_info, 'tile', tiled=True)  9.38 us
    ppermute x1, waiting for transfers between devices, with_halo(): lax.ppermute(head, axis, [((i + 1) % count, i) for i in range(ends)])  6.86 us
    dot_general x1, matrix products, on_device(): part = jnp.einsum('tmk,tkz->tmz', kxy, windows, precision=MATMUL_PRECISION)  6.69 us
    ppermute x1, starting transfers between devices, with_halo(): lax.ppermute(tail, axis, [(i, (i + 1) % count) for i in range(ends)])  4.99 us
    mul x2, other arithmetic, kron_band(): return ea[..., :, None, :] * eb[..., None, :, :]  3.93 us
    dot_general x4, matrix products, dot_rounded_data(): jnp.einsum(spec, a, b, preferred_element_type=jnp.float32)  3.56 us
  transfers between devices with their start and end apart: 4, of which 4 were waited for; matrix products, arithmetic and copies ran while one was open for 14% of the time, Pallas kernels for 0%

profile of v7, /device:TPU:0, one launch (start us, length us, event | category | flops | bytes accessed | tf_op | source)
XLA Modules:
  0.0 152.2 jit_solution(11802011564227091052)
XLA Ops:
  6.5 1.1 fusion.99
  7.7 5.0 %collective-permute-start = (f32[7,16,512]{2,1,0:T(8,128)S(1)}, f32[7,16,512]{2,1,0:T(8,128)S(1)}, u32[]{:S(2)}, u32[]{:S(2)}) collective-permute-start(f32[7,16,512]{2,1,0:T(8,128)S(1)} %get-tuple-element.15), channel_id=1, source_target_pairs={{0,8},{8,16},{16,24},{1,9},{9,17},{17,25},{2,10},{10,18},{18,26},{... | collective-permute-start | bytes 688136 | tf_op jit(solution)/shard_map/ppermute | solution.py:18
  12.7 1.3 collective-permute-start.1
  14.0 3.5 %collective-permute-done = f32[7,16,512]{2,1,0:T(8,128)S(1)} collective-permute-done((f32[7,16,512]{2,1,0:T(8,128)S(1)}, f32[7,16,512]{2,1,0:T(8,128)S(1)}, u32[]{:S(2)}, u32[]{:S(2)}) %collective-permute-start) | collective-permute-done | bytes 229408 | tf_op jit(solution)/shard_map/ppermute | solution.py:18
  17.5 6.9 %collective-permute-done.1 = f32[7,16,512]{2,1,0:T(8,128)S(1)} collective-permute-done((f32[7,16,512]{2,1,0:T(8,128)S(1)}, f32[7,16,512]{2,1,0:T(8,128)S(1)}, u32[]{:S(2)}, u32[]{:S(2)}) %collective-permute-start.1) | collective-permute-done | bytes 229408 | tf_op jit(solution)/shard_map/ppermute | solution.py:20
  24.4 1.9 %pad_maximum_fusion.4 = f32[22,16,512]{2,1,0:T(8,128)} fusion(f32[7,16,512]{2,1,0:T(8,128)S(1)} %collective-permute-done.1, f32[8,16,512]{2,1,0:T(8,128)} %param.6, f32[7,16,512]{2,1,0:T(8,128)S(1)} %collective-permute-done), kind=kLoop, calls=%fused_computation.47 | loop fusion | flops 360448 | bytes 1441792 | tf_op jit(solution)/shard_map/concatenate | solution.py:16
  26.4 0.6 fusion.106
  29.4 0.6 fusion.105
  32.8 0.6 gather_fusion.1
  33.4 0.1 fusion.104
  33.5 0.1 copy.179
  33.6 0.1 copy.180
  33.7 0.1 copy.181
  35.0 0.1 fusion.103
  35.1 0.1 copy.163
  36.6 0.1 fusion.102
  36.7 0.1 copy.197
  38.2 1.1 copy.194
  39.3 0.6 gather_fusion
  42.6 0.2 select_select_fusion.4
  42.9 0.4 select_select_fusion.3
  43.3 0.6 fusion.40
  43.8 0.2 broadcast_multiply_fusion.1
  44.1 1.5 select_select_fusion
  45.5 2.2 %pad_slice_fusion.3 = (f32[2,3,512,128]{3,2,1,0:T(8,128)S(1)}, f32[2,3,512,128]{3,2,1,0:T(8,128)S(1)}, f32[2,3,512,128]{3,2,1,0:T(8,128)}, f32[2,3,512,128]{3,2,1,0:T(8,128)}) fusion(f32[2,3,384,128]{3,2,1,0:T(8,128)S(1)} %select_select_fusion), kind=kLoop, calls=%fused_computation.16 | loop fusion | bytes 7471104 | tf_op jit(solution)/shard_map/slice | solution.py:73
  47.7 1.4 fusion.11
  49.2 0.4 select_select_fusion.2
  49.6 0.7 subtract_compare_fusion.14
  50.3 1.4 select_select_fusion.1
  51.7 3.7 %broadcast_multiply_fusion = f32[2,3,8,32,1056]{4,3,2,1,0:T(8,128)} fusion(f32[2,3,32,1056]{3,2,1,0:T(8,128)S(1)} %select_select_fusion.1, f32[2,3,8,1056]{3,2,1,0:T(8,128)S(1)} %select_select_fusion.2), kind=kLoop, calls=%fused_computation.10 | loop fusion | flops 1622016 | bytes 7501824 | tf_op jit(solution)/shard_map/mul | solution.py:56
  55.4 31.7 %all-gather.3.cloned.1.call-done = f32[22,128,512]{2,1,0:T(8,128)} async-done(((f32[22,16,512]{2,1,0:T(8,128)}), f32[22,128,512]{2,1,0:T(8,128)}) %all-gather.3.cloned.1.call-update) | async-done | bytes 5767184 | tf_op jit(solution)/shard_map/all_gather | solution.py:95
  87.2 3.4 %constant_dynamic-slice_fusion.1 = (f32[22,48,512]{2,1,0:T(8,128)S(1)}, f32[22,48,512]{2,1,0:T(8,128)S(1)}) fusion(f32[22,128,512]{2,1,0:T(8,128)} %all-gather.3.cloned.1.call-done, s32[]{:T(128)S(6)} %select_n.668, s32[]{:T(128)S(6)} %select_n.669), kind=kLoop, calls=%fused_computation.144 | loop fusion | bytes 8650760 | tf_op jit(solution)/shard_map/dynamic_slice | solution.py:106
  90.6 1.0 copy-done.2
  91.6 6.7 %fusion.8 = bf16[2,768,512]{2,1,0:T(8,128)(2,1)S(1)} fusion(f32[2,768,1056]{2,1,0:T(8,128)S(1)} %bitcast.105, f32[1,1056,512]{2,1,0:T(8,128)S(1)} %bitcast.108, f32[1,1056,512]{2,1,0:T(8,128)S(1)} %bitcast.107), kind=kOutput, calls=%fused_computation.35 | convolution fusion | flops 4984700928 | bytes 12386304 | tf_op jit(solution)/shard_map/tmk,tkz->tmz/dot_general | solution.py:115
  98.3 1.2 fusion.12
  99.5 1.2 fusion.23
  100.8 0.6 fusion.107
  101.4 0.6 copy-done.7
  101.9 0.6 convolution_add_fusion
  102.5 3.0 %fusion.16 = f32[2,256,512]{2,1,0:T(8,128)S(1)} fusion(f32[2,3,256,512]{3,2,1,0:T(8,128)S(1)} %bitcast.106, f32[2,3,512,128]{3,2,1,0:T(8,128)S(1)} %get-tuple-element.10, f32[2,3,512,128]{3,2,1,0:T(8,128)S(1)} %copy-done.4, f32[2,3,512,128]{3,2,1,0:T(8,128)S(1)} %copy-done.5, f32[2,3,512,128]{3,2,1,0:T(8,128)S(1)} %get-tuple-element.9, f32[2]{0:T(128)S(1)} %gather_fusion), kind=kOutput, calls=%fused_computation.40 | convolution fusion | flops 2420899840 | bytes 10485768 | tf_op jit(solution)/shard_map/tqmz,tqnz->tmn/dot_general | solution.py:126
  105.6 0.2 broadcast_in_dim.790
  105.9 0.7 dynamic_update_slice.6
  106.6 0.1 dynamic-slice_add_fusion
  106.7 0.6 dynamic_update_slice.7
  107.4 1.4 copy-done.3
  108.9 9.4 %all-gather = f32[8,2,2]{2,1,0:T(2,128)S(1)} all-gather(f32[1,2,2]{2,1,0:T(2,128)S(1)} %bitcast.195), channel_id=1, replica_groups=mesh['region'=4,'tile'=8] {'tile'}, dimensions={0}, use_global_device_ids=true | all-gather | bytes 144 | tf_op jit(solution)/shard_map/all_gather | solution.py:90
  118.6 24.9 %reduce-scatter.2.cloned.1.call-done = f32[8,16,512]{2,1,0:T(8,128)} async-done(((f32[8,128,512]{2,1,0:T(8,128)}), f32[8,16,512]{2,1,0:T(8,128)}) %reduce-scatter.2.cloned.1.call-update) | async-done | bytes 262160 | tf_op jit(solution)/shard_map/reduce_scatter | solution.py:133
  143.6 1.8 %multiply_divide_fusion = f32[8,16,512]{2,1,0:T(8,128)} fusion(f32[8,16,512]{2,1,0:T(8,128)S(1)} %copy-done.6, f32[8,16,512]{2,1,0:T(8,128)} %reduce-scatter.2.cloned.1.call-done, f32[16]{0:T(128)S(1)} %broadcast_add_fusion.2), kind=kLoop, calls=%fused_computation.49 | loop fusion | flops 196608 | bytes 786496 | tf_op jit(solution)/shard_map/div | solution.py:139
  (96 shorter events, 4.9 us)
Async XLA Ops:
  6.5 26.3 %copy-start = (f32[6,3,3,15]{3,2,1,0:T(4,128)S(1)}, f32[6,3,3,15]{3,2,1,0:T(4,128)}, u32[]{:S(2)}) copy-start(f32[6,3,3,15]{3,2,1,0:T(4,128)} %param.10) | copy-start | bytes 9724
  6.5 19.8 %copy-start.11 = (s32[2]{0:T(128)S(1)}, s32[2]{0:T(128)}, u32[]{:S(2)}) copy-start(s32[2]{0:T(128)} %param.8) | copy-start | bytes 28
  6.5 19.8 %copy-start.12 = (s32[2]{0:T(128)S(1)}, s32[2]{0:T(128)}, u32[]{:S(2)}) copy-start(s32[2]{0:T(128)} %param.9) | copy-start | bytes 28
  6.5 80.6 %all-gather.3.cloned.1.call-start = ((), (), s32[]{:S(2)}) async-start(), calls=%async_computation.1 | async-start | bytes 6488064 | tf_op jit(solution)/shard_map/all_gather | solution.py:95
  7.7 30.5 %copy-start.9 = (f32[8,2,32,512]{3,2,1,0:T(8,128)S(1)}, f32[8,2,32,512]{3,2,1,0:T(8,128)}, u32[]{:S(2)}) copy-start(f32[8,2,32,512]{3,2,1,0:T(8,128)} %param.7) | copy-start | bytes 3145732
  7.7 9.8 %collective-permute-start = (f32[7,16,512]{2,1,0:T(8,128)S(1)}, f32[7,16,512]{2,1,0:T(8,128)S(1)}, u32[]{:S(2)}, u32[]{:S(2)}) collective-permute-start(f32[7,16,512]{2,1,0:T(8,128)S(1)} %get-tuple-element.15), channel_id=1, source_target_pairs={{0,8},{8,16},{16,24},{1,9},{9,17},{17,25},{2,10},{10,18},{18,26},{... | collective-permute-start | bytes 688136 | tf_op jit(solution)/shard_map/ppermute | solution.py:18
  12.7 11.7 %collective-permute-start.1 = (f32[7,16,512]{2,1,0:T(8,128)S(1)}, f32[7,16,512]{2,1,0:T(8,128)S(1)}, u32[]{:S(2)}, u32[]{:S(2)}) collective-permute-start(f32[7,16,512]{2,1,0:T(8,128)S(1)} %get-tuple-element.16), channel_id=1, source_target_pairs={{8,0},{16,8},{24,16},{9,1},{17,9},{25,17},{10,2},{18,10},{26,18},{... | collective-permute-start | bytes 688136 | tf_op jit(solution)/shard_map/ppermute | solution.py:20
  26.3 13.0 %copy-start.1 = (f32[6]{0:T(128)S(1)}, f32[6]{0:T(128)}, u32[]{:S(2)}) copy-start(f32[6]{0:T(128)} %param.11) | copy-start | bytes 76
  26.3 117.2 %reduce-scatter.2.cloned.1.call-start = ((), (), s32[]{:S(2)}) async-start(), calls=%async_computation.2 | async-start | bytes 2359296 | tf_op jit(solution)/shard_map/reduce_scatter | solution.py:133
  87.2 4.4 %copy-start.2 = (f32[2,3,8,32,1056]{4,3,2,1,0:T(8,128)S(1)}, f32[2,3,8,32,1056]{4,3,2,1,0:T(8,128)}, u32[]{:S(2)}) copy-start(f32[2,3,8,32,1056]{4,3,2,1,0:T(8,128)} %broadcast_multiply_fusion) | copy-start | bytes 19464196
  91.6 6.7 %copy-start.4 = (f32[2,3,512,128]{3,2,1,0:T(8,128)S(1)}, f32[2,3,512,128]{3,2,1,0:T(8,128)}, u32[]{:S(2)}) copy-start(f32[2,3,512,128]{3,2,1,0:T(8,128)} %get-tuple-element.11) | copy-start | bytes 4718596
  91.6 6.7 %copy-start.5 = (f32[2,3,512,128]{3,2,1,0:T(8,128)S(1)}, f32[2,3,512,128]{3,2,1,0:T(8,128)}, u32[]{:S(2)}) copy-start(f32[2,3,512,128]{3,2,1,0:T(8,128)} %get-tuple-element.12) | copy-start | bytes 4718596
  98.3 1.2 copy-start.10
  99.5 1.3 copy-start.8
  100.8 1.1 copy-start.7
  106.7 36.8 %copy-start.6 = (f32[8,16,512]{2,1,0:T(8,128)S(1)}, f32[8,16,512]{2,1,0:T(8,128)}, u32[]{:S(2)}) copy-start(f32[8,16,512]{2,1,0:T(8,128)} %param.6) | copy-start | bytes 786436
  107.4 1.4 copy-start.3
Sparse Core Ops, SparseCore 0:
  26.4 60.6 all-gather.2
  108.9 34.6 reduce-scatter.1

commit v8 on v7

--- a/solution.py
+++ b/solution.py
@@ -30,7 +30,7 @@
 
 
 def dot_rounded_data(spec, data, taps, data_first):
-    data_high = data.astype(jnp.bfloat16)
+    data_high = lax.reduce_precision(data, exponent_bits=8, mantissa_bits=7).astype(jnp.bfloat16)
     taps_high, taps_low = split_bf16(taps)
     if data_first:
         terms = [(data_high, taps_high), (data_high, taps_low)]
@@ -112,7 +112,7 @@
     tz = depth_band(az, depth, 128)
 
     cells = block_x * tile_rows
-    part = jnp.einsum("tmk,tkz->tmz", kxy, windows, precision=MATMUL_PRECISION)
+    part = dot_rounded_data("tmk,tkz->tmz", windows, kxy, False)
     part = part.reshape(tile_count, rank_terms, cells, depth)
     blurred = dot_rounded_data("tqmz,tqzn->tmn", part, tz, True)
 

time: 153 us -> 152 us (level)
  waiting for transfers between devices: 67.1 us -> 59.2 us
  local copies, waits for them, and re-layouts: 20 us -> 26.9 us
    mul x0 -> x1, local copies, waits for them, and re-layouts: none -> 7.94 us  [kron_band(): return ea[..., :, None, :] * eb[..., None, :, :]]
    dot_general x4 -> x6, matrix products: 3.56 us -> 11.5 us  [dot_rounded_data(): jnp.einsum(spec, a, b, preferred_element_type=jnp.float32)]
    all_gather x1, waiting for transfers between devices: 31.7 us -> 23.9 us  [on_device(): gathered = lax.all_gather(rimmed, 'tile', axis=1, tiled=True)]
    dot_general x1 -> x0, matrix products: 6.69 us -> none  [on_device(): part = jnp.einsum('tmk,tkz->tmz', kxy, windows, precision=MATMUL_PRECISION)]
    unnamed x28 -> x30, local copies, waits for them, and re-layouts: 3.18 us -> 2.11 us
  transfers between devices with their start and end apart: 4 -> 4, of which waited for: 4 -> 4; matrix products, arithmetic and copies ran while one was open for 14% -> 19% of each run, Pallas kernels for 0% -> 0%
where the time goes in v8:
time: 152 us
  waiting for transfers between devices  59.2 us (39%)
  local copies, waits for them, and re-layouts  26.9 us (18%)
  between operations  21.5 us (14%)
  other arithmetic  14.6 us (10%)
  matrix products  14.5 us (10%)
  blocking collectives  9.18 us (6%)
  starting transfers between devices  6.19 us (4%)
    reduce_scatter x1, waiting for transfers between devices, on_device(): lax.psum_scatter(numerator, 'tile', scatter_dimension=1, tiled=True)  24.9 us
    all_gather x1, waiting for transfers between devices, on_device(): gathered = lax.all_gather(rimmed, 'tile', axis=1, tiled=True)  23.9 us
    dot_general x6, matrix products, dot_rounded_data(): jnp.einsum(spec, a, b, preferred_element_type=jnp.float32)  11.5 us
    all_gather x1, blocking collectives, on_device(): all_info = lax.all_gather(tile_info, 'tile', tiled=True)  9.18 us
    mul x1, local copies, waits for them, and re-layouts, kron_band(): return ea[..., :, None, :] * eb[..., None, :, :]  7.94 us
    ppermute x1, waiting for transfers between devices, with_halo(): lax.ppermute(head, axis, [((i + 1) % count, i) for i in range(ends)])  6.86 us
    ppermute x1, starting transfers between devices, with_halo(): lax.ppermute(tail, axis, [(i, (i + 1) % count) for i in range(ends)])  4.86 us
    mul x2, other arithmetic, kron_band(): return ea[..., :, None, :] * eb[..., None, :, :]  3.92 us
  transfers between devices with their start and end apart: 4, of which 4 were waited for; matrix products, arithmetic and copies ran while one was open for 19% of the time, Pallas kernels for 0%

profile of v8, /device:TPU:0, one launch (start us, length us, event | category | flops | bytes accessed | tf_op | source)
XLA Modules:
  0.0 152.0 jit_solution(15913894943357329853)
XLA Ops:
  6.5 1.1 fusion.103
  7.7 4.9 %collective-permute-start = (f32[7,16,512]{2,1,0:T(8,128)S(1)}, f32[7,16,512]{2,1,0:T(8,128)S(1)}, u32[]{:S(2)}, u32[]{:S(2)}) collective-permute-start(f32[7,16,512]{2,1,0:T(8,128)S(1)} %get-tuple-element.15), channel_id=1, source_target_pairs={{0,8},{8,16},{16,24},{1,9},{9,17},{17,25},{2,10},{10,18},{18,26},{... | collective-permute-start | bytes 688136 | tf_op jit(solution)/shard_map/ppermute | solution.py:18
  12.5 1.3 collective-permute-start.1
  13.8 3.5 %collective-permute-done = f32[7,16,512]{2,1,0:T(8,128)S(1)} collective-permute-done((f32[7,16,512]{2,1,0:T(8,128)S(1)}, f32[7,16,512]{2,1,0:T(8,128)S(1)}, u32[]{:S(2)}, u32[]{:S(2)}) %collective-permute-start) | collective-permute-done | bytes 229408 | tf_op jit(solution)/shard_map/ppermute | solution.py:18
  17.4 6.9 %collective-permute-done.1 = f32[7,16,512]{2,1,0:T(8,128)S(1)} collective-permute-done((f32[7,16,512]{2,1,0:T(8,128)S(1)}, f32[7,16,512]{2,1,0:T(8,128)S(1)}, u32[]{:S(2)}, u32[]{:S(2)}) %collective-permute-start.1) | collective-permute-done | bytes 229408 | tf_op jit(solution)/shard_map/ppermute | solution.py:20
  24.2 1.9 %pad_maximum_fusion.4 = f32[22,16,512]{2,1,0:T(8,128)} fusion(f32[7,16,512]{2,1,0:T(8,128)S(1)} %collective-permute-done.1, f32[8,16,512]{2,1,0:T(8,128)} %param.6, f32[7,16,512]{2,1,0:T(8,128)S(1)} %collective-permute-done), kind=kLoop, calls=%fused_computation.51 | loop fusion | flops 360448 | bytes 1441792 | tf_op jit(solution)/shard_map/concatenate | solution.py:16
  26.2 0.6 fusion.110
  29.4 0.6 fusion.109
  32.5 0.6 gather_fusion.1
  33.1 0.1 fusion.108
  33.2 0.1 copy.234
  33.3 0.1 copy.235
  34.7 0.1 fusion.107
  34.8 0.1 copy.218
  36.5 0.4 select_select_fusion.2
  36.9 0.7 subtract_compare_fusion.14
  37.5 1.4 select_select_fusion.1
  39.0 3.7 %broadcast_multiply_fusion = f32[2,3,8,32,1056]{4,3,2,1,0:T(8,128)} fusion(f32[2,3,32,1056]{3,2,1,0:T(8,128)S(1)} %select_select_fusion.1, f32[2,3,8,1056]{3,2,1,0:T(8,128)S(1)} %select_select_fusion.2), kind=kLoop, calls=%fused_computation.11 | loop fusion | flops 1622016 | bytes 7501824 | tf_op jit(solution)/shard_map/mul | solution.py:56
  42.7 7.9 %copy.250 = f32[2,768,1056]{1,2,0:T(8,128)} copy(f32[2,768,1056]{2,1,0:T(8,128)} %bitcast.106) | data formatting | bytes 12976128 | tf_op jit(solution)/shard_map/mul | solution.py:56
  50.6 0.1 fusion.106
  50.7 0.1 copy.253
  52.2 1.1 copy.249
  53.3 0.6 gather_fusion
  56.6 0.2 select_select_fusion.4
  56.9 0.4 select_select_fusion.3
  57.2 0.6 fusion.41
  57.8 0.2 broadcast_multiply_fusion.1
  58.0 1.5 select_select_fusion
  59.5 2.2 %pad_slice_fusion.3 = (f32[2,3,512,128]{3,2,1,0:T(8,128)S(1)}, f32[2,3,512,128]{3,2,1,0:T(8,128)S(1)}, f32[2,3,512,128]{3,2,1,0:T(8,128)}, f32[2,3,512,128]{3,2,1,0:T(8,128)}) fusion(f32[2,3,384,128]{3,2,1,0:T(8,128)S(1)} %select_select_fusion), kind=kLoop, calls=%fused_computation.20 | loop fusion | bytes 7471104 | tf_op jit(solution)/shard_map/slice | solution.py:73
  61.7 1.4 fusion.9
  63.1 23.9 %all-gather.3.cloned.1.call-done = f32[22,128,512]{2,1,0:T(8,128)} async-done(((f32[22,16,512]{2,1,0:T(8,128)}), f32[22,128,512]{2,1,0:T(8,128)}) %all-gather.3.cloned.1.call-update) | async-done | bytes 5767184 | tf_op jit(solution)/shard_map/all_gather | solution.py:95
  87.0 3.3 %constant_dynamic-slice_fusion.1 = (f32[22,48,512]{2,1,0:T(8,128)S(1)}, f32[22,48,512]{2,1,0:T(8,128)S(1)}) fusion(f32[22,128,512]{2,1,0:T(8,128)} %all-gather.3.cloned.1.call-done, s32[]{:T(128)S(6)} %select_n.668, s32[]{:T(128)S(6)} %select_n.669), kind=kLoop, calls=%fused_computation.148 | loop fusion | bytes 8650760 | tf_op jit(solution)/shard_map/dynamic_slice | solution.py:106
  90.3 5.2 %fusion.3 = f32[2,768,512]{2,1,0:T(8,128)S(1)} fusion(f32[2,768,1056]{1,2,0:T(8,128)} %copy.250, f32[1,1056,512]{2,1,0:T(8,128)S(1)} %bitcast.112, f32[1,1056,512]{2,1,0:T(8,128)S(1)} %bitcast.110), kind=kOutput, calls=%fused_computation.12 | convolution fusion | flops 1669054464 | bytes 13959168 | tf_op jit(solution)/shard_map/tmk,tkz->tmz/dot_general | solution.py:39
  95.6 2.2 %reduce-precision_convert_fusion.4 = bf16[2,768,512]{2,1,0:T(8,128)(2,1)S(1)} fusion(f32[2,768,512]{2,1,0:T(8,128)S(1)} %fusion.3, f32[2,768,1056]{1,2,0:T(8,128)S(1)} %bitcast.109, f32[1,1056,512]{2,1,0:T(8,128)S(1)} %bitcast.113, f32[1,1056,512]{2,1,0:T(8,128)S(1)} %bitcast.111), kind=kOutput, calls=%fused_computation.16 | convolution fusion | flops 1669791744 | bytes 15532032 | tf_op jit(solution)/shard_map/tmk,tkz->tmz/dot_general | solution.py:39
  97.9 1.3 fusion.10
  99.2 1.5 %fusion.24 = bf16[2,256,512]{2,1,0:T(8,128)(2,1)S(1)} fusion(f32[2,256,512]{2,1,0:T(8,128)S(1)} %bitcast.119, f32[2,256,512]{2,1,0:T(8,128)S(1)} %fusion.10, bf16[2,3,256,512]{3,2,1,0:T(8,128)(2,1)S(1)} %bitcast.117, f32[2,3,512,128]{3,2,1,0:T(8,128)S(1)} %get-tuple-element.10, f32[2,3,512,128]{3,2,1,0:T(8,128)S(1)} %copy-done.3, ...), kind=kOutput, calls=%fused_computation.47 | convolution fusion | flops 815792128 | bytes 10485760 | tf_op jit(solution)/shard_map/tqmz,tqzn->tmn/dot_general | solution.py:39
  100.8 0.6 fusion.111
  101.3 0.6 copy-done.6
  101.9 0.6 convolution_add_fusion
  102.5 3.0 %fusion.14 = f32[2,256,512]{2,1,0:T(8,128)S(1)} fusion(f32[2,3,256,512]{3,2,1,0:T(8,128)S(1)} %bitcast.107, f32[2,3,512,128]{3,2,1,0:T(8,128)S(1)} %get-tuple-element.10, f32[2,3,512,128]{3,2,1,0:T(8,128)S(1)} %copy-done.3, f32[2,3,512,128]{3,2,1,0:T(8,128)S(1)} %copy-done.4, f32[2,3,512,128]{3,2,1,0:T(8,128)S(1)} %get-tuple-element.9, f32[2]{0:T(128)S(1)} %gather_fusion), kind=kOutput, calls=%fused_computation.43 | convolution fusion | flops 2420899840 | bytes 10485768 | tf_op jit(solution)/shard_map/tqmz,tqnz->tmn/dot_general | solution.py:126
  105.6 0.2 broadcast_in_dim.790
  105.8 0.7 dynamic_update_slice.6
  106.6 0.1 dynamic-slice_add_fusion
  106.7 0.7 dynamic_update_slice.7
  107.5 1.3 copy-done.2
  109.0 9.2 %all-gather = f32[8,2,2]{2,1,0:T(2,128)S(1)} all-gather(f32[1,2,2]{2,1,0:T(2,128)S(1)} %bitcast.200), channel_id=1, replica_groups=mesh['region'=4,'tile'=8] {'tile'}, dimensions={0}, use_global_device_ids=true | all-gather | bytes 144 | tf_op jit(solution)/shard_map/all_gather | solution.py:90
  118.5 24.9 %reduce-scatter.2.cloned.1.call-done = f32[8,16,512]{2,1,0:T(8,128)} async-done(((f32[8,128,512]{2,1,0:T(8,128)}), f32[8,16,512]{2,1,0:T(8,128)}) %reduce-scatter.2.cloned.1.call-update) | async-done | bytes 262160 | tf_op jit(solution)/shard_map/reduce_scatter | solution.py:133
  143.4 1.8 %multiply_divide_fusion = f32[8,16,512]{2,1,0:T(8,128)} fusion(f32[8,16,512]{2,1,0:T(8,128)S(1)} %copy-done.5, f32[8,16,512]{2,1,0:T(8,128)} %reduce-scatter.2.cloned.1.call-done, f32[16]{0:T(128)S(1)} %broadcast_add_fusion.2), kind=kLoop, calls=%fused_computation.53 | loop fusion | flops 196608 | bytes 786496 | tf_op jit(solution)/shard_map/div | solution.py:139
  (101 shorter events, 5.0 us)
Async XLA Ops:
  6.5 26.0 %copy-start = (f32[6,3,3,15]{3,2,1,0:T(4,128)S(1)}, f32[6,3,3,15]{3,2,1,0:T(4,128)}, u32[]{:S(2)}) copy-start(f32[6,3,3,15]{3,2,1,0:T(4,128)} %param.10) | copy-start | bytes 9724
  6.5 19.7 %copy-start.10 = (s32[2]{0:T(128)S(1)}, s32[2]{0:T(128)}, u32[]{:S(2)}) copy-start(s32[2]{0:T(128)} %param.8) | copy-start | bytes 28
  6.5 19.7 %copy-start.11 = (s32[2]{0:T(128)S(1)}, s32[2]{0:T(128)}, u32[]{:S(2)}) copy-start(s32[2]{0:T(128)} %param.9) | copy-start | bytes 28
  6.5 80.5 %all-gather.3.cloned.1.call-start = ((), (), s32[]{:S(2)}) async-start(), calls=%async_computation.1 | async-start | bytes 6488064 | tf_op jit(solution)/shard_map/all_gather | solution.py:95
  7.7 9.7 %collective-permute-start = (f32[7,16,512]{2,1,0:T(8,128)S(1)}, f32[7,16,512]{2,1,0:T(8,128)S(1)}, u32[]{:S(2)}, u32[]{:S(2)}) collective-permute-start(f32[7,16,512]{2,1,0:T(8,128)S(1)} %get-tuple-element.15), channel_id=1, source_target_pairs={{0,8},{8,16},{16,24},{1,9},{9,17},{17,25},{2,10},{10,18},{18,26},{... | collective-permute-start | bytes 688136 | tf_op jit(solution)/shard_map/ppermute | solution.py:18
  12.5 11.7 %collective-permute-start.1 = (f32[7,16,512]{2,1,0:T(8,128)S(1)}, f32[7,16,512]{2,1,0:T(8,128)S(1)}, u32[]{:S(2)}, u32[]{:S(2)}) collective-permute-start(f32[7,16,512]{2,1,0:T(8,128)S(1)} %get-tuple-element.16), channel_id=1, source_target_pairs={{8,0},{16,8},{24,16},{9,1},{17,9},{25,17},{10,2},{18,10},{26,18},{... | collective-permute-start | bytes 688136 | tf_op jit(solution)/shard_map/ppermute | solution.py:20
  26.2 117.2 %reduce-scatter.2.cloned.1.call-start = ((), (), s32[]{:S(2)}) async-start(), calls=%async_computation.2 | async-start | bytes 2359296 | tf_op jit(solution)/shard_map/reduce_scatter | solution.py:133
  42.7 9.5 %copy-start.8 = (f32[8,2,32,512]{3,2,1,0:T(8,128)S(1)}, f32[8,2,32,512]{3,2,1,0:T(8,128)}, u32[]{:S(2)}) copy-start(f32[8,2,32,512]{3,2,1,0:T(8,128)} %param.7) | copy-start | bytes 3145732
  50.6 2.7 %copy-start.1 = (f32[6]{0:T(128)S(1)}, f32[6]{0:T(128)}, u32[]{:S(2)}) copy-start(f32[6]{0:T(128)} %param.11) | copy-start | bytes 76
  87.0 8.5 %slice-start = ((s8[6488064]{0:T(1024)(128)(4,1)}), s8[4194304]{0:T(1024)(128)(4,1)S(1)}, s32[]{:S(2)}) async-start(s8[6488064]{0:T(1024)(128)(4,1)} %bitcast.108), calls=%async_computation.3 | async-start | bytes 8388608
  90.3 5.3 %slice-start.1 = ((s8[6488064]{0:T(1024)(128)(4,1)}), s8[2293760]{0:T(1024)(128)(4,1)S(1)}, s32[]{:S(2)}) async-start(s8[6488064]{0:T(1024)(128)(4,1)} %bitcast.108), calls=%async_computation.4 | async-start | bytes 4587520
  95.6 2.3 %copy-start.3 = (f32[2,3,512,128]{3,2,1,0:T(8,128)S(1)}, f32[2,3,512,128]{3,2,1,0:T(8,128)}, u32[]{:S(2)}) copy-start(f32[2,3,512,128]{3,2,1,0:T(8,128)} %get-tuple-element.11) | copy-start | bytes 4718596
  95.6 2.3 %copy-start.4 = (f32[2,3,512,128]{3,2,1,0:T(8,128)S(1)}, f32[2,3,512,128]{3,2,1,0:T(8,128)}, u32[]{:S(2)}) copy-start(f32[2,3,512,128]{3,2,1,0:T(8,128)} %get-tuple-element.12) | copy-start | bytes 4718596
  97.8 1.3 copy-start.9
  99.2 1.6 %copy-start.7 = (bf16[2,768,256]{2,1,0:T(8,128)(2,1)S(1)}, bf16[2,768,256]{2,1,0:T(8,128)(2,1)}, u32[]{:S(2)}) copy-start(bf16[2,768,256]{2,1,0:T(8,128)(2,1)} %get-tuple-element.8) | copy-start | bytes 2359300
  100.8 1.1 copy-start.6
  106.6 36.8 %copy-start.5 = (f32[8,16,512]{2,1,0:T(8,128)S(1)}, f32[8,16,512]{2,1,0:T(8,128)}, u32[]{:S(2)}) copy-start(f32[8,16,512]{2,1,0:T(8,128)} %param.6) | copy-start | bytes 786436
  107.5 1.4 copy-start.2
Sparse Core Ops, SparseCore 0:
  26.3 60.6 all-gather.2
  109.0 34.3 reduce-scatter.1

commit v9 on v7

--- a/solution.py
+++ b/solution.py
@@ -1,7 +1,11 @@
+import functools
+
 import jax
 import jax.numpy as jnp
 from jax import lax
 from jax.sharding import PartitionSpec as P
+from jax.experimental import pallas as pl
+from jax.experimental.pallas import tpu as pltpu
 
 PRIOR_WEIGHT = 0.25
 MATMUL_PRECISION = lax.Precision.HIGH
@@ -74,6 +78,39 @@
     return jnp.concatenate(cols, axis=-1)
 
 
+def tile_kernel(win_rows, rank_terms, starts_ref, gathered_ref, kxy_hi, kxy_lo, tz_hi, tz_lo, fxy_hi, fxy_lo,
+                fz_hi, fz_lo, obs_ref, out_ref, window, sem):
+    j = pl.program_id(0)
+    start = pl.multiple_of(starts_ref[j], 8)
+    copy = pltpu.make_async_copy(gathered_ref.at[:, pl.ds(start, win_rows), :], window, sem)
+    copy.start()
+    copy.wait()
+    win_x, _, depth = window.shape
+    data = window[...].reshape(win_x * win_rows, depth).astype(jnp.bfloat16)
+    f32 = jnp.float32
+    part = jnp.dot(kxy_hi[0], data, preferred_element_type=f32) + jnp.dot(kxy_lo[0], data, preferred_element_type=f32)
+    cells = part.shape[0] // rank_terms
+    blurred = None
+    for q in range(rank_terms):
+        p = part[q * cells : (q + 1) * cells].astype(jnp.bfloat16)
+        term = jnp.dot(p, tz_hi[0, q], preferred_element_type=f32) + jnp.dot(p, tz_lo[0, q], preferred_element_type=f32)
+        blurred = term if blurred is None else blurred + term
+    quotient = (obs_ref[0] / blurred).astype(jnp.bfloat16)
+    part = jnp.dot(fxy_hi[0], quotient, preferred_element_type=f32) + jnp.dot(fxy_lo[0], quotient, preferred_element_type=f32)
+    correction = None
+    for q in range(rank_terms):
+        c = part[q * cells : (q + 1) * cells]
+        c_hi = c.astype(jnp.bfloat16)
+        c_lo = (c - c_hi.astype(f32)).astype(jnp.bfloat16)
+        term = (
+            jnp.dot(c_hi, fz_hi[0, q], preferred_element_type=f32)
+            + jnp.dot(c_lo, fz_hi[0, q], preferred_element_type=f32)
+            + jnp.dot(c_hi, fz_lo[0, q], preferred_element_type=f32)
+        )
+        correction = term if correction is None else correction + term
+    out_ref[0] = correction
+
+
 def on_device(estimate, observed, tile_offset, tile_view, psf_taps, view_weight):
     kt = psf_taps.shape[3]
     rim = (kt - 1) // 2
@@ -83,7 +120,7 @@
     rank_terms = psf_taps.shape[1]
     group_size = lax.axis_size("tile")
     region_rows = block_y * group_size
-    win_rows = -(-(tile_rows + 2 * rim) // 8) * 8
+    win_rows = -(-(tile_rows + 2 * rim + 7) // 8) * 8
     win_x = block_x + 2 * rim
 
     tile_info = jnp.stack([tile_offset.astype(jnp.float32), view_weight[tile_view]], axis=1)
@@ -100,30 +137,46 @@
     ay = filters[:, :, 1]
     az = filters[:, :, 2]
 
-    starts = jnp.clip(tile_offset - rim, 0, region_rows - win_rows)
+    starts = jnp.clip(((tile_offset - rim) // 8) * 8, 0, region_rows - win_rows)
     shifts = tile_offset - rim - starts
-    windows = jnp.stack(
-        [lax.dynamic_slice_in_dim(gathered, starts[j], win_rows, 1) for j in range(tile_count)]
-    ).reshape(tile_count, win_x * win_rows, depth)
-
     kxy = kron_band(ax, ay, block_x, tile_rows, win_rows, win_x * win_rows, 0, shifts[:, None]).reshape(
         tile_count, rank_terms * block_x * tile_rows, win_x * win_rows
     )
     tz = depth_band(az, depth, 128)
 
     cells = block_x * tile_rows
-    part = jnp.einsum("tmk,tkz->tmz", kxy, windows, precision=MATMUL_PRECISION)
-    part = part.reshape(tile_count, rank_terms, cells, depth)
-    blurred = dot_rounded_data("tqmz,tqzn->tmn", part, tz, True)
-
-    quotient = observed.transpose(1, 0, 2, 3).reshape(tile_count, cells, depth) / blurred
-
     fxy = kron_band(ax[..., ::-1], ay[..., ::-1], block_x, tile_rows, tile_rows, cells, -rim, -rim).reshape(
         tile_count, rank_terms * cells, cells
     )
-    part = dot_rounded_data("tmk,tkz->tmz", quotient, fxy, False)
-    part = part.reshape(tile_count, rank_terms, cells, depth)
-    correction = jnp.einsum("tqmz,tqnz->tmn", part, tz, precision=MATMUL_PRECISION)
+    obs = observed.transpose(1, 0, 2, 3).reshape(tile_count, cells, depth)
+    kxy_hi, kxy_lo = split_bf16(kxy)
+    tz_hi, tz_lo = split_bf16(tz)
+    fz_hi, fz_lo = split_bf16(jnp.swapaxes(tz, -1, -2))
+    fxy_hi, fxy_lo = split_bf16(fxy)
+    per_tile = lambda *shape: pl.BlockSpec((1,) + shape, lambda j, s: (j,) + (0,) * len(shape))
+    correction = pl.pallas_call(
+        functools.partial(tile_kernel, win_rows, rank_terms),
+        grid_spec=pltpu.PrefetchScalarGridSpec(
+            num_scalar_prefetch=1,
+            grid=(tile_count,),
+            in_specs=[
+                pl.BlockSpec(memory_space=pl.ANY),
+                per_tile(rank_terms * cells, win_x * win_rows),
+                per_tile(rank_terms * cells, win_x * win_rows),
+                per_tile(rank_terms, depth, depth),
+                per_tile(rank_terms, depth, depth),
+                per_tile(rank_terms * cells, cells),
+                per_tile(rank_terms * cells, cells),
+                per_tile(rank_terms, depth, depth),
+                per_tile(rank_terms, depth, depth),
+                per_tile(cells, depth),
+            ],
+            out_specs=per_tile(cells, depth),
+            scratch_shapes=[pltpu.VMEM((win_x, win_rows, depth), jnp.float32), pltpu.SemaphoreType.DMA(())],
+        ),
+        out_shape=jax.ShapeDtypeStruct((tile_count, cells, depth), jnp.float32),
+        compiler_params=pltpu.CompilerParams(vmem_limit_bytes=60 * 1024 * 1024),
+    )(starts, gathered, kxy_hi, kxy_lo, tz_hi, tz_lo, fxy_hi, fxy_lo, fz_hi, fz_lo, obs)
     weighted = (weight[:, None, None] * correction).reshape(tile_count, block_x, tile_rows, depth)
 
     numerator = jnp.zeros((block_x, region_rows, depth), jnp.float32)

time: 153 us -> 157 us (1.026)
  Pallas kernels: 0 us -> 21.5 us
  waiting for transfers between devices: 67.1 us -> 51.2 us
  matrix products: 13.2 us -> 0 us
  other arithmetic: 14.6 us -> 26.3 us
  local copies, waits for them, and re-layouts: 20 us -> 24.4 us
  between operations: 21.6 us -> 17.6 us
    pallas_call x0 -> x1, Pallas kernels: none -> 21.5 us  [on_device(): pl.pallas_call(functools.partial(tile_kernel, win_rows, rank_terms), grid...]
    all_gather x1, waiting for transfers between devices: 31.7 us -> 16.6 us  [on_device(): gathered = lax.all_gather(rimmed, 'tile', axis=1, tiled=True)]
    dot_general x6 -> x0, matrix products: 13.2 us -> none  [the longest x1 6.69 us: on_device(): part = jnp.einsum('tmk,tkz->tmz', kxy, windows, precision=MATMUL_PRECISION)]
    convert_element_type x1 -> x4, other arithmetic: 1.38 us -> 13 us  [split_bf16(): return (high.astype(jnp.bfloat16), (values - high).astype(jnp.bfloat16))]
    convert_element_type x0 -> x2, local copies, waits for them, and re-layouts: none -> 9.36 us  [split_bf16(): return (high.astype(jnp.bfloat16), (values - high).astype(jnp.bfloat16))]
    dynamic_slice x1 -> x0, local copies, waits for them, and re-layouts: 3.37 us -> none  [on_device(): lax.dynamic_slice_in_dim(gathered, starts[j], win_rows, 1)]
    mul x2, other arithmetic: 3.93 us -> 1.11 us  [kron_band(): return ea[..., :, None, :] * eb[..., None, :, :]]
    slice x1, local copies, waits for them, and re-layouts: 2.18 us -> 0.56 us  [depth_band(): cols.append(col[..., block:block + depth, :])]
  transfers between devices with their start and end apart: 4 -> 4, of which waited for: 4 -> 4; matrix products, arithmetic and copies ran while one was open for 14% -> 26% of each run, Pallas kernels for 0% -> 0%
where the time goes in v9:
time: 157 us; the launch traced here: 156 us
  waiting for transfers between devices  51.2 us (33%)
  other arithmetic  26.3 us (17%)
  local copies, waits for them, and re-layouts  24.4 us (16%)
  Pallas kernels  21.5 us (14%)
  between operations  17.6 us (11%)
  blocking collectives  9.18 us (6%)
  starting transfers between devices  6.19 us (4%)
    reduce_scatter x1, waiting for transfers between devices, on_device(): lax.psum_scatter(numerator, 'tile', scatter_dimension=1, tiled=True)  24.9 us
    pallas_call x1, Pallas kernels, on_device(): pl.pallas_call(functools.partial(tile_kernel, win_rows, rank_terms), grid...  21.5 us
    all_gather x1, waiting for transfers between devices, on_device(): gathered = lax.all_gather(rimmed, 'tile', axis=1, tiled=True)  16.6 us
    convert_element_type x4, other arithmetic, split_bf16(): return (high.astype(jnp.bfloat16), (values - high).astype(jnp.bfloat16))  13 us
    convert_element_type x2, local copies, waits for them, and re-layouts, split_bf16(): return (high.astype(jnp.bfloat16), (values - high).astype(jnp.bfloat16))  9.36 us
    all_gather x1, blocking collectives, on_device(): all_info = lax.all_gather(tile_info, 'tile', tiled=True)  9.18 us
    ppermute x1, waiting for transfers between devices, with_halo(): lax.ppermute(head, axis, [((i + 1) % count, i) for i in range(ends)])  6.86 us
    ppermute x1, starting transfers between devices, with_halo(): lax.ppermute(tail, axis, [(i, (i + 1) % count) for i in range(ends)])  4.86 us
  transfers between devices with their start and end apart: 4, of which 4 were waited for; matrix products, arithmetic and copies ran while one was open for 26% of the time, Pallas kernels for 0%

profile of v9, /device:TPU:0, one launch (start us, length us, event | category | flops | bytes accessed | tf_op | source)
XLA Modules:
  0.0 156.4 jit_solution(17606281767694895602)
XLA Ops:
  6.5 1.1 fusion.73
  7.6 4.9 %collective-permute-start = (f32[7,16,512]{2,1,0:T(8,128)S(1)}, f32[7,16,512]{2,1,0:T(8,128)S(1)}, u32[]{:S(2)}, u32[]{:S(2)}) collective-permute-start(f32[7,16,512]{2,1,0:T(8,128)S(1)} %get-tuple-element.21), channel_id=1, source_target_pairs={{0,8},{8,16},{16,24},{1,9},{9,17},{17,25},{2,10},{10,18},{18,26},{... | collective-permute-start | bytes 688136 | tf_op jit(solution)/shard_map/ppermute | solution.py:22
  12.5 1.3 collective-permute-start.1
  13.8 0.7 compare_select_fusion
  14.5 2.9 %collective-permute-done = f32[7,16,512]{2,1,0:T(8,128)S(1)} collective-permute-done((f32[7,16,512]{2,1,0:T(8,128)S(1)}, f32[7,16,512]{2,1,0:T(8,128)S(1)}, u32[]{:S(2)}, u32[]{:S(2)}) %collective-permute-start) | collective-permute-done | bytes 229408 | tf_op jit(solution)/shard_map/ppermute | solution.py:22
  17.3 6.9 %collective-permute-done.1 = f32[7,16,512]{2,1,0:T(8,128)S(1)} collective-permute-done((f32[7,16,512]{2,1,0:T(8,128)S(1)}, f32[7,16,512]{2,1,0:T(8,128)S(1)}, u32[]{:S(2)}, u32[]{:S(2)}) %collective-permute-start.1) | collective-permute-done | bytes 229408 | tf_op jit(solution)/shard_map/ppermute | solution.py:24
  24.2 1.9 %pad_maximum_fusion.1 = f32[22,16,512]{2,1,0:T(8,128)} fusion(f32[7,16,512]{2,1,0:T(8,128)S(1)} %collective-permute-done.1, f32[8,16,512]{2,1,0:T(8,128)} %param.6, f32[7,16,512]{2,1,0:T(8,128)S(1)} %collective-permute-done), kind=kLoop, calls=%fused_computation.38 | loop fusion | flops 360448 | bytes 1441792 | tf_op jit(solution)/shard_map/concatenate | solution.py:20
  26.2 0.6 fusion.79
  29.4 0.6 gather_fusion.1
  30.0 0.1 fusion.76
  30.1 0.1 copy.199
  30.5 0.1 copy.203
  31.6 0.5 fusion.18
  32.1 1.5 select_select_fusion
  33.6 0.6 pad_slice_fusion.3
  34.2 3.7 %fusion.1 = (bf16[2,3,512,512]{2,3,1,0:T(8,128)(2,1)}, bf16[2,3,512,512]{2,3,1,0:T(8,128)(2,1)}) fusion(f32[2,3,512,128]{2,3,1,0:T(8,128)S(1)} %get-tuple-element.16, f32[2,3,512,128]{2,3,1,0:T(8,128)S(1)} %get-tuple-element.17, f32[2,3,512,128]{2,3,1,0:T(8,128)S(1)} %get-tuple-element.18, f32[2,3,512,128]{2,3,1,0:T(8,128)S(1)} %get-tuple-element.15), kind=kLoop, calls=%fused_computation.9 | loop fusion | flops 11010048 | bytes 12582912 | tf_op jit(solution)/shard_map/convert_element_type | solution.py:33
  37.8 4.7 %copy.215.tz_hi = bf16[2,3,512,512]{3,2,1,0:T(8,128)(2,1)} copy(bf16[2,3,512,512]{2,3,1,0:T(8,128)(2,1)} %get-tuple-element.12) | data formatting | bytes 6291456 | tf_op jit(solution)/shard_map/convert_element_type | solution.py:33
  42.5 4.7 %copy.216.tz_lo = bf16[2,3,512,512]{3,2,1,0:T(8,128)(2,1)} copy(bf16[2,3,512,512]{2,3,1,0:T(8,128)(2,1)} %get-tuple-element.11) | data formatting | bytes 6291456 | tf_op jit(solution)/shard_map/convert_element_type | solution.py:33
  47.2 0.1 fusion.78
  47.3 0.1 copy.183
  48.8 0.1 fusion.77
  48.9 0.1 copy.167
  50.4 2.3 %copy.214 = f32[2,8,32,512]{3,2,1,0:T(8,128)} copy(f32[2,8,32,512]{3,2,0,1:T(8,128)} %bitcast.80) | data formatting | bytes 2097152 | tf_op jit(solution)/shard_map/transpose | solution.py:151
  52.7 0.6 gather_fusion
  54.7 0.5 add_subtract_fusion
  55.3 0.2 select_select_fusion.4
  55.5 0.4 select_select_fusion.3
  55.9 0.2 broadcast_multiply_fusion.1
  56.1 1.4 fusion.3
  57.6 0.5 copy-done.3
  58.1 0.5 copy-done.5
  58.6 3.3 %fusion.2 = (bf16[2,3,512,512]{3,2,1,0:T(8,128)(2,1)}, bf16[2,3,512,512]{3,2,1,0:T(8,128)(2,1)}) fusion(f32[2,3,512,128]{2,3,1,0:T(8,128)S(1)} %get-tuple-element.16, f32[2,3,512,128]{2,3,1,0:T(8,128)S(1)} %copy-done.3, f32[2,3,512,128]{2,3,1,0:T(8,128)S(1)} %copy-done.5, f32[2,3,512,128]{2,3,1,0:T(8,128)S(1)} %get-tuple-element.15), kind=kLoop, calls=%fused_computation.10 | loop fusion | flops 11010048 | bytes 12582912 | tf_op jit(solution)/shard_map/convert_element_type | solution.py:33
  62.0 0.4 select_select_fusion.2
  62.4 0.9 subtract_compare_fusion.14
  63.3 1.6 %select_select_fusion.1 = f32[2,3,32,1232]{3,2,1,0:T(8,128)S(1)} fusion(f32[2,3]{1,0:T(2,128)S(1)} %bitcast.112, f32[2,3]{1,0:T(2,128)S(1)} %bitcast.110, f32[2,3]{1,0:T(2,128)S(1)} %bitcast.108, f32[2,3]{1,0:T(2,128)S(1)} %bitcast.106, f32[2,3]{1,0:T(2,128)S(1)} %bitcast.104, f32[2,3]{1,0:T(2,128)S(1)} %bitcast.102, f32[2,3]{1,0:T(2,128)S(1)} %bitcast.100, ...), kind=kLoop, calls=%fused_computation.36 | loop fusion | flops 3548160 | bytes 2129256 | tf_op jit(solution)/shard_map/jit(_where)/select_n | solution.py:59
  65.0 0.9 broadcast_multiply_fusion
  65.9 4.5 %fusion = (bf16[2,768,1232]{2,1,0:T(8,128)(2,1)}, bf16[2,768,1232]{2,1,0:T(8,128)(2,1)}) fusion(f32[2,3,8,32,1232]{4,3,2,1,0:T(8,128)S(1)} %broadcast_multiply_fusion), kind=kLoop, calls=%fused_computation.8 | loop fusion | flops 7569408 | bytes 15138816 | tf_op jit(solution)/shard_map/convert_element_type | solution.py:33
  70.4 16.6 %all-gather.3.cloned.1.call-done.gathered_ref = f32[22,128,512]{2,1,0:T(8,128)} async-done(((f32[22,16,512]{2,1,0:T(8,128)}), f32[22,128,512]{2,1,0:T(8,128)}) %all-gather.3.cloned.1.call-update) | async-done | bytes 5767184 | tf_op jit(solution)/shard_map/all_gather | solution.py:132
  87.0 21.5 %shard_map.64 = f32[2,256,512]{2,1,0:T(8,128)} custom-call(s32[2]{0:T(128)} %get-tuple-element.6.starts_ref, f32[22,128,512]{2,1,0:T(8,128)} %all-gather.3.cloned.1.call-done.gathered_ref, bf16[2,768,1232]{2,1,0:T(8,128)(2,1)} %get-tuple-element.8.kxy_hi, bf16[2,768,1232]{2,1,0:T(8,128)(2,1)} %get-tuple-element.7.kxy_lo, ...), custom_call_target="tpu_custom_call" | custom-call | tf_op jit(solution)/shard_map/pallas_call | solution.py:157
  108.5 1.4 broadcast_multiply_fusion.2
  110.0 0.2 broadcast_in_dim.790
  110.3 0.7 dynamic_update_slice.6
  111.0 0.1 dynamic-slice_add_fusion
  111.2 0.7 dynamic_update_slice.7
  111.9 1.3 copy-done.6
  113.4 9.2 %all-gather = f32[8,2,2]{2,1,0:T(2,128)S(1)} all-gather(f32[1,2,2]{2,1,0:T(2,128)S(1)} %bitcast.159), channel_id=1, replica_groups=mesh['region'=4,'tile'=8] {'tile'}, dimensions={0}, use_global_device_ids=true | all-gather | bytes 144 | tf_op jit(solution)/shard_map/all_gather | solution.py:127
  122.9 24.9 %reduce-scatter.2.cloned.1.call-done = f32[8,16,512]{2,1,0:T(8,128)} async-done(((f32[8,128,512]{2,1,0:T(8,128)}), f32[8,16,512]{2,1,0:T(8,128)}) %reduce-scatter.2.cloned.1.call-update) | async-done | bytes 262160 | tf_op jit(solution)/shard_map/reduce_scatter | solution.py:186
  147.8 1.8 %multiply_divide_fusion = f32[8,16,512]{2,1,0:T(8,128)} fusion(f32[8,16,512]{2,1,0:T(8,128)S(1)} %copy-done.7, f32[8,16,512]{2,1,0:T(8,128)} %reduce-scatter.2.cloned.1.call-done, f32[16]{0:T(128)S(1)} %broadcast_add_fusion.2), kind=kLoop, calls=%fused_computation.41 | loop fusion | flops 196608 | bytes 786496 | tf_op jit(solution)/shard_map/div | solution.py:192
  (88 shorter events, 4.9 us)
Async XLA Ops:
  6.5 22.8 %copy-start = (f32[6,3,3,15]{3,2,1,0:T(4,128)S(1)}, f32[6,3,3,15]{3,2,1,0:T(4,128)}, u32[]{:S(2)}) copy-start(f32[6,3,3,15]{3,2,1,0:T(4,128)} %param.10) | copy-start | bytes 9724
  6.5 19.7 %copy-start.8 = (s32[2]{0:T(128)S(1)}, s32[2]{0:T(128)}, u32[]{:S(2)}) copy-start(s32[2]{0:T(128)} %param.8) | copy-start | bytes 28
  6.5 80.5 %all-gather.3.cloned.1.call-start = ((), (), s32[]{:S(2)}) async-start(), calls=%async_computation.1 | async-start | bytes 6488064 | tf_op jit(solution)/shard_map/all_gather | solution.py:132
  7.6 9.7 %collective-permute-start = (f32[7,16,512]{2,1,0:T(8,128)S(1)}, f32[7,16,512]{2,1,0:T(8,128)S(1)}, u32[]{:S(2)}, u32[]{:S(2)}) collective-permute-start(f32[7,16,512]{2,1,0:T(8,128)S(1)} %get-tuple-element.21), channel_id=1, source_target_pairs={{0,8},{8,16},{16,24},{1,9},{9,17},{17,25},{2,10},{10,18},{18,26},{... | collective-permute-start | bytes 688136 | tf_op jit(solution)/shard_map/ppermute | solution.py:22
  12.5 11.7 %collective-permute-start.1 = (f32[7,16,512]{2,1,0:T(8,128)S(1)}, f32[7,16,512]{2,1,0:T(8,128)S(1)}, u32[]{:S(2)}, u32[]{:S(2)}) collective-permute-start(f32[7,16,512]{2,1,0:T(8,128)S(1)} %get-tuple-element.22), channel_id=1, source_target_pairs={{8,0},{16,8},{24,16},{9,1},{17,9},{25,17},{10,2},{18,10},{26,18},{... | collective-permute-start | bytes 688136 | tf_op jit(solution)/shard_map/ppermute | solution.py:24
  26.2 121.7 %reduce-scatter.2.cloned.1.call-start = ((), (), s32[]{:S(2)}) async-start(), calls=%async_computation.2 | async-start | bytes 2359296 | tf_op jit(solution)/shard_map/reduce_scatter | solution.py:186
  34.1 3.7 %copy-start.2 = (f32[2,3,512,128]{2,3,1,0:T(8,128)}, f32[2,3,512,128]{2,3,1,0:T(8,128)S(1)}, u32[]{:S(2)}) copy-start(f32[2,3,512,128]{2,3,1,0:T(8,128)S(1)} %get-tuple-element.17) | copy-start | bytes 4718596
  34.1 3.7 %copy-start.4 = (f32[2,3,512,128]{2,3,1,0:T(8,128)}, f32[2,3,512,128]{2,3,1,0:T(8,128)S(1)}, u32[]{:S(2)}) copy-start(f32[2,3,512,128]{2,3,1,0:T(8,128)S(1)} %get-tuple-element.18) | copy-start | bytes 4718596
  47.2 5.5 %copy-start.1 = (f32[6]{0:T(128)S(1)}, f32[6]{0:T(128)}, u32[]{:S(2)}) copy-start(f32[6]{0:T(128)} %param.11) | copy-start | bytes 76
  56.1 2.0 %copy-start.3 = (f32[2,3,512,128]{2,3,1,0:T(8,128)S(1)}, f32[2,3,512,128]{2,3,1,0:T(8,128)}, u32[]{:S(2)}) copy-start(f32[2,3,512,128]{2,3,1,0:T(8,128)} %copy-done.2) | copy-start | bytes 4718596
  56.1 2.5 %copy-start.5 = (f32[2,3,512,128]{2,3,1,0:T(8,128)S(1)}, f32[2,3,512,128]{2,3,1,0:T(8,128)}, u32[]{:S(2)}) copy-start(f32[2,3,512,128]{2,3,1,0:T(8,128)} %copy-done.4) | copy-start | bytes 4718596
  111.1 36.7 %copy-start.7 = (f32[8,16,512]{2,1,0:T(8,128)S(1)}, f32[8,16,512]{2,1,0:T(8,128)}, u32[]{:S(2)}) copy-start(f32[8,16,512]{2,1,0:T(8,128)} %param.6) | copy-start | bytes 786436
  111.9 1.3 copy-start.6
Sparse Core Ops, SparseCore 0:
  26.3 60.6 all-gather.2
  113.4 34.3 reduce-scatter.1

commit v10 on v9

--- a/solution.py
+++ b/solution.py
@@ -79,7 +79,7 @@
 
 
 def tile_kernel(win_rows, rank_terms, starts_ref, gathered_ref, kxy_hi, kxy_lo, tz_hi, tz_lo, fxy_hi, fxy_lo,
-                fz_hi, fz_lo, obs_ref, out_ref, window, sem):
+                obs_ref, out_ref, window, sem):
     j = pl.program_id(0)
     start = pl.multiple_of(starts_ref[j], 8)
     copy = pltpu.make_async_copy(gathered_ref.at[:, pl.ds(start, win_rows), :], window, sem)
@@ -102,10 +102,11 @@
         c = part[q * cells : (q + 1) * cells]
         c_hi = c.astype(jnp.bfloat16)
         c_lo = (c - c_hi.astype(f32)).astype(jnp.bfloat16)
+        nt = (((1,), (1,)), ((), ()))
         term = (
-            jnp.dot(c_hi, fz_hi[0, q], preferred_element_type=f32)
-            + jnp.dot(c_lo, fz_hi[0, q], preferred_element_type=f32)
-            + jnp.dot(c_hi, fz_lo[0, q], preferred_element_type=f32)
+            lax.dot_general(c_hi, tz_hi[0, q], nt, preferred_element_type=f32)
+            + lax.dot_general(c_lo, tz_hi[0, q], nt, preferred_element_type=f32)
+            + lax.dot_general(c_hi, tz_lo[0, q], nt, preferred_element_type=f32)
         )
         correction = term if correction is None else correction + term
     out_ref[0] = correction
@@ -151,7 +152,6 @@
     obs = observed.transpose(1, 0, 2, 3).reshape(tile_count, cells, depth)
     kxy_hi, kxy_lo = split_bf16(kxy)
     tz_hi, tz_lo = split_bf16(tz)
-    fz_hi, fz_lo = split_bf16(jnp.swapaxes(tz, -1, -2))
     fxy_hi, fxy_lo = split_bf16(fxy)
     per_tile = lambda *shape: pl.BlockSpec((1,) + shape, lambda j, s: (j,) + (0,) * len(shape))
     correction = pl.pallas_call(
@@ -167,8 +167,6 @@
                 per_tile(rank_terms, depth, depth),
                 per_tile(rank_terms * cells, cells),
                 per_tile(rank_terms * cells, cells),
-                per_tile(rank_terms, depth, depth),
-                per_tile(rank_terms, depth, depth),
                 per_tile(cells, depth),
             ],
             out_specs=per_tile(cells, depth),
@@ -176,7 +174,7 @@
         ),
         out_shape=jax.ShapeDtypeStruct((tile_count, cells, depth), jnp.float32),
         compiler_params=pltpu.CompilerParams(vmem_limit_bytes=60 * 1024 * 1024),
-    )(starts, gathered, kxy_hi, kxy_lo, tz_hi, tz_lo, fxy_hi, fxy_lo, fz_hi, fz_lo, obs)
+    )(starts, gathered, kxy_hi, kxy_lo, tz_hi, tz_lo, fxy_hi, fxy_lo, obs)
     weighted = (weight[:, None, None] * correction).reshape(tile_count, block_x, tile_rows, depth)
 
     numerator = jnp.zeros((block_x, region_rows, depth), jnp.float32)

time: 157 us -> 155 us (0.987)
  waiting for transfers between devices: 51.2 us -> 67.7 us
  local copies, waits for them, and re-layouts: 24.4 us -> 12.7 us
  other arithmetic: 26.3 us -> 21.7 us
  Pallas kernels: 21.5 us -> 19.7 us
    all_gather x1, waiting for transfers between devices: 16.6 us -> 32.2 us  [on_device(): gathered = lax.all_gather(rimmed, 'tile', axis=1, tiled=True)]
    convert_element_type x2 -> x0, local copies, waits for them, and re-layouts: 9.36 us -> none  [split_bf16(): return (high.astype(jnp.bfloat16), (values - high).astype(jnp.bfloat16))]
    convert_element_type x4 -> x3, other arithmetic: 13 us -> 9.03 us  [split_bf16(): return (high.astype(jnp.bfloat16), (values - high).astype(jnp.bfloat16))]
    pallas_call x1, Pallas kernels: 21.5 us -> 19.7 us  [on_device(): pl.pallas_call(functools.partial(tile_kernel, win_rows, rank_terms), grid...]
  transfers between devices with their start and end apart: 4 -> 4, of which waited for: 4 -> 4; matrix products, arithmetic and copies ran while one was open for 26% -> 16% of each run, Pallas kernels for 0% -> 0%
where the time goes in v10:
time: 155 us
  waiting for transfers between devices  67.7 us (44%)
  other arithmetic  21.7 us (14%)
  Pallas kernels  19.7 us (13%)
  between operations  17.6 us (11%)
  local copies, waits for them, and re-layouts  12.7 us (8%)
  blocking collectives  9.11 us (6%)
  starting transfers between devices  6.32 us (4%)
    all_gather x1, waiting for transfers between devices, on_device(): gathered = lax.all_gather(rimmed, 'tile', axis=1, tiled=True)  32.2 us
    reduce_scatter x1, waiting for transfers between devices, on_device(): lax.psum_scatter(numerator, 'tile', scatter_dimension=1, tiled=True)  25.1 us
    pallas_call x1, Pallas kernels, on_device(): pl.pallas_call(functools.partial(tile_kernel, win_rows, rank_terms), grid...  19.7 us
    all_gather x1, blocking collectives, on_device(): all_info = lax.all_gather(tile_info, 'tile', tiled=True)  9.11 us
    convert_element_type x3, other arithmetic, split_bf16(): return (high.astype(jnp.bfloat16), (values - high).astype(jnp.bfloat16))  9.03 us
    ppermute x1, waiting for transfers between devices, with_halo(): lax.ppermute(head, axis, [((i + 1) % count, i) for i in range(ends)])  6.86 us
    ppermute x1, starting transfers between devices, with_halo(): lax.ppermute(tail, axis, [(i, (i + 1) % count) for i in range(ends)])  4.99 us
    ppermute x1, waiting for transfers between devices, with_halo(): lax.ppermute(tail, axis, [(i, (i + 1) % count) for i in range(ends)])  3.53 us
  transfers between devices with their start and end apart: 4, of which 4 were waited for; matrix products, arithmetic and copies ran while one was open for 16% of the time, Pallas kernels for 0%

profile of v10, /device:TPU:0, one launch (start us, length us, event | category | flops | bytes accessed | tf_op | source)
XLA Modules:
  0.0 154.9 jit_solution(7290704754410406574)
XLA Ops:
  6.5 1.1 fusion.72
  7.7 5.0 %collective-permute-start = (f32[7,16,512]{2,1,0:T(8,128)S(1)}, f32[7,16,512]{2,1,0:T(8,128)S(1)}, u32[]{:S(2)}, u32[]{:S(2)}) collective-permute-start(f32[7,16,512]{2,1,0:T(8,128)S(1)} %get-tuple-element.19), channel_id=1, source_target_pairs={{0,8},{8,16},{16,24},{1,9},{9,17},{17,25},{2,10},{10,18},{18,26},{... | collective-permute-start | bytes 688136 | tf_op jit(solution)/shard_map/ppermute | solution.py:22
  12.7 1.3 collective-permute-start.1
  14.0 3.5 %collective-permute-done = f32[7,16,512]{2,1,0:T(8,128)S(1)} collective-permute-done((f32[7,16,512]{2,1,0:T(8,128)S(1)}, f32[7,16,512]{2,1,0:T(8,128)S(1)}, u32[]{:S(2)}, u32[]{:S(2)}) %collective-permute-start) | collective-permute-done | bytes 229408 | tf_op jit(solution)/shard_map/ppermute | solution.py:22
  17.5 6.9 %collective-permute-done.1 = f32[7,16,512]{2,1,0:T(8,128)S(1)} collective-permute-done((f32[7,16,512]{2,1,0:T(8,128)S(1)}, f32[7,16,512]{2,1,0:T(8,128)S(1)}, u32[]{:S(2)}, u32[]{:S(2)}) %collective-permute-start.1) | collective-permute-done | bytes 229408 | tf_op jit(solution)/shard_map/ppermute | solution.py:24
  24.4 1.9 %pad_maximum_fusion.1 = f32[22,16,512]{2,1,0:T(8,128)} fusion(f32[7,16,512]{2,1,0:T(8,128)S(1)} %collective-permute-done.1, f32[8,16,512]{2,1,0:T(8,128)} %param.6, f32[7,16,512]{2,1,0:T(8,128)S(1)} %collective-permute-done), kind=kLoop, calls=%fused_computation.35 | loop fusion | flops 360448 | bytes 1441792 | tf_op jit(solution)/shard_map/concatenate | solution.py:20
  26.4 0.6 fusion.78
  29.6 0.6 gather_fusion.1
  30.2 0.1 fusion.75
  30.3 0.1 copy.193
  30.4 0.1 copy.194
  30.5 0.1 copy.195
  30.6 0.1 copy.196
  30.7 0.1 copy.197
  30.8 0.1 copy.198
  31.1 0.1 copy.201
  31.8 0.1 fusion.77
  31.9 0.1 copy.177
  32.0 0.1 copy.178
  33.4 0.1 fusion.76
  33.5 0.1 copy.161
  35.0 1.1 copy.208
  36.0 0.6 gather_fusion
  38.1 0.5 add_subtract_fusion
  38.6 0.2 select_select_fusion.4
  38.9 0.4 select_select_fusion.3
  39.3 0.6 fusion.17
  39.8 0.2 broadcast_multiply_fusion.1
  40.0 1.5 select_select_fusion
  41.6 0.6 pad_slice_fusion.3
  42.1 1.4 fusion.2
  43.6 3.1 %fusion.1 = (bf16[2,3,512,512]{3,2,1,0:T(8,128)(2,1)}, bf16[2,3,512,512]{3,2,1,0:T(8,128)(2,1)}) fusion(f32[2,3,512,128]{3,2,1,0:T(8,128)S(1)} %get-tuple-element.14, f32[2,3,512,128]{3,2,1,0:T(8,128)S(1)} %get-tuple-element.15, f32[2,3,512,128]{3,2,1,0:T(8,128)S(1)} %get-tuple-element.16, f32[2,3,512,128]{3,2,1,0:T(8,128)S(1)} %get-tuple-element.13), kind=kLoop, calls=%fused_computation.7 | loop fusion | flops 11010048 | bytes 12582912 | tf_op jit(solution)/shard_map/convert_element_type | solution.py:33
  46.8 0.4 select_select_fusion.2
  47.2 0.7 subtract_compare_fusion.14
  48.0 1.6 %select_select_fusion.1 = f32[2,3,32,1232]{3,2,1,0:T(8,128)S(1)} fusion(f32[2,3]{1,0:T(2,128)S(1)} %bitcast.109, f32[2,3]{1,0:T(2,128)S(1)} %bitcast.107, f32[2,3]{1,0:T(2,128)S(1)} %bitcast.105, f32[2,3]{1,0:T(2,128)S(1)} %bitcast.103, f32[2,3]{1,0:T(2,128)S(1)} %bitcast.101, f32[2,3]{1,0:T(2,128)S(1)} %bitcast.99, f32[2,3]{1,0:T(2,128)S(1)} %bitcast.97, ...), kind=kLoop, calls=%fused_computation.33 | loop fusion | flops 3548160 | bytes 2129256 | tf_op jit(solution)/shard_map/jit(_where)/select_n | solution.py:59
  49.6 0.9 broadcast_multiply_fusion
  50.5 4.5 %fusion = (bf16[2,768,1232]{2,1,0:T(8,128)(2,1)}, bf16[2,768,1232]{2,1,0:T(8,128)(2,1)}) fusion(f32[2,3,8,32,1232]{4,3,2,1,0:T(8,128)S(1)} %broadcast_multiply_fusion), kind=kLoop, calls=%fused_computation.6 | loop fusion | flops 7569408 | bytes 15138816 | tf_op jit(solution)/shard_map/convert_element_type | solution.py:33
  55.0 32.2 %all-gather.3.cloned.1.call-done.gathered_ref = f32[22,128,512]{2,1,0:T(8,128)} async-done(((f32[22,16,512]{2,1,0:T(8,128)}), f32[22,128,512]{2,1,0:T(8,128)}) %all-gather.3.cloned.1.call-update) | async-done | bytes 5767184 | tf_op jit(solution)/shard_map/all_gather | solution.py:133
  87.2 19.7 %shard_map.64 = f32[2,256,512]{2,1,0:T(8,128)} custom-call(s32[2]{0:T(128)} %get-tuple-element.6.starts_ref, f32[22,128,512]{2,1,0:T(8,128)} %all-gather.3.cloned.1.call-done.gathered_ref, bf16[2,768,1232]{2,1,0:T(8,128)(2,1)} %get-tuple-element.8.kxy_hi, bf16[2,768,1232]{2,1,0:T(8,128)(2,1)} %get-tuple-element.7.kxy_lo, ...), custom_call_target="tpu_custom_call" | custom-call | tf_op jit(solution)/shard_map/pallas_call | solution.py:157
  106.9 1.4 broadcast_multiply_fusion.2
  108.4 0.2 broadcast_in_dim.790
  108.7 0.7 dynamic_update_slice.6
  109.4 0.1 dynamic-slice_add_fusion
  109.5 0.7 dynamic_update_slice.7
  110.3 1.4 copy-done.2
  111.8 9.1 %all-gather = f32[8,2,2]{2,1,0:T(2,128)S(1)} all-gather(f32[1,2,2]{2,1,0:T(2,128)S(1)} %bitcast.156), channel_id=1, replica_groups=mesh['region'=4,'tile'=8] {'tile'}, dimensions={0}, use_global_device_ids=true | all-gather | bytes 144 | tf_op jit(solution)/shard_map/all_gather | solution.py:128
  121.2 25.1 %reduce-scatter.2.cloned.1.call-done = f32[8,16,512]{2,1,0:T(8,128)} async-done(((f32[8,128,512]{2,1,0:T(8,128)}), f32[8,16,512]{2,1,0:T(8,128)}) %reduce-scatter.2.cloned.1.call-update) | async-done | bytes 262160 | tf_op jit(solution)/shard_map/reduce_scatter | solution.py:184
  146.3 1.8 %multiply_divide_fusion = f32[8,16,512]{2,1,0:T(8,128)} fusion(f32[8,16,512]{2,1,0:T(8,128)S(1)} %copy-done.3, f32[8,16,512]{2,1,0:T(8,128)} %reduce-scatter.2.cloned.1.call-done, f32[16]{0:T(128)S(1)} %broadcast_add_fusion.2), kind=kLoop, calls=%fused_computation.38 | loop fusion | flops 196608 | bytes 786496 | tf_op jit(solution)/shard_map/div | solution.py:190
  (81 shorter events, 4.4 us)
Async XLA Ops:
  6.5 23.0 %copy-start = (f32[6,3,3,15]{3,2,1,0:T(4,128)S(1)}, f32[6,3,3,15]{3,2,1,0:T(4,128)}, u32[]{:S(2)}) copy-start(f32[6,3,3,15]{3,2,1,0:T(4,128)} %param.10) | copy-start | bytes 9724
  6.5 19.8 %copy-start.5 = (s32[2]{0:T(128)S(1)}, s32[2]{0:T(128)}, u32[]{:S(2)}) copy-start(s32[2]{0:T(128)} %param.8) | copy-start | bytes 28
  6.5 23.0 %copy-start.6 = (s32[2]{0:T(128)S(1)}, s32[2]{0:T(128)}, u32[]{:S(2)}) copy-start(s32[2]{0:T(128)} %param.9) | copy-start | bytes 28
  6.5 80.6 %all-gather.3.cloned.1.call-start = ((), (), s32[]{:S(2)}) async-start(), calls=%async_computation.1 | async-start | bytes 6488064 | tf_op jit(solution)/shard_map/all_gather | solution.py:133
  7.7 27.3 %copy-start.4 = (f32[8,2,32,512]{3,2,1,0:T(8,128)S(1)}, f32[8,2,32,512]{3,2,1,0:T(8,128)}, u32[]{:S(2)}) copy-start(f32[8,2,32,512]{3,2,1,0:T(8,128)} %param.7) | copy-start | bytes 3145732
  7.7 9.8 %collective-permute-start = (f32[7,16,512]{2,1,0:T(8,128)S(1)}, f32[7,16,512]{2,1,0:T(8,128)S(1)}, u32[]{:S(2)}, u32[]{:S(2)}) collective-permute-start(f32[7,16,512]{2,1,0:T(8,128)S(1)} %get-tuple-element.19), channel_id=1, source_target_pairs={{0,8},{8,16},{16,24},{1,9},{9,17},{17,25},{2,10},{10,18},{18,26},{... | collective-permute-start | bytes 688136 | tf_op jit(solution)/shard_map/ppermute | solution.py:22
  12.7 11.7 %collective-permute-start.1 = (f32[7,16,512]{2,1,0:T(8,128)S(1)}, f32[7,16,512]{2,1,0:T(8,128)S(1)}, u32[]{:S(2)}, u32[]{:S(2)}) collective-permute-start(f32[7,16,512]{2,1,0:T(8,128)S(1)} %get-tuple-element.20), channel_id=1, source_target_pairs={{8,0},{16,8},{24,16},{9,1},{17,9},{25,17},{10,2},{18,10},{26,18},{... | collective-permute-start | bytes 688136 | tf_op jit(solution)/shard_map/ppermute | solution.py:24
  26.3 9.7 %copy-start.1 = (f32[6]{0:T(128)S(1)}, f32[6]{0:T(128)}, u32[]{:S(2)}) copy-start(f32[6]{0:T(128)} %param.11) | copy-start | bytes 76
  26.3 120.0 %reduce-scatter.2.cloned.1.call-start = ((), (), s32[]{:S(2)}) async-start(), calls=%async_computation.2 | async-start | bytes 2359296 | tf_op jit(solution)/shard_map/reduce_scatter | solution.py:184
  109.5 36.8 %copy-start.3 = (f32[8,16,512]{2,1,0:T(8,128)S(1)}, f32[8,16,512]{2,1,0:T(8,128)}, u32[]{:S(2)}) copy-start(f32[8,16,512]{2,1,0:T(8,128)} %param.6) | copy-start | bytes 786436
  110.3 1.4 copy-start.2
Sparse Core Ops, SparseCore 0:
  26.4 60.6 all-gather.2
  111.8 34.4 reduce-scatter.1

commit v11 on v9

--- a/solution.py
+++ b/solution.py
@@ -90,23 +90,39 @@
     f32 = jnp.float32
     part = jnp.dot(kxy_hi[0], data, preferred_element_type=f32) + jnp.dot(kxy_lo[0], data, preferred_element_type=f32)
     cells = part.shape[0] // rank_terms
+    depth_blocks = depth // 128
+
+    def along_depth(rows, strip_hi, strip_lo, q, passes):
+        out = []
+        for b in range(depth_blocks):
+            lo = max(b - 1, 0)
+            hi = min(b + 2, depth_blocks)
+            sub = slice((lo - b + 1) * 128, (hi - b + 1) * 128)
+            cols = slice(lo * 128, hi * 128)
+            acc = None
+            for a, m in passes(rows[:, cols], strip_hi[0, q, sub], strip_lo[0, q, sub]):
+                t = jnp.dot(a, m, preferred_element_type=f32)
+                acc = t if acc is None else acc + t
+            out.append(acc)
+        return jnp.concatenate(out, axis=1)
+
+    two = lambda a, mh, ml: [(a, mh), (a, ml)]
     blurred = None
     for q in range(rank_terms):
         p = part[q * cells : (q + 1) * cells].astype(jnp.bfloat16)
-        term = jnp.dot(p, tz_hi[0, q], preferred_element_type=f32) + jnp.dot(p, tz_lo[0, q], preferred_element_type=f32)
+        term = along_depth(p, tz_hi, tz_lo, q, two)
         blurred = term if blurred is None else blurred + term
     quotient = (obs_ref[0] / blurred).astype(jnp.bfloat16)
     part = jnp.dot(fxy_hi[0], quotient, preferred_element_type=f32) + jnp.dot(fxy_lo[0], quotient, preferred_element_type=f32)
+    def three(a, mh, ml):
+        a_hi = a.astype(jnp.bfloat16)
+        a_lo = (a - a_hi.astype(f32)).astype(jnp.bfloat16)
+        return [(a_hi, mh), (a_lo, mh), (a_hi, ml)]
+
     correction = None
     for q in range(rank_terms):
         c = part[q * cells : (q + 1) * cells]
-        c_hi = c.astype(jnp.bfloat16)
-        c_lo = (c - c_hi.astype(f32)).astype(jnp.bfloat16)
-        term = (
-            jnp.dot(c_hi, fz_hi[0, q], preferred_element_type=f32)
-            + jnp.dot(c_lo, fz_hi[0, q], preferred_element_type=f32)
-            + jnp.dot(c_hi, fz_lo[0, q], preferred_element_type=f32)
-        )
+        term = along_depth(c, fz_hi, fz_lo, q, three)
         correction = term if correction is None else correction + term
     out_ref[0] = correction
 
@@ -142,16 +158,22 @@
     kxy = kron_band(ax, ay, block_x, tile_rows, win_rows, win_x * win_rows, 0, shifts[:, None]).reshape(
         tile_count, rank_terms * block_x * tile_rows, win_x * win_rows
     )
-    tz = depth_band(az, depth, 128)
+    si = lax.broadcasted_iota(jnp.int32, (3 * 128, 128), 0)
+    sj = lax.broadcasted_iota(jnp.int32, (3 * 128, 128), 1)
+    sd = si - 128 - sj + rim
+    strip = jnp.zeros((tile_count, rank_terms, 3 * 128, 128), jnp.float32)
+    for k in range(kt):
+        strip = jnp.where(sd == k, az[..., k, None, None], strip)
 
     cells = block_x * tile_rows
     fxy = kron_band(ax[..., ::-1], ay[..., ::-1], block_x, tile_rows, tile_rows, cells, -rim, -rim).reshape(
         tile_count, rank_terms * cells, cells
     )
+    fxy = weight[:, None, None] * fxy
     obs = observed.transpose(1, 0, 2, 3).reshape(tile_count, cells, depth)
     kxy_hi, kxy_lo = split_bf16(kxy)
-    tz_hi, tz_lo = split_bf16(tz)
-    fz_hi, fz_lo = split_bf16(jnp.swapaxes(tz, -1, -2))
+    tz_hi, tz_lo = split_bf16(strip)
+    fz_hi, fz_lo = split_bf16(strip[..., ::-1, ::-1])
     fxy_hi, fxy_lo = split_bf16(fxy)
     per_tile = lambda *shape: pl.BlockSpec((1,) + shape, lambda j, s: (j,) + (0,) * len(shape))
     correction = pl.pallas_call(
@@ -163,12 +185,12 @@
                 pl.BlockSpec(memory_space=pl.ANY),
                 per_tile(rank_terms * cells, win_x * win_rows),
                 per_tile(rank_terms * cells, win_x * win_rows),
-                per_tile(rank_terms, depth, depth),
-                per_tile(rank_terms, depth, depth),
+                per_tile(rank_terms, 3 * 128, 128),
+                per_tile(rank_terms, 3 * 128, 128),
                 per_tile(rank_terms * cells, cells),
                 per_tile(rank_terms * cells, cells),
-                per_tile(rank_terms, depth, depth),
-                per_tile(rank_terms, depth, depth),
+                per_tile(rank_terms, 3 * 128, 128),
+                per_tile(rank_terms, 3 * 128, 128),
                 per_tile(cells, depth),
             ],
             out_specs=per_tile(cells, depth),
@@ -177,7 +199,7 @@
         out_shape=jax.ShapeDtypeStruct((tile_count, cells, depth), jnp.float32),
         compiler_params=pltpu.CompilerParams(vmem_limit_bytes=60 * 1024 * 1024),
     )(starts, gathered, kxy_hi, kxy_lo, tz_hi, tz_lo, fxy_hi, fxy_lo, fz_hi, fz_lo, obs)
-    weighted = (weight[:, None, None] * correction).reshape(tile_count, block_x, tile_rows, depth)
+    weighted = correction.reshape(tile_count, block_x, tile_rows, depth)
 
     numerator = jnp.zeros((block_x, region_rows, depth), jnp.float32)
     for j in range(tile_count):

time: 157 us -> 155 us (0.987)
  waiting for transfers between devices: 51.2 us -> 62.2 us
  local copies, waits for them, and re-layouts: 24.4 us -> 17.9 us
  other arithmetic: 26.3 us -> 22 us
  Pallas kernels: 21.5 us -> 19.7 us
    all_gather x1, waiting for transfers between devices: 16.6 us -> 26.6 us  [on_device(): gathered = lax.all_gather(rimmed, 'tile', axis=1, tiled=True)]
    convert_element_type x2 -> x0, local copies, waits for them, and re-layouts: 9.36 us -> none  [split_bf16(): return (high.astype(jnp.bfloat16), (values - high).astype(jnp.bfloat16))]
    convert_element_type x4 -> x5, other arithmetic: 13 us -> 10.6 us  [split_bf16(): return (high.astype(jnp.bfloat16), (values - high).astype(jnp.bfloat16))]
    slice x16, local copies, waits for them, and re-layouts: 1.58 us -> 3.84 us  [kron_band(): ea = jnp.where(da == k, taps_a[..., k, None, None], ea)]
    select_n x2 -> x1, other arithmetic: 2.14 us -> 0.01 us  [on_device(): filters = psf_taps[tile_view]]
    pallas_call x1, Pallas kernels: 21.5 us -> 19.7 us  [on_device(): pl.pallas_call(functools.partial(tile_kernel, win_rows, rank_terms), grid...]
    rev x0 -> x1, local copies, waits for them, and re-layouts: none -> 1.6 us  [on_device(): fz_hi, fz_lo = split_bf16(strip[..., ::-1, ::-1])]
  transfers between devices with their start and end apart: 4 -> 4, of which waited for: 4 -> 4; matrix products, arithmetic and copies ran while one was open for 26% -> 20% of each run, Pallas kernels for 0% -> 0%
where the time goes in v11:
time: 155 us
  waiting for transfers between devices  62.2 us (40%)
  other arithmetic  22 us (14%)
  Pallas kernels  19.7 us (13%)
  local copies, waits for them, and re-layouts  17.9 us (12%)
  between operations  17.4 us (11%)
  blocking collectives  9.18 us (6%)
  starting transfers between devices  6.19 us (4%)
    all_gather x1, waiting for transfers between devices, on_device(): gathered = lax.all_gather(rimmed, 'tile', axis=1, tiled=True)  26.6 us
    reduce_scatter x1, waiting for transfers between devices, on_device(): lax.psum_scatter(numerator, 'tile', scatter_dimension=1, tiled=True)  25.2 us
    pallas_call x1, Pallas kernels, on_device(): pl.pallas_call(functools.partial(tile_kernel, win_rows, rank_terms), grid...  19.7 us
    convert_element_type x5, other arithmetic, split_bf16(): return (high.astype(jnp.bfloat16), (values - high).astype(jnp.bfloat16))  10.6 us
    all_gather x1, blocking collectives, on_device(): all_info = lax.all_gather(tile_info, 'tile', tiled=True)  9.18 us
    ppermute x1, waiting for transfers between devices, with_halo(): lax.ppermute(head, axis, [((i + 1) % count, i) for i in range(ends)])  6.86 us
    ppermute x1, starting transfers between devices, with_halo(): lax.ppermute(tail, axis, [(i, (i + 1) % count) for i in range(ends)])  4.86 us
    slice x16, local copies, waits for them, and re-layouts, kron_band(): ea = jnp.where(da == k, taps_a[..., k, None, None], ea)  3.84 us
  transfers between devices with their start and end apart: 4, of which 4 were waited for; matrix products, arithmetic and copies ran while one was open for 20% of the time, Pallas kernels for 0%

profile of v11, /device:TPU:0, one launch (start us, length us, event | category | flops | bytes accessed | tf_op | source)
XLA Modules:
  0.0 154.5 jit_solution(18307741882151941065)
XLA Ops:
  6.5 1.1 fusion.73
  7.7 4.9 %collective-permute-start = (f32[7,16,512]{2,1,0:T(8,128)S(1)}, f32[7,16,512]{2,1,0:T(8,128)S(1)}, u32[]{:S(2)}, u32[]{:S(2)}) collective-permute-start(f32[7,16,512]{2,1,0:T(8,128)S(1)} %get-tuple-element.17), channel_id=1, source_target_pairs={{0,8},{8,16},{16,24},{1,9},{9,17},{17,25},{2,10},{10,18},{18,26},{... | collective-permute-start | bytes 688136 | tf_op jit(solution)/shard_map/ppermute | solution.py:22
  12.5 1.3 collective-permute-start.1
  13.8 3.5 %collective-permute-done = f32[7,16,512]{2,1,0:T(8,128)S(1)} collective-permute-done((f32[7,16,512]{2,1,0:T(8,128)S(1)}, f32[7,16,512]{2,1,0:T(8,128)S(1)}, u32[]{:S(2)}, u32[]{:S(2)}) %collective-permute-start) | collective-permute-done | bytes 229408 | tf_op jit(solution)/shard_map/ppermute | solution.py:22
  17.4 6.9 %collective-permute-done.1 = f32[7,16,512]{2,1,0:T(8,128)S(1)} collective-permute-done((f32[7,16,512]{2,1,0:T(8,128)S(1)}, f32[7,16,512]{2,1,0:T(8,128)S(1)}, u32[]{:S(2)}, u32[]{:S(2)}) %collective-permute-start.1) | collective-permute-done | bytes 229408 | tf_op jit(solution)/shard_map/ppermute | solution.py:24
  24.2 1.9 %pad_maximum_fusion = f32[22,16,512]{2,1,0:T(8,128)} fusion(f32[7,16,512]{2,1,0:T(8,128)S(1)} %collective-permute-done.1, f32[8,16,512]{2,1,0:T(8,128)} %param.6, f32[7,16,512]{2,1,0:T(8,128)S(1)} %collective-permute-done), kind=kLoop, calls=%fused_computation.34 | loop fusion | flops 360448 | bytes 1441792 | tf_op jit(solution)/shard_map/concatenate | solution.py:20
  26.2 0.6 fusion.79
  29.2 0.6 gather_fusion
  29.8 0.1 fusion.78
  30.0 0.1 copy.177
  30.1 0.1 copy.178
  31.4 0.1 fusion.77
  31.5 0.1 copy.161
  31.8 0.1 copy.172
  32.6 0.6 copy.166
  33.2 0.7 copy.167
  33.9 0.7 copy.168
  34.6 0.7 copy.169
  35.3 0.1 fusion.76
  35.4 0.1 copy.193
  36.9 0.6 fusion.18
  37.5 2.5 %fusion.2 = (bf16[2,3,384,128]{3,2,1,0:T(8,128)(2,1)}, f32[2,3,384,128]{3,2,1,0:T(8,128)S(1)}) fusion(f32[2,3]{1,0:T(2,128)S(1)} %bitcast.158, pred[384,128]{1,0:T(8,128)(4,1)S(1)} %get-tuple-element.130, f32[2,3]{1,0:T(2,128)S(1)} %bitcast.157, pred[384,128]{1,0:T(8,128)(4,1)S(1)} %get-tuple-element.131, f32[2,3]{1,0:T(2,128)S(1)} %bitcast.156, ...), kind=kLoop, calls=%fused_computation.29 | loop fusion | flops 5308416 | bytes 2507112 | tf_op jit(solution)/shard_map/convert_element_type | solution.py:33
  39.9 1.6 %rev.2 = f32[2,3,384,128]{3,2,1,0:T(8,128)S(1)} reverse(f32[2,3,384,128]{3,2,1,0:T(8,128)S(1)} %get-tuple-element.6), dimensions={2,3} | reverse | bytes 2359296 | tf_op jit(solution)/shard_map/rev | solution.py:176
  41.5 1.3 gather_fusion.1
  42.8 1.1 copy.208
  45.2 1.3 add_subtract_fusion
  46.5 0.9 select_select_fusion.4
  47.5 0.4 select_select_fusion.3
  47.9 0.9 reduce-precision_convert_fusion.3.tz_hi
  48.8 0.2 broadcast_multiply_fusion.1
  49.0 1.2 fusion.3
  50.2 1.5 fusion.1
  51.9 0.4 select_select_fusion.2
  52.3 0.9 subtract_compare_fusion.14
  53.2 1.7 %select_select_fusion.1 = f32[2,3,32,1232]{3,2,1,0:T(8,128)S(1)} fusion(f32[2,3]{1,0:T(2,128)S(1)} %bitcast.112, f32[2,3]{1,0:T(2,128)S(1)} %bitcast.110, f32[2,3]{1,0:T(2,128)S(1)} %bitcast.108, f32[2,3]{1,0:T(2,128)S(1)} %bitcast.106, f32[2,3]{1,0:T(2,128)S(1)} %bitcast.104, f32[2,3]{1,0:T(2,128)S(1)} %bitcast.102, f32[2,3]{1,0:T(2,128)S(1)} %bitcast.100, ...), kind=kLoop, calls=%fused_computation.32 | loop fusion | flops 3548160 | bytes 2129256 | tf_op jit(solution)/shard_map/jit(_where)/select_n | solution.py:59
  54.8 1.0 broadcast_multiply_fusion
  55.9 4.5 %fusion = (bf16[2,768,1232]{2,1,0:T(8,128)(2,1)}, bf16[2,768,1232]{2,1,0:T(8,128)(2,1)}) fusion(f32[2,3,8,32,1232]{4,3,2,1,0:T(8,128)S(1)} %broadcast_multiply_fusion), kind=kLoop, calls=%fused_computation.4 | loop fusion | flops 7569408 | bytes 15138816 | tf_op jit(solution)/shard_map/convert_element_type | solution.py:33
  60.4 26.6 %all-gather.3.cloned.1.call-done.gathered_ref = f32[22,128,512]{2,1,0:T(8,128)} async-done(((f32[22,16,512]{2,1,0:T(8,128)}), f32[22,128,512]{2,1,0:T(8,128)}) %all-gather.3.cloned.1.call-update) | async-done | bytes 5767184 | tf_op jit(solution)/shard_map/all_gather | solution.py:148
  87.0 19.7 %shard_map.64 = f32[2,256,512]{2,1,0:T(8,128)} custom-call(s32[2]{0:T(128)} %get-tuple-element.8.starts_ref, f32[22,128,512]{2,1,0:T(8,128)} %all-gather.3.cloned.1.call-done.gathered_ref, bf16[2,768,1232]{2,1,0:T(8,128)(2,1)} %get-tuple-element.10.kxy_hi, bf16[2,768,1232]{2,1,0:T(8,128)(2,1)} %get-tuple-element.9.kxy_lo, ...), custom_call_target="tpu_custom_call" | custom-call | tf_op jit(solution)/shard_map/pallas_call | solution.py:179
  106.6 1.3 fusion.72
  107.9 0.2 broadcast_in_dim.790
  108.2 0.7 dynamic_update_slice.6
  108.8 0.1 dynamic-slice_add_fusion
  109.0 0.8 dynamic_update_slice.7
  109.8 1.3 copy-done.2
  111.2 9.2 %all-gather = f32[8,2,2]{2,1,0:T(2,128)S(1)} all-gather(f32[1,2,2]{2,1,0:T(2,128)S(1)} %bitcast.159), channel_id=1, replica_groups=mesh['region'=4,'tile'=8] {'tile'}, dimensions={0}, use_global_device_ids=true | all-gather | bytes 144 | tf_op jit(solution)/shard_map/all_gather | solution.py:143
  120.8 25.2 %reduce-scatter.2.cloned.1.call-done = f32[8,16,512]{2,1,0:T(8,128)} async-done(((f32[8,128,512]{2,1,0:T(8,128)}), f32[8,16,512]{2,1,0:T(8,128)}) %reduce-scatter.2.cloned.1.call-update) | async-done | bytes 262160 | tf_op jit(solution)/shard_map/reduce_scatter | solution.py:208
  146.0 1.8 %multiply_divide_fusion = f32[8,16,512]{2,1,0:T(8,128)} fusion(f32[8,16,512]{2,1,0:T(8,128)S(1)} %copy-done.3, f32[8,16,512]{2,1,0:T(8,128)} %reduce-scatter.2.cloned.1.call-done, f32[16]{0:T(128)S(1)} %broadcast_add_fusion.2), kind=kLoop, calls=%fused_computation.36 | loop fusion | flops 196608 | bytes 786496 | tf_op jit(solution)/shard_map/div | solution.py:214
  (97 shorter events, 4.4 us)
Async XLA Ops:
  6.5 22.7 %copy-start = (f32[6,3,3,15]{3,2,1,0:T(4,128)S(1)}, f32[6,3,3,15]{3,2,1,0:T(4,128)}, u32[]{:S(2)}) copy-start(f32[6,3,3,15]{3,2,1,0:T(4,128)} %param.10) | copy-start | bytes 9724
  6.5 80.4 %all-gather.3.cloned.1.call-start = ((), (), s32[]{:S(2)}) async-start(), calls=%async_computation.1 | async-start | bytes 6488064 | tf_op jit(solution)/shard_map/all_gather | solution.py:148
  7.6 18.6 %copy-start.10 = (s32[2]{0:T(128)S(1)}, s32[2]{0:T(128)}, u32[]{:S(2)}) copy-start(s32[2]{0:T(128)} %param.8) | copy-start | bytes 28
  7.7 21.5 %copy-start.14 = (s32[2]{0:T(128)S(1)}, s32[2]{0:T(128)}, u32[]{:S(2)}) copy-start(s32[2]{0:T(128)} %param.9) | copy-start | bytes 28
  7.7 9.7 %collective-permute-start = (f32[7,16,512]{2,1,0:T(8,128)S(1)}, f32[7,16,512]{2,1,0:T(8,128)S(1)}, u32[]{:S(2)}, u32[]{:S(2)}) collective-permute-start(f32[7,16,512]{2,1,0:T(8,128)S(1)} %get-tuple-element.17), channel_id=1, source_target_pairs={{0,8},{8,16},{16,24},{1,9},{9,17},{17,25},{2,10},{10,18},{18,26},{... | collective-permute-start | bytes 688136 | tf_op jit(solution)/shard_map/ppermute | solution.py:22
  12.5 11.7 %collective-permute-start.1 = (f32[7,16,512]{2,1,0:T(8,128)S(1)}, f32[7,16,512]{2,1,0:T(8,128)S(1)}, u32[]{:S(2)}, u32[]{:S(2)}) collective-permute-start(f32[7,16,512]{2,1,0:T(8,128)S(1)} %get-tuple-element.18), channel_id=1, source_target_pairs={{8,0},{16,8},{24,16},{9,1},{17,9},{25,17},{10,2},{18,10},{26,18},{... | collective-permute-start | bytes 688136 | tf_op jit(solution)/shard_map/ppermute | solution.py:24
  26.1 119.8 %reduce-scatter.2.cloned.1.call-start = ((), (), s32[]{:S(2)}) async-start(), calls=%async_computation.2 | async-start | bytes 2359296 | tf_op jit(solution)/shard_map/reduce_scatter | solution.py:208
  29.2 2.2 %copy-start.9 = (s32[1024]{0:T(1024)}, s32[1024]{0:T(1024)S(1)}, u32[]{:S(2)}) copy-start(s32[1024]{0:T(1024)S(1)} %pad_clamp_fusion) | copy-start | bytes 12292
  39.9 1.6 %copy-start.1 = (f32[6]{0:T(128)S(1)}, f32[6]{0:T(128)}, u32[]{:S(2)}) copy-start(f32[6]{0:T(128)} %param.11) | copy-start | bytes 76
  39.9 2.9 %copy-start.4 = (f32[8,2,32,512]{3,2,1,0:T(8,128)S(1)}, f32[8,2,32,512]{3,2,1,0:T(8,128)}, u32[]{:S(2)}) copy-start(f32[8,2,32,512]{3,2,1,0:T(8,128)} %param.7) | copy-start | bytes 3145732
  42.8 3.7 %copy-start.5 = (f32[2,3,1]{1,0,2:T(2,128)S(1)}, f32[2,3,1]{1,0,2:T(2,128)}, u32[]{:S(2)}) copy-start(f32[2,3,1]{1,0,2:T(2,128)} %copy.166) | copy-start | bytes 76
  49.0 1.3 copy-start.11
  50.2 1.6 %copy-start.6 = (f32[2,3,1]{1,0,2:T(2,128)S(1)}, f32[2,3,1]{1,0,2:T(2,128)}, u32[]{:S(2)}) copy-start(f32[2,3,1]{1,0,2:T(2,128)} %copy.167) | copy-start | bytes 76
  50.2 1.6 %copy-start.7 = (f32[2,3,1]{1,0,2:T(2,128)S(1)}, f32[2,3,1]{1,0,2:T(2,128)}, u32[]{:S(2)}) copy-start(f32[2,3,1]{1,0,2:T(2,128)} %copy.168) | copy-start | bytes 76
  50.2 1.6 %copy-start.8 = (f32[2,3,1]{1,0,2:T(2,128)S(1)}, f32[2,3,1]{1,0,2:T(2,128)}, u32[]{:S(2)}) copy-start(f32[2,3,1]{1,0,2:T(2,128)} %copy.169) | copy-start | bytes 76
  109.7 1.4 copy-start.2
  109.7 1.4 copy-start.12
  109.7 1.4 copy-start.13
  109.8 36.2 %copy-start.3 = (f32[8,16,512]{2,1,0:T(8,128)S(1)}, f32[8,16,512]{2,1,0:T(8,128)}, u32[]{:S(2)}) copy-start(f32[8,16,512]{2,1,0:T(8,128)} %param.6) | copy-start | bytes 786436
Sparse Core Ops, SparseCore 0:
  26.3 60.6 all-gather.2
  111.2 34.6 reduce-scatter.1

commit v12 on v7

--- a/solution.py
+++ b/solution.py
@@ -118,19 +118,28 @@
 
     quotient = observed.transpose(1, 0, 2, 3).reshape(tile_count, cells, depth) / blurred
 
-    fxy = kron_band(ax[..., ::-1], ay[..., ::-1], block_x, tile_rows, tile_rows, cells, -rim, -rim).reshape(
-        tile_count, rank_terms * cells, cells
-    )
+    ry = ay[..., ::-1]
+    rx = ax[..., ::-1]
+    ci = lax.broadcasted_iota(jnp.int32, (tile_rows, cells), 1)
+    fy_d = ci % tile_rows - lax.broadcasted_iota(jnp.int32, (tile_rows, cells), 0) + rim
+    fx_d = lax.broadcasted_iota(jnp.int32, (block_x, cells), 1) // tile_rows - lax.broadcasted_iota(
+        jnp.int32, (block_x, cells), 0
+    ) + rim
+    fy_e = jnp.zeros((tile_count, rank_terms, tile_rows, cells), jnp.float32)
+    fx_e = jnp.zeros((tile_count, rank_terms, block_x, cells), jnp.float32)
+    for k in range(kt):
+        fy_e = jnp.where(fy_d == k, ry[..., k, None, None], fy_e)
+        fx_e = jnp.where(fx_d == k, rx[..., k, None, None], fx_e)
+    fxy = (fy_e[:, :, :, None, :] * fx_e[:, :, None, :, :]).reshape(tile_count, rank_terms * cells, cells)
     part = dot_rounded_data("tmk,tkz->tmz", quotient, fxy, False)
     part = part.reshape(tile_count, rank_terms, cells, depth)
     correction = jnp.einsum("tqmz,tqnz->tmn", part, tz, precision=MATMUL_PRECISION)
-    weighted = (weight[:, None, None] * correction).reshape(tile_count, block_x, tile_rows, depth)
-
-    numerator = jnp.zeros((block_x, region_rows, depth), jnp.float32)
-    for j in range(tile_count):
-        current = lax.dynamic_slice_in_dim(numerator, tile_offset[j], tile_rows, 1)
-        numerator = lax.dynamic_update_slice_in_dim(numerator, current + weighted[j], tile_offset[j], 1)
-    own_numerator = lax.psum_scatter(numerator, "tile", scatter_dimension=1, tiled=True)
+    weighted = (weight[:, None, None] * correction).reshape(tile_count, tile_rows, block_x, depth)
+    rows_all = lax.broadcasted_iota(jnp.int32, (tile_count, region_rows, tile_rows), 1)
+    rows_tile = lax.broadcasted_iota(jnp.int32, (tile_count, region_rows, tile_rows), 2)
+    place = (rows_all - rows_tile == tile_offset[:, None, None]).astype(jnp.float32)
+    numerator = jnp.einsum("jYy,jyxz->Yxz", place, weighted, precision=lax.Precision.HIGHEST)
+    own_numerator = lax.psum_scatter(numerator, "tile", scatter_dimension=0, tiled=True).transpose(1, 0, 2)
 
     me = lax.axis_index("tile")
     rows = me * block_y + jnp.arange(block_y, dtype=jnp.int32)

time: 153 us -> 152 us (level)
  waiting for transfers between devices: 67.1 us -> 72.7 us
  local copies, waits for them, and re-layouts: 20 us -> 16 us
  between operations: 21.6 us -> 17.6 us
  matrix products: 13.2 us -> 16.3 us
    all_gather x1, waiting for transfers between devices: 31.7 us -> 37.2 us  [on_device(): gathered = lax.all_gather(rimmed, 'tile', axis=1, tiled=True)]
    dot_general x0 -> x1, matrix products: none -> 3.05 us  [on_device(): jnp.einsum('jYy,jyxz->Yxz', place, weighted, precision=lax.Precision.HIGH...]
    unnamed x28 -> x24, local copies, waits for them, and re-layouts: 3.18 us -> 1.27 us
    slice x34 -> x32, local copies, waits for them, and re-layouts: 3.87 us -> 3.16 us  [the longest x16 1.58 us: on_device(): fy_e = jnp.where(fy_d == k, ry[..., k, None, None], fy_e)]
    mul x2 -> x1, other arithmetic: 3.93 us -> 3.73 us  [kron_band(): return ea[..., :, None, :] * eb[..., None, :, :]]
  transfers between devices with their start and end apart: 4 -> 4, of which waited for: 4 -> 4; matrix products, arithmetic and copies ran while one was open for 14% -> 13% of each run, Pallas kernels for 0% -> 0%
where the time goes in v12:
time: 152 us; the launch traced here: 151 us
  waiting for transfers between devices  72.7 us (48%)
  between operations  17.6 us (12%)
  matrix products  16.3 us (11%)
  local copies, waits for them, and re-layouts  16 us (11%)
  other arithmetic  13.2 us (9%)
  blocking collectives  9.3 us (6%)
  starting transfers between devices  6.32 us (4%)
    all_gather x1, waiting for transfers between devices, on_device(): gathered = lax.all_gather(rimmed, 'tile', axis=1, tiled=True)  37.2 us
    reduce_scatter x1, waiting for transfers between devices, on_device(): lax.psum_scatter(numerator, 'tile', scatter_dimension=0, tiled=True)  25.1 us
    all_gather x1, blocking collectives, on_device(): all_info = lax.all_gather(tile_info, 'tile', tiled=True)  9.3 us
    ppermute x1, waiting for transfers between devices, with_halo(): lax.ppermute(head, axis, [((i + 1) % count, i) for i in range(ends)])  6.86 us
    dot_general x1, matrix products, on_device(): part = jnp.einsum('tmk,tkz->tmz', kxy, windows, precision=MATMUL_PRECISION)  6.69 us
    ppermute x1, starting transfers between devices, with_halo(): lax.ppermute(tail, axis, [(i, (i + 1) % count) for i in range(ends)])  4.99 us
    mul x1, other arithmetic, kron_band(): return ea[..., :, None, :] * eb[..., None, :, :]  3.73 us
    dot_general x4, matrix products, dot_rounded_data(): jnp.einsum(spec, a, b, preferred_element_type=jnp.float32)  3.57 us
  transfers between devices with their start and end apart: 4, of which 4 were waited for; matrix products, arithmetic and copies ran while one was open for 13% of the time, Pallas kernels for 0%

profile of v12, /device:TPU:0, one launch (start us, length us, event | category | flops | bytes accessed | tf_op | source)
XLA Modules:
  0.0 151.4 jit_solution(9300233017488999494)
XLA Ops:
  6.5 1.1 fusion.104
  7.7 5.0 %collective-permute-start = (f32[7,16,512]{2,1,0:T(8,128)S(1)}, f32[7,16,512]{2,1,0:T(8,128)S(1)}, u32[]{:S(2)}, u32[]{:S(2)}) collective-permute-start(f32[7,16,512]{2,1,0:T(8,128)S(1)} %get-tuple-element.13), channel_id=1, source_target_pairs={{0,8},{8,16},{16,24},{1,9},{9,17},{17,25},{2,10},{10,18},{18,26},{... | collective-permute-start | bytes 688136 | tf_op jit(solution)/shard_map/ppermute | solution.py:18
  12.7 1.3 collective-permute-start.1
  14.0 3.5 %collective-permute-done = f32[7,16,512]{2,1,0:T(8,128)S(1)} collective-permute-done((f32[7,16,512]{2,1,0:T(8,128)S(1)}, f32[7,16,512]{2,1,0:T(8,128)S(1)}, u32[]{:S(2)}, u32[]{:S(2)}) %collective-permute-start) | collective-permute-done | bytes 229408 | tf_op jit(solution)/shard_map/ppermute | solution.py:18
  17.5 6.9 %collective-permute-done.1 = f32[7,16,512]{2,1,0:T(8,128)S(1)} collective-permute-done((f32[7,16,512]{2,1,0:T(8,128)S(1)}, f32[7,16,512]{2,1,0:T(8,128)S(1)}, u32[]{:S(2)}, u32[]{:S(2)}) %collective-permute-start.1) | collective-permute-done | bytes 229408 | tf_op jit(solution)/shard_map/ppermute | solution.py:20
  24.4 1.9 %pad_maximum_fusion.4 = f32[22,16,512]{2,1,0:T(8,128)} fusion(f32[7,16,512]{2,1,0:T(8,128)S(1)} %collective-permute-done.1, f32[8,16,512]{2,1,0:T(8,128)} %param.6, f32[7,16,512]{2,1,0:T(8,128)S(1)} %collective-permute-done), kind=kLoop, calls=%fused_computation.50 | loop fusion | flops 360448 | bytes 1441792 | tf_op jit(solution)/shard_map/concatenate | solution.py:16
  26.4 0.6 fusion.110
  29.6 0.6 gather_fusion.1
  30.2 0.1 fusion.108
  30.3 0.1 copy.174
  30.4 0.1 copy.175
  30.5 0.1 copy.176
  30.6 0.1 copy.177
  30.7 0.1 copy.178
  30.8 0.1 copy.179
  30.9 0.1 copy.180
  31.0 0.1 copy.166
  31.8 0.1 fusion.109
  31.9 0.1 copy.182
  32.0 0.1 copy.183
  33.4 0.1 fusion.107
  33.5 0.1 copy.200
  35.0 1.1 copy.197
  36.1 0.6 gather_fusion
  38.2 0.2 select_select_fusion.4
  38.4 0.4 select_select_fusion.3
  38.8 0.6 fusion.43
  39.4 0.1 broadcast_multiply_fusion.1
  39.5 1.5 select_select_fusion
  41.0 2.4 %pad_slice_fusion.3 = (f32[2,3,512,128]{3,2,1,0:T(8,128)S(1)}, f32[2,3,512,128]{3,2,1,0:T(8,128)}, f32[2,3,512,128]{3,2,1,0:T(8,128)}, f32[2,3,512,128]{3,2,1,0:T(8,128)}) fusion(f32[2,3,384,128]{3,2,1,0:T(8,128)S(1)} %select_select_fusion), kind=kLoop, calls=%fused_computation.16 | loop fusion | bytes 7471104 | tf_op jit(solution)/shard_map/slice | solution.py:73
  43.4 0.2 fusion.11
  43.8 0.4 select_select_fusion.2
  44.1 0.7 subtract_compare_fusion.14
  44.8 1.4 select_select_fusion.1
  46.3 3.7 %broadcast_multiply_fusion = f32[2,3,8,32,1056]{4,3,2,1,0:T(8,128)} fusion(f32[2,3,32,1056]{3,2,1,0:T(8,128)S(1)} %select_select_fusion.1, f32[2,3,8,1056]{3,2,1,0:T(8,128)S(1)} %select_select_fusion.2), kind=kLoop, calls=%fused_computation.10 | loop fusion | flops 1622016 | bytes 7501824 | tf_op jit(solution)/shard_map/mul | solution.py:56
  50.0 37.2 %all-gather.3.cloned.1.call-done = f32[22,128,512]{2,1,0:T(8,128)} async-done(((f32[22,16,512]{2,1,0:T(8,128)}), f32[22,128,512]{2,1,0:T(8,128)}) %all-gather.3.cloned.1.call-update) | async-done | bytes 5767184 | tf_op jit(solution)/shard_map/all_gather | solution.py:95
  87.2 3.4 %constant_dynamic-slice_fusion.1 = (f32[22,48,512]{2,1,0:T(8,128)S(1)}, f32[22,48,512]{2,1,0:T(8,128)S(1)}) fusion(f32[22,128,512]{2,1,0:T(8,128)} %all-gather.3.cloned.1.call-done, s32[]{:T(128)S(6)} %select_n.661, s32[]{:T(128)S(6)} %select_n.662), kind=kLoop, calls=%fused_computation.155 | loop fusion | bytes 8650760 | tf_op jit(solution)/shard_map/dynamic_slice | solution.py:106
  90.5 1.0 copy-done.2
  91.6 6.7 %fusion.8 = bf16[2,768,512]{2,1,0:T(8,128)(2,1)S(1)} fusion(f32[2,768,1056]{2,1,0:T(8,128)S(1)} %bitcast.115, f32[1,1056,512]{2,1,0:T(8,128)S(1)} %bitcast.117, f32[1,1056,512]{2,1,0:T(8,128)S(1)} %bitcast.116), kind=kOutput, calls=%fused_computation.35 | convolution fusion | flops 4984700928 | bytes 12386304 | tf_op jit(solution)/shard_map/tmk,tkz->tmz/dot_general | solution.py:115
  98.3 1.2 fusion.12
  99.5 1.2 fusion.24
  100.8 0.6 fusion.111
  101.3 0.6 convolution_add_fusion
  101.9 3.0 %fusion.17 = f32[2,32,8,512]{3,2,1,0:T(8,128)S(1)} fusion(f32[2,3,256,512]{3,2,1,0:T(8,128)S(1)} %bitcast.118, f32[2,3,512,128]{3,2,1,0:T(8,128)S(1)} %copy-done.4, f32[2,3,512,128]{3,2,1,0:T(8,128)S(1)} %copy-done.5, f32[2,3,512,128]{3,2,1,0:T(8,128)S(1)} %copy-done.6, f32[2,3,512,128]{3,2,1,0:T(8,128)S(1)} %get-tuple-element.9, f32[2]{0:T(128)S(1)} %gather_fusion), kind=kOutput, calls=%fused_computation.42 | convolution fusion | flops 2420899840 | bytes 10485768 | tf_op jit(solution)/shard_map/tqmz,tqnz->tmn/dot_general | solution.py:136
  104.9 3.0 %convolution_bitcast_fusion = f32[128,8,512]{2,0,1:T(8,128)} fusion(f32[2,32,8,512]{3,2,1,0:T(8,128)S(1)} %fusion.17, s32[2]{0:T(128)S(1)} %copy-done.9), kind=kOutput, calls=%fused_computation.36 | convolution fusion | flops 402669568 | bytes 3145736 | tf_op jit(solution)/shard_map/jYy,jyxz->Yxz/dot_general | solution.py:141
  108.1 9.3 %all-gather = f32[8,2,2]{2,1,0:T(2,128)S(1)} all-gather(f32[1,2,2]{2,1,0:T(2,128)S(1)} %bitcast.202), channel_id=1, replica_groups=mesh['region'=4,'tile'=8] {'tile'}, dimensions={0}, use_global_device_ids=true | all-gather | bytes 144 | tf_op jit(solution)/shard_map/all_gather | solution.py:90
  117.8 25.1 %reduce-scatter.2.cloned.1.call-done = f32[16,8,512]{2,0,1:T(8,128)} async-done(((f32[128,8,512]{2,0,1:T(8,128)}), f32[16,8,512]{2,0,1:T(8,128)}) %reduce-scatter.2.cloned.1.call-update) | async-done | bytes 262160 | tf_op jit(solution)/shard_map/reduce_scatter | solution.py:142
  142.8 1.8 %fusion.28 = f32[8,16,512]{2,1,0:T(8,128)} fusion(f32[8,16,512]{2,1,0:T(8,128)S(1)} %copy-done.3, f32[16,8,512]{2,0,1:T(8,128)} %reduce-scatter.2.cloned.1.call-done, f32[16]{0:T(128)S(1)} %broadcast_add_fusion.2), kind=kLoop, calls=%fused_computation.52 | loop fusion | flops 196608 | bytes 786496 | tf_op jit(solution)/shard_map/div | solution.py:148
  (88 shorter events, 4.2 us)
Async XLA Ops:
  6.5 23.1 %copy-start = (f32[6,3,3,15]{3,2,1,0:T(4,128)S(1)}, f32[6,3,3,15]{3,2,1,0:T(4,128)}, u32[]{:S(2)}) copy-start(f32[6,3,3,15]{3,2,1,0:T(4,128)} %param.10) | copy-start | bytes 9724
  6.5 19.8 %copy-start.9 = (s32[2]{0:T(128)S(1)}, s32[2]{0:T(128)}, u32[]{:S(2)}) copy-start(s32[2]{0:T(128)} %param.8) | copy-start | bytes 28
  6.5 19.8 %copy-start.10 = (s32[2]{0:T(128)S(1)}, s32[2]{0:T(128)}, u32[]{:S(2)}) copy-start(s32[2]{0:T(128)} %param.9) | copy-start | bytes 28
  6.5 80.6 %all-gather.3.cloned.1.call-start = ((), (), s32[]{:S(2)}) async-start(), calls=%async_computation.1 | async-start | bytes 6488064 | tf_op jit(solution)/shard_map/all_gather | solution.py:95
  7.7 27.3 %copy-start.7 = (f32[8,2,32,512]{3,2,1,0:T(8,128)S(1)}, f32[8,2,32,512]{3,2,1,0:T(8,128)}, u32[]{:S(2)}) copy-start(f32[8,2,32,512]{3,2,1,0:T(8,128)} %param.7) | copy-start | bytes 3145732
  7.7 9.8 %collective-permute-start = (f32[7,16,512]{2,1,0:T(8,128)S(1)}, f32[7,16,512]{2,1,0:T(8,128)S(1)}, u32[]{:S(2)}, u32[]{:S(2)}) collective-permute-start(f32[7,16,512]{2,1,0:T(8,128)S(1)} %get-tuple-element.13), channel_id=1, source_target_pairs={{0,8},{8,16},{16,24},{1,9},{9,17},{17,25},{2,10},{10,18},{18,26},{... | collective-permute-start | bytes 688136 | tf_op jit(solution)/shard_map/ppermute | solution.py:18
  12.7 11.7 %collective-permute-start.1 = (f32[7,16,512]{2,1,0:T(8,128)S(1)}, f32[7,16,512]{2,1,0:T(8,128)S(1)}, u32[]{:S(2)}, u32[]{:S(2)}) collective-permute-start(f32[7,16,512]{2,1,0:T(8,128)S(1)} %get-tuple-element.14), channel_id=1, source_target_pairs={{8,0},{16,8},{24,16},{9,1},{17,9},{25,17},{10,2},{18,10},{26,18},{... | collective-permute-start | bytes 688136 | tf_op jit(solution)/shard_map/ppermute | solution.py:20
  26.3 9.8 %copy-start.1 = (f32[6]{0:T(128)S(1)}, f32[6]{0:T(128)}, u32[]{:S(2)}) copy-start(f32[6]{0:T(128)} %param.11) | copy-start | bytes 76
  26.3 116.5 %reduce-scatter.2.cloned.1.call-start = ((), (), s32[]{:S(2)}) async-start(), calls=%async_computation.2 | async-start | bytes 2359296 | tf_op jit(solution)/shard_map/reduce_scatter | solution.py:142
  87.2 4.4 %copy-start.2 = (f32[2,3,8,32,1056]{4,3,2,1,0:T(8,128)S(1)}, f32[2,3,8,32,1056]{4,3,2,1,0:T(8,128)}, u32[]{:S(2)}) copy-start(f32[2,3,8,32,1056]{4,3,2,1,0:T(8,128)} %broadcast_multiply_fusion) | copy-start | bytes 19464196
  91.6 6.7 %copy-start.4 = (f32[2,3,512,128]{3,2,1,0:T(8,128)S(1)}, f32[2,3,512,128]{3,2,1,0:T(8,128)}, u32[]{:S(2)}) copy-start(f32[2,3,512,128]{3,2,1,0:T(8,128)} %get-tuple-element.10) | copy-start | bytes 4718596
  91.6 6.7 %copy-start.5 = (f32[2,3,512,128]{3,2,1,0:T(8,128)S(1)}, f32[2,3,512,128]{3,2,1,0:T(8,128)}, u32[]{:S(2)}) copy-start(f32[2,3,512,128]{3,2,1,0:T(8,128)} %get-tuple-element.11) | copy-start | bytes 4718596
  91.6 6.7 %copy-start.6 = (f32[2,3,512,128]{3,2,1,0:T(8,128)S(1)}, f32[2,3,512,128]{3,2,1,0:T(8,128)}, u32[]{:S(2)}) copy-start(f32[2,3,512,128]{3,2,1,0:T(8,128)} %get-tuple-element.12) | copy-start | bytes 4718596
  98.3 1.2 copy-start.8
  108.0 34.9 %copy-start.3 = (f32[8,16,512]{2,1,0:T(8,128)S(1)}, f32[8,16,512]{2,1,0:T(8,128)}, u32[]{:S(2)}) copy-start(f32[8,16,512]{2,1,0:T(8,128)} %param.6) | copy-start | bytes 786436
Sparse Core Ops, SparseCore 0:
  26.4 60.6 all-gather.2
  108.1 34.6 reduce-scatter.1

commit v13 on v12

--- a/solution.py
+++ b/solution.py
@@ -138,7 +138,7 @@
     rows_all = lax.broadcasted_iota(jnp.int32, (tile_count, region_rows, tile_rows), 1)
     rows_tile = lax.broadcasted_iota(jnp.int32, (tile_count, region_rows, tile_rows), 2)
     place = (rows_all - rows_tile == tile_offset[:, None, None]).astype(jnp.float32)
-    numerator = jnp.einsum("jYy,jyxz->Yxz", place, weighted, precision=lax.Precision.HIGHEST)
+    numerator = jnp.einsum("jYy,jyxz->Yxz", place, weighted, precision=MATMUL_PRECISION)
     own_numerator = lax.psum_scatter(numerator, "tile", scatter_dimension=0, tiled=True).transpose(1, 0, 2)
 
     me = lax.axis_index("tile")

time: 152 us -> 151 us (level)
  no operation moved by 1% of the time
where the time goes in v13:
time: 151 us
  waiting for transfers between devices  72.7 us (48%)
  between operations  17.6 us (12%)
  local copies, waits for them, and re-layouts  16 us (11%)
  matrix products  15.9 us (11%)
  other arithmetic  13.2 us (9%)
  blocking collectives  9.29 us (6%)
  starting transfers between devices  6.32 us (4%)
    all_gather x1, waiting for transfers between devices, on_device(): gathered = lax.all_gather(rimmed, 'tile', axis=1, tiled=True)  37.2 us
    reduce_scatter x1, waiting for transfers between devices, on_device(): lax.psum_scatter(numerator, 'tile', scatter_dimension=0, tiled=True)  25.1 us
    all_gather x1, blocking collectives, on_device(): all_info = lax.all_gather(tile_info, 'tile', tiled=True)  9.29 us
    ppermute x1, waiting for transfers between devices, with_halo(): lax.ppermute(head, axis, [((i + 1) % count, i) for i in range(ends)])  6.86 us
    dot_general x1, matrix products, on_device(): part = jnp.einsum('tmk,tkz->tmz', kxy, windows, precision=MATMUL_PRECISION)  6.69 us
    ppermute x1, starting transfers between devices, with_halo(): lax.ppermute(tail, axis, [(i, (i + 1) % count) for i in range(ends)])  4.99 us
    mul x1, other arithmetic, kron_band(): return ea[..., :, None, :] * eb[..., None, :, :]  3.73 us
    dot_general x4, matrix products, dot_rounded_data(): jnp.einsum(spec, a, b, preferred_element_type=jnp.float32)  3.57 us
  transfers between devices with their start and end apart: 4, of which 4 were waited for; matrix products, arithmetic and copies ran while one was open for 13% of the time, Pallas kernels for 0%

profile of v13, /device:TPU:0, one launch (start us, length us, event | category | flops | bytes accessed | tf_op | source)
XLA Modules:
  0.0 151.0 jit_solution(276308969041790570)
XLA Ops:
  6.5 1.1 fusion.104
  7.7 5.0 %collective-permute-start = (f32[7,16,512]{2,1,0:T(8,128)S(1)}, f32[7,16,512]{2,1,0:T(8,128)S(1)}, u32[]{:S(2)}, u32[]{:S(2)}) collective-permute-start(f32[7,16,512]{2,1,0:T(8,128)S(1)} %get-tuple-element.13), channel_id=1, source_target_pairs={{0,8},{8,16},{16,24},{1,9},{9,17},{17,25},{2,10},{10,18},{18,26},{... | collective-permute-start | bytes 688136 | tf_op jit(solution)/shard_map/ppermute | solution.py:18
  12.7 1.3 collective-permute-start.1
  14.0 3.5 %collective-permute-done = f32[7,16,512]{2,1,0:T(8,128)S(1)} collective-permute-done((f32[7,16,512]{2,1,0:T(8,128)S(1)}, f32[7,16,512]{2,1,0:T(8,128)S(1)}, u32[]{:S(2)}, u32[]{:S(2)}) %collective-permute-start) | collective-permute-done | bytes 229408 | tf_op jit(solution)/shard_map/ppermute | solution.py:18
  17.5 6.9 %collective-permute-done.1 = f32[7,16,512]{2,1,0:T(8,128)S(1)} collective-permute-done((f32[7,16,512]{2,1,0:T(8,128)S(1)}, f32[7,16,512]{2,1,0:T(8,128)S(1)}, u32[]{:S(2)}, u32[]{:S(2)}) %collective-permute-start.1) | collective-permute-done | bytes 229408 | tf_op jit(solution)/shard_map/ppermute | solution.py:20
  24.4 1.9 %pad_maximum_fusion.4 = f32[22,16,512]{2,1,0:T(8,128)} fusion(f32[7,16,512]{2,1,0:T(8,128)S(1)} %collective-permute-done.1, f32[8,16,512]{2,1,0:T(8,128)} %param.6, f32[7,16,512]{2,1,0:T(8,128)S(1)} %collective-permute-done), kind=kLoop, calls=%fused_computation.50 | loop fusion | flops 360448 | bytes 1441792 | tf_op jit(solution)/shard_map/concatenate | solution.py:16
  26.4 0.6 fusion.110
  29.6 0.6 gather_fusion.1
  30.2 0.1 fusion.108
  30.3 0.1 copy.174
  30.6 0.1 copy.177
  30.7 0.1 copy.178
  30.8 0.1 copy.179
  30.9 0.1 copy.180
  31.0 0.1 copy.166
  31.1 0.1 copy.167
  31.2 0.1 copy.168
  31.8 0.1 fusion.109
  31.9 0.1 copy.182
  32.0 0.1 copy.183
  33.4 0.1 fusion.107
  33.5 0.1 copy.200
  35.0 1.1 copy.197
  36.1 0.6 gather_fusion
  38.2 0.2 select_select_fusion.4
  38.4 0.4 select_select_fusion.3
  38.8 0.6 fusion.43
  39.4 0.1 broadcast_multiply_fusion.1
  39.5 1.5 select_select_fusion
  41.0 2.4 %pad_slice_fusion.3 = (f32[2,3,512,128]{3,2,1,0:T(8,128)S(1)}, f32[2,3,512,128]{3,2,1,0:T(8,128)}, f32[2,3,512,128]{3,2,1,0:T(8,128)}, f32[2,3,512,128]{3,2,1,0:T(8,128)}) fusion(f32[2,3,384,128]{3,2,1,0:T(8,128)S(1)} %select_select_fusion), kind=kLoop, calls=%fused_computation.16 | loop fusion | bytes 7471104 | tf_op jit(solution)/shard_map/slice | solution.py:73
  43.4 0.2 fusion.11
  43.8 0.4 select_select_fusion.2
  44.1 0.7 subtract_compare_fusion.14
  44.8 1.4 select_select_fusion.1
  46.3 3.7 %broadcast_multiply_fusion = f32[2,3,8,32,1056]{4,3,2,1,0:T(8,128)} fusion(f32[2,3,32,1056]{3,2,1,0:T(8,128)S(1)} %select_select_fusion.1, f32[2,3,8,1056]{3,2,1,0:T(8,128)S(1)} %select_select_fusion.2), kind=kLoop, calls=%fused_computation.10 | loop fusion | flops 1622016 | bytes 7501824 | tf_op jit(solution)/shard_map/mul | solution.py:56
  50.0 37.2 %all-gather.3.cloned.1.call-done = f32[22,128,512]{2,1,0:T(8,128)} async-done(((f32[22,16,512]{2,1,0:T(8,128)}), f32[22,128,512]{2,1,0:T(8,128)}) %all-gather.3.cloned.1.call-update) | async-done | bytes 5767184 | tf_op jit(solution)/shard_map/all_gather | solution.py:95
  87.2 3.4 %constant_dynamic-slice_fusion.1 = (f32[22,48,512]{2,1,0:T(8,128)S(1)}, f32[22,48,512]{2,1,0:T(8,128)S(1)}) fusion(f32[22,128,512]{2,1,0:T(8,128)} %all-gather.3.cloned.1.call-done, s32[]{:T(128)S(6)} %select_n.661, s32[]{:T(128)S(6)} %select_n.662), kind=kLoop, calls=%fused_computation.155 | loop fusion | bytes 8650760 | tf_op jit(solution)/shard_map/dynamic_slice | solution.py:106
  90.5 1.0 copy-done.2
  91.6 6.7 %fusion.8 = bf16[2,768,512]{2,1,0:T(8,128)(2,1)S(1)} fusion(f32[2,768,1056]{2,1,0:T(8,128)S(1)} %bitcast.115, f32[1,1056,512]{2,1,0:T(8,128)S(1)} %bitcast.117, f32[1,1056,512]{2,1,0:T(8,128)S(1)} %bitcast.116), kind=kOutput, calls=%fused_computation.35 | convolution fusion | flops 4984700928 | bytes 12386304 | tf_op jit(solution)/shard_map/tmk,tkz->tmz/dot_general | solution.py:115
  98.3 1.2 fusion.12
  99.5 1.2 fusion.24
  100.8 0.6 fusion.111
  101.3 0.6 convolution_add_fusion
  101.9 3.0 %fusion.17 = f32[2,32,8,512]{3,2,1,0:T(8,128)S(1)} fusion(f32[2,3,256,512]{3,2,1,0:T(8,128)S(1)} %bitcast.118, f32[2,3,512,128]{3,2,1,0:T(8,128)S(1)} %copy-done.4, f32[2,3,512,128]{3,2,1,0:T(8,128)S(1)} %copy-done.5, f32[2,3,512,128]{3,2,1,0:T(8,128)S(1)} %copy-done.6, f32[2,3,512,128]{3,2,1,0:T(8,128)S(1)} %get-tuple-element.9, f32[2]{0:T(128)S(1)} %gather_fusion), kind=kOutput, calls=%fused_computation.42 | convolution fusion | flops 2420899840 | bytes 10485768 | tf_op jit(solution)/shard_map/tqmz,tqnz->tmn/dot_general | solution.py:136
  104.9 2.6 %convolution_bitcast_fusion = f32[128,8,512]{2,0,1:T(8,128)} fusion(f32[2,32,8,512]{3,2,1,0:T(8,128)S(1)} %fusion.17, s32[2]{0:T(128)S(1)} %copy-done.9), kind=kOutput, calls=%fused_computation.36 | convolution fusion | flops 201342976 | bytes 3145736 | tf_op jit(solution)/shard_map/jYy,jyxz->Yxz/dot_general | solution.py:141
  107.7 9.3 %all-gather = f32[8,2,2]{2,1,0:T(2,128)S(1)} all-gather(f32[1,2,2]{2,1,0:T(2,128)S(1)} %bitcast.202), channel_id=1, replica_groups=mesh['region'=4,'tile'=8] {'tile'}, dimensions={0}, use_global_device_ids=true | all-gather | bytes 144 | tf_op jit(solution)/shard_map/all_gather | solution.py:90
  117.3 25.1 %reduce-scatter.2.cloned.1.call-done = f32[16,8,512]{2,0,1:T(8,128)} async-done(((f32[128,8,512]{2,0,1:T(8,128)}), f32[16,8,512]{2,0,1:T(8,128)}) %reduce-scatter.2.cloned.1.call-update) | async-done | bytes 262160 | tf_op jit(solution)/shard_map/reduce_scatter | solution.py:142
  142.4 1.8 %fusion.28 = f32[8,16,512]{2,1,0:T(8,128)} fusion(f32[8,16,512]{2,1,0:T(8,128)S(1)} %copy-done.3, f32[16,8,512]{2,0,1:T(8,128)} %reduce-scatter.2.cloned.1.call-done, f32[16]{0:T(128)S(1)} %broadcast_add_fusion.2), kind=kLoop, calls=%fused_computation.52 | loop fusion | flops 196608 | bytes 786496 | tf_op jit(solution)/shard_map/div | solution.py:148
  (88 shorter events, 4.2 us)
Async XLA Ops:
  6.5 23.1 %copy-start = (f32[6,3,3,15]{3,2,1,0:T(4,128)S(1)}, f32[6,3,3,15]{3,2,1,0:T(4,128)}, u32[]{:S(2)}) copy-start(f32[6,3,3,15]{3,2,1,0:T(4,128)} %param.10) | copy-start | bytes 9724
  6.5 19.8 %copy-start.9 = (s32[2]{0:T(128)S(1)}, s32[2]{0:T(128)}, u32[]{:S(2)}) copy-start(s32[2]{0:T(128)} %param.8) | copy-start | bytes 28
  6.5 19.8 %copy-start.10 = (s32[2]{0:T(128)S(1)}, s32[2]{0:T(128)}, u32[]{:S(2)}) copy-start(s32[2]{0:T(128)} %param.9) | copy-start | bytes 28
  6.5 80.6 %all-gather.3.cloned.1.call-start = ((), (), s32[]{:S(2)}) async-start(), calls=%async_computation.1 | async-start | bytes 6488064 | tf_op jit(solution)/shard_map/all_gather | solution.py:95
  7.7 27.3 %copy-start.7 = (f32[8,2,32,512]{3,2,1,0:T(8,128)S(1)}, f32[8,2,32,512]{3,2,1,0:T(8,128)}, u32[]{:S(2)}) copy-start(f32[8,2,32,512]{3,2,1,0:T(8,128)} %param.7) | copy-start | bytes 3145732
  7.7 9.8 %collective-permute-start = (f32[7,16,512]{2,1,0:T(8,128)S(1)}, f32[7,16,512]{2,1,0:T(8,128)S(1)}, u32[]{:S(2)}, u32[]{:S(2)}) collective-permute-start(f32[7,16,512]{2,1,0:T(8,128)S(1)} %get-tuple-element.13), channel_id=1, source_target_pairs={{0,8},{8,16},{16,24},{1,9},{9,17},{17,25},{2,10},{10,18},{18,26},{... | collective-permute-start | bytes 688136 | tf_op jit(solution)/shard_map/ppermute | solution.py:18
  12.7 11.7 %collective-permute-start.1 = (f32[7,16,512]{2,1,0:T(8,128)S(1)}, f32[7,16,512]{2,1,0:T(8,128)S(1)}, u32[]{:S(2)}, u32[]{:S(2)}) collective-permute-start(f32[7,16,512]{2,1,0:T(8,128)S(1)} %get-tuple-element.14), channel_id=1, source_target_pairs={{8,0},{16,8},{24,16},{9,1},{17,9},{25,17},{10,2},{18,10},{26,18},{... | collective-permute-start | bytes 688136 | tf_op jit(solution)/shard_map/ppermute | solution.py:20
  26.3 9.8 %copy-start.1 = (f32[6]{0:T(128)S(1)}, f32[6]{0:T(128)}, u32[]{:S(2)}) copy-start(f32[6]{0:T(128)} %param.11) | copy-start | bytes 76
  26.3 116.1 %reduce-scatter.2.cloned.1.call-start = ((), (), s32[]{:S(2)}) async-start(), calls=%async_computation.2 | async-start | bytes 2359296 | tf_op jit(solution)/shard_map/reduce_scatter | solution.py:142
  87.2 4.4 %copy-start.2 = (f32[2,3,8,32,1056]{4,3,2,1,0:T(8,128)S(1)}, f32[2,3,8,32,1056]{4,3,2,1,0:T(8,128)}, u32[]{:S(2)}) copy-start(f32[2,3,8,32,1056]{4,3,2,1,0:T(8,128)} %broadcast_multiply_fusion) | copy-start | bytes 19464196
  91.6 6.7 %copy-start.4 = (f32[2,3,512,128]{3,2,1,0:T(8,128)S(1)}, f32[2,3,512,128]{3,2,1,0:T(8,128)}, u32[]{:S(2)}) copy-start(f32[2,3,512,128]{3,2,1,0:T(8,128)} %get-tuple-element.10) | copy-start | bytes 4718596
  91.6 6.7 %copy-start.5 = (f32[2,3,512,128]{3,2,1,0:T(8,128)S(1)}, f32[2,3,512,128]{3,2,1,0:T(8,128)}, u32[]{:S(2)}) copy-start(f32[2,3,512,128]{3,2,1,0:T(8,128)} %get-tuple-element.11) | copy-start | bytes 4718596
  91.6 6.7 %copy-start.6 = (f32[2,3,512,128]{3,2,1,0:T(8,128)S(1)}, f32[2,3,512,128]{3,2,1,0:T(8,128)}, u32[]{:S(2)}) copy-start(f32[2,3,512,128]{3,2,1,0:T(8,128)} %get-tuple-element.12) | copy-start | bytes 4718596
  98.3 1.2 copy-start.8
  107.5 34.9 %copy-start.3 = (f32[8,16,512]{2,1,0:T(8,128)S(1)}, f32[8,16,512]{2,1,0:T(8,128)}, u32[]{:S(2)}) copy-start(f32[8,16,512]{2,1,0:T(8,128)} %param.6) | copy-start | bytes 786436
Sparse Core Ops, SparseCore 0:
  26.4 60.6 all-gather.2
  107.7 34.6 reduce-scatter.1

commit v14 on v13

--- a/solution.py
+++ b/solution.py
@@ -145,7 +145,8 @@
     rows = me * block_y + jnp.arange(block_y, dtype=jnp.int32)
     inside = (rows[None, :] >= all_offset[:, None]) & (rows[None, :] < all_offset[:, None] + tile_rows)
     own_coverage = jnp.sum(jnp.where(inside, all_weight[:, None], 0.0), axis=0)
-    return estimate * (own_numerator + PRIOR_WEIGHT) / (own_coverage[None, :, None] + PRIOR_WEIGHT)
+    scale = lax.optimization_barrier(estimate / (own_coverage[None, :, None] + PRIOR_WEIGHT))
+    return scale * (own_numerator + PRIOR_WEIGHT)
 
 
 def solution(mesh):

time: 151 us -> 151 us (level)
    mul x0 -> x1, other arithmetic: none -> 1.71 us  [on_device(): return scale * (own_numerator + PRIOR_WEIGHT)]
    div x1, other arithmetic: 1.75 us -> 0.09 us  [on_device(): estimate / (own_coverage[None, :, None] + PRIOR_WEIGHT)]
where the time goes in v14:
time: 151 us
  waiting for transfers between devices  72.3 us (48%)
  between operations  17.6 us (12%)
  local copies, waits for them, and re-layouts  16.1 us (11%)
  matrix products  15.9 us (11%)
  other arithmetic  13.3 us (9%)
  blocking collectives  9.17 us (6%)
  starting transfers between devices  6.32 us (4%)
    all_gather x1, waiting for transfers between devices, on_device(): gathered = lax.all_gather(rimmed, 'tile', axis=1, tiled=True)  37.2 us
    reduce_scatter x1, waiting for transfers between devices, on_device(): lax.psum_scatter(numerator, 'tile', scatter_dimension=0, tiled=True)  24.8 us
    all_gather x1, blocking collectives, on_device(): all_info = lax.all_gather(tile_info, 'tile', tiled=True)  9.17 us
    ppermute x1, waiting for transfers between devices, with_halo(): lax.ppermute(head, axis, [((i + 1) % count, i) for i in range(ends)])  6.86 us
    dot_general x1, matrix products, on_device(): part = jnp.einsum('tmk,tkz->tmz', kxy, windows, precision=MATMUL_PRECISION)  6.69 us
    ppermute x1, starting transfers between devices, with_halo(): lax.ppermute(tail, axis, [(i, (i + 1) % count) for i in range(ends)])  4.99 us
    mul x1, other arithmetic, kron_band(): return ea[..., :, None, :] * eb[..., None, :, :]  3.73 us
    dot_general x4, matrix products, dot_rounded_data(): jnp.einsum(spec, a, b, preferred_element_type=jnp.float32)  3.57 us
  transfers between devices with their start and end apart: 4, of which 4 were waited for; matrix products, arithmetic and copies ran while one was open for 13% of the time, Pallas kernels for 0%

profile of v14, /device:TPU:0, one launch (start us, length us, event | category | flops | bytes accessed | tf_op | source)
XLA Modules:
  0.0 150.7 jit_solution(18136579271497681693)
XLA Ops:
  6.5 1.1 fusion.103
  7.7 5.0 %collective-permute-start = (f32[7,16,512]{2,1,0:T(8,128)S(1)}, f32[7,16,512]{2,1,0:T(8,128)S(1)}, u32[]{:S(2)}, u32[]{:S(2)}) collective-permute-start(f32[7,16,512]{2,1,0:T(8,128)S(1)} %get-tuple-element.13), channel_id=1, source_target_pairs={{0,8},{8,16},{16,24},{1,9},{9,17},{17,25},{2,10},{10,18},{18,26},{... | collective-permute-start | bytes 688136 | tf_op jit(solution)/shard_map/ppermute | solution.py:18
  12.7 1.3 collective-permute-start.1
  14.0 3.5 %collective-permute-done = f32[7,16,512]{2,1,0:T(8,128)S(1)} collective-permute-done((f32[7,16,512]{2,1,0:T(8,128)S(1)}, f32[7,16,512]{2,1,0:T(8,128)S(1)}, u32[]{:S(2)}, u32[]{:S(2)}) %collective-permute-start) | collective-permute-done | bytes 229408 | tf_op jit(solution)/shard_map/ppermute | solution.py:18
  17.5 6.9 %collective-permute-done.1 = f32[7,16,512]{2,1,0:T(8,128)S(1)} collective-permute-done((f32[7,16,512]{2,1,0:T(8,128)S(1)}, f32[7,16,512]{2,1,0:T(8,128)S(1)}, u32[]{:S(2)}, u32[]{:S(2)}) %collective-permute-start.1) | collective-permute-done | bytes 229408 | tf_op jit(solution)/shard_map/ppermute | solution.py:20
  24.4 1.9 %pad_maximum_fusion.4 = f32[22,16,512]{2,1,0:T(8,128)} fusion(f32[7,16,512]{2,1,0:T(8,128)S(1)} %collective-permute-done.1, f32[8,16,512]{2,1,0:T(8,128)} %param.6, f32[7,16,512]{2,1,0:T(8,128)S(1)} %collective-permute-done), kind=kLoop, calls=%fused_computation.50 | loop fusion | flops 360448 | bytes 1441792 | tf_op jit(solution)/shard_map/concatenate | solution.py:16
  26.4 0.6 fusion.109
  29.6 0.6 gather_fusion.1
  30.2 0.1 fusion.107
  30.3 0.1 copy.169
  30.4 0.1 copy.170
  30.5 0.1 copy.171
  30.6 0.1 copy.172
  31.0 0.1 copy.176
  31.1 0.1 copy.177
  31.2 0.1 copy.178
  31.3 0.1 copy.179
  31.8 0.1 fusion.108
  31.9 0.1 copy.184
  32.0 0.1 copy.185
  33.4 0.1 fusion.106
  33.5 0.1 copy.202
  35.0 1.1 copy.199
  36.1 0.6 gather_fusion
  38.2 0.2 select_select_fusion.4
  38.4 0.4 select_select_fusion.3
  38.8 0.6 fusion.42
  39.4 0.1 broadcast_multiply_fusion.1
  39.5 1.5 select_select_fusion
  41.0 2.4 %pad_slice_fusion.3 = (f32[2,3,512,128]{3,2,1,0:T(8,128)S(1)}, f32[2,3,512,128]{3,2,1,0:T(8,128)}, f32[2,3,512,128]{3,2,1,0:T(8,128)}, f32[2,3,512,128]{3,2,1,0:T(8,128)}) fusion(f32[2,3,384,128]{3,2,1,0:T(8,128)S(1)} %select_select_fusion), kind=kLoop, calls=%fused_computation.16 | loop fusion | bytes 7471104 | tf_op jit(solution)/shard_map/slice | solution.py:73
  43.4 0.2 fusion.11
  43.8 0.4 select_select_fusion.2
  44.1 0.7 subtract_compare_fusion.14
  44.8 1.4 select_select_fusion.1
  46.3 3.7 %broadcast_multiply_fusion = f32[2,3,8,32,1056]{4,3,2,1,0:T(8,128)} fusion(f32[2,3,32,1056]{3,2,1,0:T(8,128)S(1)} %select_select_fusion.1, f32[2,3,8,1056]{3,2,1,0:T(8,128)S(1)} %select_select_fusion.2), kind=kLoop, calls=%fused_computation.10 | loop fusion | flops 1622016 | bytes 7501824 | tf_op jit(solution)/shard_map/mul | solution.py:56
  50.0 37.2 %all-gather.3.cloned.1.call-done = f32[22,128,512]{2,1,0:T(8,128)} async-done(((f32[22,16,512]{2,1,0:T(8,128)}), f32[22,128,512]{2,1,0:T(8,128)}) %all-gather.3.cloned.1.call-update) | async-done | bytes 5767184 | tf_op jit(solution)/shard_map/all_gather | solution.py:95
  87.2 3.5 %constant_dynamic-slice_fusion.1 = (f32[22,48,512]{2,1,0:T(8,128)S(1)}, f32[22,48,512]{2,1,0:T(8,128)S(1)}) fusion(f32[22,128,512]{2,1,0:T(8,128)} %all-gather.3.cloned.1.call-done, s32[]{:T(128)S(6)} %select_n.662, s32[]{:T(128)S(6)} %select_n.663), kind=kLoop, calls=%fused_computation.153 | loop fusion | bytes 8650760 | tf_op jit(solution)/shard_map/dynamic_slice | solution.py:106
  90.6 1.0 copy-done.2
  91.7 6.7 %fusion.8 = bf16[2,768,512]{2,1,0:T(8,128)(2,1)S(1)} fusion(f32[2,768,1056]{2,1,0:T(8,128)S(1)} %bitcast.113, f32[1,1056,512]{2,1,0:T(8,128)S(1)} %bitcast.115, f32[1,1056,512]{2,1,0:T(8,128)S(1)} %bitcast.114), kind=kOutput, calls=%fused_computation.35 | convolution fusion | flops 4984700928 | bytes 12386304 | tf_op jit(solution)/shard_map/tmk,tkz->tmz/dot_general | solution.py:115
  98.4 1.2 fusion.12
  99.6 1.2 fusion.24
  100.9 0.6 fusion.110
  101.5 0.6 convolution_add_fusion
  102.0 3.0 %fusion.17 = f32[2,32,8,512]{3,2,1,0:T(8,128)S(1)} fusion(f32[2,3,256,512]{3,2,1,0:T(8,128)S(1)} %bitcast.116, f32[2,3,512,128]{3,2,1,0:T(8,128)S(1)} %copy-done.4, f32[2,3,512,128]{3,2,1,0:T(8,128)S(1)} %copy-done.5, f32[2,3,512,128]{3,2,1,0:T(8,128)S(1)} %copy-done.6, f32[2,3,512,128]{3,2,1,0:T(8,128)S(1)} %get-tuple-element.9, f32[2]{0:T(128)S(1)} %gather_fusion), kind=kOutput, calls=%fused_computation.42 | convolution fusion | flops 2420899840 | bytes 10485768 | tf_op jit(solution)/shard_map/tqmz,tqnz->tmn/dot_general | solution.py:136
  105.0 2.6 %convolution_bitcast_fusion = f32[128,8,512]{2,0,1:T(8,128)} fusion(f32[2,32,8,512]{3,2,1,0:T(8,128)S(1)} %fusion.17, s32[2]{0:T(128)S(1)} %copy-done.9), kind=kOutput, calls=%fused_computation.36 | convolution fusion | flops 201342976 | bytes 3145736 | tf_op jit(solution)/shard_map/jYy,jyxz->Yxz/dot_general | solution.py:141
  107.8 9.2 %all-gather = f32[8,2,2]{2,1,0:T(2,128)S(1)} all-gather(f32[1,2,2]{2,1,0:T(2,128)S(1)} %bitcast.200), channel_id=1, replica_groups=mesh['region'=4,'tile'=8] {'tile'}, dimensions={0}, use_global_device_ids=true | all-gather | bytes 144 | tf_op jit(solution)/shard_map/all_gather | solution.py:90
  117.4 24.8 %reduce-scatter.2.cloned.1.call-done = f32[16,8,512]{2,0,1:T(8,128)} async-done(((f32[128,8,512]{2,0,1:T(8,128)}), f32[16,8,512]{2,0,1:T(8,128)}) %reduce-scatter.2.cloned.1.call-update) | async-done | bytes 262160 | tf_op jit(solution)/shard_map/reduce_scatter | solution.py:142
  142.2 1.7 %bitcast_multiply_fusion = f32[8,16,512]{2,1,0:T(8,128)} fusion(f32[8,16,512]{2,1,0:T(8,128)S(1)} %broadcast_divide_fusion, f32[16,8,512]{2,0,1:T(8,128)} %reduce-scatter.2.cloned.1.call-done), kind=kLoop, calls=%fused_computation.51 | loop fusion | flops 131072 | bytes 786432 | tf_op jit(solution)/shard_map/mul | solution.py:149
  (89 shorter events, 4.3 us)
Async XLA Ops:
  6.5 23.1 %copy-start = (f32[6,3,3,15]{3,2,1,0:T(4,128)S(1)}, f32[6,3,3,15]{3,2,1,0:T(4,128)}, u32[]{:S(2)}) copy-start(f32[6,3,3,15]{3,2,1,0:T(4,128)} %param.10) | copy-start | bytes 9724
  6.5 19.8 %copy-start.9 = (s32[2]{0:T(128)S(1)}, s32[2]{0:T(128)}, u32[]{:S(2)}) copy-start(s32[2]{0:T(128)} %param.8) | copy-start | bytes 28
  6.5 19.8 %copy-start.10 = (s32[2]{0:T(128)S(1)}, s32[2]{0:T(128)}, u32[]{:S(2)}) copy-start(s32[2]{0:T(128)} %param.9) | copy-start | bytes 28
  6.5 80.6 %all-gather.3.cloned.1.call-start = ((), (), s32[]{:S(2)}) async-start(), calls=%async_computation.1 | async-start | bytes 6488064 | tf_op jit(solution)/shard_map/all_gather | solution.py:95
  7.7 27.3 %copy-start.7 = (f32[8,2,32,512]{3,2,1,0:T(8,128)S(1)}, f32[8,2,32,512]{3,2,1,0:T(8,128)}, u32[]{:S(2)}) copy-start(f32[8,2,32,512]{3,2,1,0:T(8,128)} %param.7) | copy-start | bytes 3145732
  7.7 9.8 %collective-permute-start = (f32[7,16,512]{2,1,0:T(8,128)S(1)}, f32[7,16,512]{2,1,0:T(8,128)S(1)}, u32[]{:S(2)}, u32[]{:S(2)}) collective-permute-start(f32[7,16,512]{2,1,0:T(8,128)S(1)} %get-tuple-element.13), channel_id=1, source_target_pairs={{0,8},{8,16},{16,24},{1,9},{9,17},{17,25},{2,10},{10,18},{18,26},{... | collective-permute-start | bytes 688136 | tf_op jit(solution)/shard_map/ppermute | solution.py:18
  12.7 11.7 %collective-permute-start.1 = (f32[7,16,512]{2,1,0:T(8,128)S(1)}, f32[7,16,512]{2,1,0:T(8,128)S(1)}, u32[]{:S(2)}, u32[]{:S(2)}) collective-permute-start(f32[7,16,512]{2,1,0:T(8,128)S(1)} %get-tuple-element.14), channel_id=1, source_target_pairs={{8,0},{16,8},{24,16},{9,1},{17,9},{25,17},{10,2},{18,10},{26,18},{... | collective-permute-start | bytes 688136 | tf_op jit(solution)/shard_map/ppermute | solution.py:20
  26.3 9.8 %copy-start.1 = (f32[6]{0:T(128)S(1)}, f32[6]{0:T(128)}, u32[]{:S(2)}) copy-start(f32[6]{0:T(128)} %param.11) | copy-start | bytes 76
  26.3 115.9 %reduce-scatter.2.cloned.1.call-start = ((), (), s32[]{:S(2)}) async-start(), calls=%async_computation.2 | async-start | bytes 2359296 | tf_op jit(solution)/shard_map/reduce_scatter | solution.py:142
  87.2 4.5 %copy-start.2 = (f32[2,3,8,32,1056]{4,3,2,1,0:T(8,128)S(1)}, f32[2,3,8,32,1056]{4,3,2,1,0:T(8,128)}, u32[]{:S(2)}) copy-start(f32[2,3,8,32,1056]{4,3,2,1,0:T(8,128)} %broadcast_multiply_fusion) | copy-start | bytes 19464196
  91.7 6.7 %copy-start.4 = (f32[2,3,512,128]{3,2,1,0:T(8,128)S(1)}, f32[2,3,512,128]{3,2,1,0:T(8,128)}, u32[]{:S(2)}) copy-start(f32[2,3,512,128]{3,2,1,0:T(8,128)} %get-tuple-element.10) | copy-start | bytes 4718596
  91.7 6.7 %copy-start.5 = (f32[2,3,512,128]{3,2,1,0:T(8,128)S(1)}, f32[2,3,512,128]{3,2,1,0:T(8,128)}, u32[]{:S(2)}) copy-start(f32[2,3,512,128]{3,2,1,0:T(8,128)} %get-tuple-element.11) | copy-start | bytes 4718596
  91.7 6.7 %copy-start.6 = (f32[2,3,512,128]{3,2,1,0:T(8,128)S(1)}, f32[2,3,512,128]{3,2,1,0:T(8,128)}, u32[]{:S(2)}) copy-start(f32[2,3,512,128]{3,2,1,0:T(8,128)} %get-tuple-element.12) | copy-start | bytes 4718596
  98.4 1.2 copy-start.8
  107.7 9.7 %copy-start.3 = (f32[8,16,512]{2,1,0:T(8,128)S(1)}, f32[8,16,512]{2,1,0:T(8,128)}, u32[]{:S(2)}) copy-start(f32[8,16,512]{2,1,0:T(8,128)} %param.6) | copy-start | bytes 786436
Sparse Core Ops, SparseCore 0:
  26.4 60.6 all-gather.2
  107.8 34.3 reduce-scatter.1

commit v15 on v13

--- a/solution.py
+++ b/solution.py
@@ -112,9 +112,19 @@
     tz = depth_band(az, depth, 128)
 
     cells = block_x * tile_rows
-    part = jnp.einsum("tmk,tkz->tmz", kxy, windows, precision=MATMUL_PRECISION)
-    part = part.reshape(tile_count, rank_terms, cells, depth)
-    blurred = dot_rounded_data("tqmz,tqzn->tmn", part, tz, True)
+    half_x = block_x // 2
+    span_x = half_x + 2 * rim
+    kxy6 = kxy.reshape(tile_count, rank_terms, block_x, tile_rows, win_x, win_rows)
+    blurred = []
+    for g in range(2):
+        k_g = kxy6[:, :, g * half_x : (g + 1) * half_x, :, g * half_x : g * half_x + span_x].reshape(
+            tile_count, rank_terms * half_x * tile_rows, span_x * win_rows
+        )
+        w_g = windows[:, g * half_x * win_rows : (g * half_x + span_x) * win_rows]
+        part = jnp.einsum("tmk,tkz->tmz", k_g, w_g, precision=MATMUL_PRECISION)
+        part = part.reshape(tile_count, rank_terms, half_x * tile_rows, depth)
+        blurred.append(dot_rounded_data("tqmz,tqzn->tmn", part, tz, True))
+    blurred = jnp.concatenate(blurred, axis=1)
 
     quotient = observed.transpose(1, 0, 2, 3).reshape(tile_count, cells, depth) / blurred
 

time: 151 us -> 155 us (1.026)
  waiting for transfers between devices: 72.7 us -> 34.2 us
  local copies, waits for them, and re-layouts: 16 us -> 45.8 us
  other arithmetic: 13.2 us -> 22.5 us
  blocking collectives: 9.29 us -> 11.9 us
    all_gather x1, waiting for transfers between devices: 37.2 us -> 0.01 us  [on_device(): gathered = lax.all_gather(rimmed, 'tile', axis=1, tiled=True)]
    reshape x0 -> x2, local copies, waits for them, and re-layouts: none -> 13.4 us  [on_device(): kxy6[:, :, g * half_x:(g + 1) * half_x, :, g * half_x:g * half_x + span_x]]
    slice x0 -> x1, local copies, waits for them, and re-layouts: none -> 13.2 us  [on_device(): kxy6[:, :, g * half_x:(g + 1) * half_x, :, g * half_x:g * half_x + span_x]]
    mul x1, other arithmetic: 3.73 us -> 8.76 us  [kron_band(): return ea[..., :, None, :] * eb[..., None, :, :]]
    all_gather x1, blocking collectives: 9.29 us -> 11.9 us  [on_device(): all_info = lax.all_gather(tile_info, 'tile', tiled=True)]
    dot_general x4 -> x6, matrix products: 3.57 us -> 4.83 us  [dot_rounded_data(): jnp.einsum(spec, a, b, preferred_element_type=jnp.float32)]
    dot_general x1 -> x2, matrix products: 6.69 us -> 5.89 us  [on_device(): part = jnp.einsum('tmk,tkz->tmz', k_g, w_g, precision=MATMUL_PRECISION)]
  transfers between devices with their start and end apart: 4 -> 4, of which waited for: 4 -> 3; matrix products, arithmetic and copies ran while one was open for 13% -> 37% of each run, Pallas kernels for 0% -> 0%
where the time goes in v15:
time: 155 us
  local copies, waits for them, and re-layouts  45.8 us (30%)
  waiting for transfers between devices  34.2 us (22%)
  other arithmetic  22.5 us (15%)
  between operations  17.9 us (12%)
  matrix products  16.3 us (11%)
  blocking collectives  11.9 us (8%)
  starting transfers between devices  6.19 us (4%)
    reduce_scatter x1, waiting for transfers between devices, on_device(): lax.psum_scatter(numerator, 'tile', scatter_dimension=0, tiled=True)  23.8 us
    reshape x2, local copies, waits for them, and re-layouts, on_device(): kxy6[:, :, g * half_x:(g + 1) * half_x, :, g * half_x:g * half_x + span_x]  13.4 us
    slice x1, local copies, waits for them, and re-layouts, on_device(): kxy6[:, :, g * half_x:(g + 1) * half_x, :, g * half_x:g * half_x + span_x]  13.2 us
    all_gather x1, blocking collectives, on_device(): all_info = lax.all_gather(tile_info, 'tile', tiled=True)  11.9 us
    mul x1, other arithmetic, kron_band(): return ea[..., :, None, :] * eb[..., None, :, :]  8.76 us
    ppermute x1, waiting for transfers between devices, with_halo(): lax.ppermute(head, axis, [((i + 1) % count, i) for i in range(ends)])  6.86 us
    dot_general x2, matrix products, on_device(): part = jnp.einsum('tmk,tkz->tmz', k_g, w_g, precision=MATMUL_PRECISION)  5.89 us
    ppermute x1, starting transfers between devices, with_halo(): lax.ppermute(tail, axis, [(i, (i + 1) % count) for i in range(ends)])  4.86 us
  transfers between devices with their start and end apart: 4, of which 3 were waited for; matrix products, arithmetic and copies ran while one was open for 37% of the time, Pallas kernels for 0%

profile of v15, /device:TPU:0, one launch (start us, length us, event | category | flops | bytes accessed | tf_op | source)
XLA Modules:
  0.0 154.9 jit_solution(12673401944017679916)
XLA Ops:
  6.5 1.1 fusion.94
  7.7 4.9 %collective-permute-start = (f32[7,16,512]{2,1,0:T(8,128)S(1)}, f32[7,16,512]{2,1,0:T(8,128)S(1)}, u32[]{:S(2)}, u32[]{:S(2)}) collective-permute-start(f32[7,16,512]{2,1,0:T(8,128)S(1)} %get-tuple-element.30), channel_id=1, source_target_pairs={{0,8},{8,16},{16,24},{1,9},{9,17},{17,25},{2,10},{10,18},{18,26},{... | collective-permute-start | bytes 688136 | tf_op jit(solution)/shard_map/ppermute | solution.py:18
  12.5 1.3 collective-permute-start.1
  13.8 3.5 %collective-permute-done = f32[7,16,512]{2,1,0:T(8,128)S(1)} collective-permute-done((f32[7,16,512]{2,1,0:T(8,128)S(1)}, f32[7,16,512]{2,1,0:T(8,128)S(1)}, u32[]{:S(2)}, u32[]{:S(2)}) %collective-permute-start) | collective-permute-done | bytes 229408 | tf_op jit(solution)/shard_map/ppermute | solution.py:18
  17.4 6.9 %collective-permute-done.1 = f32[7,16,512]{2,1,0:T(8,128)S(1)} collective-permute-done((f32[7,16,512]{2,1,0:T(8,128)S(1)}, f32[7,16,512]{2,1,0:T(8,128)S(1)}, u32[]{:S(2)}, u32[]{:S(2)}) %collective-permute-start.1) | collective-permute-done | bytes 229408 | tf_op jit(solution)/shard_map/ppermute | solution.py:20
  24.2 1.9 %pad_maximum_fusion.5 = f32[22,16,512]{2,1,0:T(8,128)} fusion(f32[7,16,512]{2,1,0:T(8,128)S(1)} %collective-permute-done.1, f32[8,16,512]{2,1,0:T(8,128)} %param.6, f32[7,16,512]{2,1,0:T(8,128)S(1)} %collective-permute-done), kind=kLoop, calls=%fused_computation.55 | loop fusion | flops 360448 | bytes 1441792 | tf_op jit(solution)/shard_map/concatenate | solution.py:16
  26.3 0.7 fusion.100
  29.6 0.6 gather_fusion.1
  30.2 0.1 fusion.98
  30.3 0.1 copy.176
  30.4 0.1 copy.177
  32.1 0.1 fusion.99
  33.7 0.2 fusion.49
  34.0 0.8 select_select_fusion.2
  34.8 2.0 %subtract_compare_fusion.14 = (pred[2,32,22,48]{3,2,1,0:T(8,128)(4,1)S(1)}, pred[2,32,22,48]{3,2,1,0:T(8,128)(4,1)S(1)}, pred[2,32,22,48]{3,2,1,0:T(8,128)(4,1)S...) fusion(s32[2]{0:T(128)S(1)} %get-tuple-element.143, ...), kind=kLoop, calls=%fused_computation.21 | loop fusion | flops 1081344 | bytes 1148936 | tf_op jit(solution)/shard_map/eq | solution.py:55
  36.8 2.4 %select_select_fusion = f32[2,3,32,22,48]{4,3,2,1,0:T(8,128)S(1)} fusion(f32[2,3]{1,0:T(2,128)S(1)} %bitcast.151, f32[2,3]{1,0:T(2,128)S(1)} %bitcast.153, f32[2,3]{1,0:T(2,128)S(1)} %bitcast.155, f32[2,3]{1,0:T(2,128)S(1)} %bitcast.157, f32[2,3]{1,0:T(2,128)S(1)} %bitcast.159, f32[2,3]{1,0:T(2,128)S(1)} %bitcast.161, f32[2,3]{1,0:T(2,128)S(1)} %bitcast.163, ...), kind=kLoop, calls=%fused_computation.33 | loop fusion | flops 3041280 | bytes 1825128 | tf_op jit(solution)/shard_map/jit(_where)/select_n | solution.py:55
  39.3 8.8 %broadcast_multiply_fusion = f32[2,3,8,32,22,48]{5,4,3,2,1,0:T(8,128)} fusion(f32[2,3,32,22,48]{4,3,2,1,0:T(8,128)S(1)} %select_select_fusion, f32[2,3,8,22,48]{4,3,2,1,0:T(8,128)S(1)} %select_select_fusion.2), kind=kLoop, calls=%fused_computation.2 | loop fusion | flops 1622016 | bytes 7501824 | tf_op jit(solution)/shard_map/mul | solution.py:56
  48.0 13.2 %fusion.93 = (f32[2,3,4,32,18,48]{5,4,3,2,1,0:T(8,128)}, f32[2,3,4,32,18,48]{5,4,3,2,1,0:T(8,128)}) fusion(f32[2,3,8,32,22,48]{5,4,3,2,1,0:T(8,128)} %broadcast_multiply_fusion), kind=kLoop, calls=%fused_computation.167 | loop fusion | bytes 10616832 | tf_op jit(solution)/shard_map/slice | solution.py:120
  61.2 6.0 %reshape.522 = f32[2,384,864]{2,1,0:T(8,128)S(1)} reshape(f32[2,3,4,32,18,48]{5,4,3,2,1,0:T(8,128)} %get-tuple-element.5) | data formatting | bytes 5308416 | tf_op jit(solution)/shard_map/reshape | solution.py:120
  67.2 0.1 fusion.97
  68.8 7.4 %reshape.523 = f32[2,384,864]{2,1,0:T(8,128)} reshape(f32[2,3,4,32,18,48]{5,4,3,2,1,0:T(8,128)} %get-tuple-element.6) | data formatting | bytes 5308416 | tf_op jit(solution)/shard_map/reshape | solution.py:120
  76.2 2.3 %copy.199 = f32[2,8,32,512]{3,2,1,0:T(8,128)} copy(f32[2,8,32,512]{3,2,0,1:T(8,128)} %bitcast.128) | data formatting | bytes 2097152 | tf_op jit(solution)/shard_map/transpose | solution.py:129
  78.5 0.6 gather_fusion
  80.5 0.2 select_select_fusion.4
  80.8 0.4 select_select_fusion.3
  81.2 0.6 fusion.34
  81.8 0.1 broadcast_multiply_fusion.1
  81.9 1.5 select_select_fusion.1
  83.4 3.0 %pad_slice_fusion.6 = (f32[2,3,512,128]{3,2,1,0:T(8,128)}, f32[2,3,512,128]{3,2,1,0:T(8,128)}, f32[2,3,512,128]{3,2,1,0:T(8,128)}, f32[2,3,512,128]{3,2,1,0:T(8,128)}) fusion(f32[2,3,384,128]{3,2,1,0:T(8,128)S(1)} %select_select_fusion.1), kind=kLoop, calls=%fused_computation.32 | loop fusion | bytes 7471104 | tf_op jit(solution)/shard_map/slice | solution.py:73
  86.4 1.4 fusion.6
  87.8 3.3 %constant_dynamic-slice_fusion.1 = (f32[22,48,512]{2,1,0:T(8,128)S(1)}, f32[22,48,512]{2,1,0:T(8,128)S(1)}) fusion(f32[22,128,512]{2,1,0:T(8,128)} %all-gather.3.cloned.1.call-done, s32[]{:T(128)S(6)} %select_n.677, s32[]{:T(128)S(6)} %select_n.678), kind=kLoop, calls=%fused_computation.161 | loop fusion | bytes 8650760 | tf_op jit(solution)/shard_map/dynamic_slice | solution.py:106
  91.2 2.9 %fusion.8 = bf16[2,384,512]{2,1,0:T(8,128)(2,1)S(1)} fusion(f32[2,384,864]{2,1,0:T(8,128)S(1)} %reshape.522, f32[1,1056,512]{2,1,0:T(8,128)S(1)} %bitcast.123, f32[1,1056,512]{2,1,0:T(8,128)S(1)} %bitcast.125), kind=kOutput, calls=%fused_computation.40 | convolution fusion | flops 2039709696 | bytes 7766016 | tf_op jit(solution)/shard_map/tmk,tkz->tmz/dot_general | solution.py:124
  94.1 1.2 convolution_bitcast_fusion.4
  95.3 0.8 fusion.13
  96.1 1.0 copy-done.3
  97.1 2.9 %fusion.7 = bf16[2,384,512]{2,1,0:T(8,128)(2,1)S(1)} fusion(f32[2,384,864]{2,1,0:T(8,128)S(1)} %copy-done.3, f32[1,1056,512]{2,1,0:T(8,128)S(1)} %bitcast.126, f32[1,1056,512]{2,1,0:T(8,128)S(1)} %bitcast.124), kind=kOutput, calls=%fused_computation.39 | convolution fusion | flops 2039709696 | bytes 7766016 | tf_op jit(solution)/shard_map/tmk,tkz->tmz/dot_general | solution.py:124
  100.0 0.9 convolution_bitcast_fusion.2
  101.0 0.8 fusion.14
  101.8 0.4 copy-done.4
  102.2 0.2 fusion.15
  102.4 0.9 copy-done.7
  103.3 0.6 fusion.101
  103.9 0.6 convolution_add_fusion
  104.5 3.0 %fusion.12 = f32[2,32,8,512]{3,2,1,0:T(8,128)S(1)} fusion(f32[2,3,256,512]{3,2,1,0:T(8,128)S(1)} %bitcast.127, f32[2]{0:T(128)S(1)} %gather_fusion, f32[2,3,512,128]{3,2,1,0:T(8,128)S(1)} %copy-done.9, f32[2,3,512,128]{3,2,1,0:T(8,128)S(1)} %copy-done.10, f32[2,3,512,128]{3,2,1,0:T(8,128)S(1)} %copy-done.11, f32[2,3,512,128]{3,2,1,0:T(8,128)S(1)} %copy-done.8), kind=kOutput, calls=%fused_computation.43 | convolution fusion | flops 2420899840 | bytes 10485768 | tf_op jit(solution)/shard_map/tqmz,tqnz->tmn/dot_general | solution.py:146
  107.5 2.6 %convolution_bitcast_fusion = f32[128,8,512]{2,0,1:T(8,128)} fusion(f32[2,32,8,512]{3,2,1,0:T(8,128)S(1)} %fusion.12, s32[2]{0:T(128)S(1)} %copy-done.12), kind=kOutput, calls=%fused_computation.37 | convolution fusion | flops 201342976 | bytes 3145736 | tf_op jit(solution)/shard_map/jYy,jyxz->Yxz/dot_general | solution.py:151
  110.3 11.9 %all-gather = f32[8,2,2]{2,1,0:T(2,128)S(1)} all-gather(f32[1,2,2]{2,1,0:T(2,128)S(1)} %bitcast.212), channel_id=1, replica_groups=mesh['region'=4,'tile'=8] {'tile'}, dimensions={0}, use_global_device_ids=true | all-gather | bytes 144 | tf_op jit(solution)/shard_map/all_gather | solution.py:90
  122.6 23.8 %reduce-scatter.2.cloned.1.call-done = f32[16,8,512]{2,0,1:T(8,128)} async-done(((f32[128,8,512]{2,0,1:T(8,128)}), f32[16,8,512]{2,0,1:T(8,128)}) %reduce-scatter.2.cloned.1.call-update) | async-done | bytes 262160 | tf_op jit(solution)/shard_map/reduce_scatter | solution.py:152
  146.3 1.8 %fusion.19 = f32[8,16,512]{2,1,0:T(8,128)} fusion(f32[8,16,512]{2,1,0:T(8,128)S(1)} %copy-done.5, f32[16,8,512]{2,0,1:T(8,128)} %reduce-scatter.2.cloned.1.call-done, f32[16]{0:T(128)S(1)} %broadcast_add_fusion.2), kind=kLoop, calls=%fused_computation.59 | loop fusion | flops 196608 | bytes 786496 | tf_op jit(solution)/shard_map/div | solution.py:158
  (105 shorter events, 5.3 us)
Async XLA Ops:
  6.5 23.1 %copy-start = (f32[6,3,3,15]{3,2,1,0:T(4,128)S(1)}, f32[6,3,3,15]{3,2,1,0:T(4,128)}, u32[]{:S(2)}) copy-start(f32[6,3,3,15]{3,2,1,0:T(4,128)} %param.10) | copy-start | bytes 9724
  6.5 19.7 %copy-start.12 = (s32[2]{0:T(128)S(1)}, s32[2]{0:T(128)}, u32[]{:S(2)}) copy-start(s32[2]{0:T(128)} %param.8) | copy-start | bytes 28
  6.5 19.7 %copy-start.13 = (s32[2]{0:T(128)S(1)}, s32[2]{0:T(128)}, u32[]{:S(2)}) copy-start(s32[2]{0:T(128)} %param.9) | copy-start | bytes 28
  6.5 81.2 %all-gather.3.cloned.1.call-start = ((), (), s32[]{:S(2)}) async-start(), calls=%async_computation.1 | async-start | bytes 6488064 | tf_op jit(solution)/shard_map/all_gather | solution.py:95
  7.7 9.7 %collective-permute-start = (f32[7,16,512]{2,1,0:T(8,128)S(1)}, f32[7,16,512]{2,1,0:T(8,128)S(1)}, u32[]{:S(2)}, u32[]{:S(2)}) collective-permute-start(f32[7,16,512]{2,1,0:T(8,128)S(1)} %get-tuple-element.30), channel_id=1, source_target_pairs={{0,8},{8,16},{16,24},{1,9},{9,17},{17,25},{2,10},{10,18},{18,26},{... | collective-permute-start | bytes 688136 | tf_op jit(solution)/shard_map/ppermute | solution.py:18
  12.5 11.7 %collective-permute-start.1 = (f32[7,16,512]{2,1,0:T(8,128)S(1)}, f32[7,16,512]{2,1,0:T(8,128)S(1)}, u32[]{:S(2)}, u32[]{:S(2)}) collective-permute-start(f32[7,16,512]{2,1,0:T(8,128)S(1)} %get-tuple-element.31), channel_id=1, source_target_pairs={{8,0},{16,8},{24,16},{9,1},{17,9},{25,17},{10,2},{18,10},{26,18},{... | collective-permute-start | bytes 688136 | tf_op jit(solution)/shard_map/ppermute | solution.py:20
  26.2 120.1 %reduce-scatter.2.cloned.1.call-start = ((), (), s32[]{:S(2)}) async-start(), calls=%async_computation.2 | async-start | bytes 2359296 | tf_op jit(solution)/shard_map/reduce_scatter | solution.py:152
  76.1 2.3 %copy-start.2 = (f32[6]{0:T(128)S(1)}, f32[6]{0:T(128)}, u32[]{:S(2)}) copy-start(f32[6]{0:T(128)} %param.11) | copy-start | bytes 76
  91.1 3.0 %copy-start.8 = (f32[2,3,512,128]{3,2,1,0:T(8,128)S(1)}, f32[2,3,512,128]{3,2,1,0:T(8,128)}, u32[]{:S(2)}) copy-start(f32[2,3,512,128]{3,2,1,0:T(8,128)} %get-tuple-element.11) | copy-start | bytes 4718596
  91.1 3.0 %copy-start.9 = (f32[2,3,512,128]{3,2,1,0:T(8,128)S(1)}, f32[2,3,512,128]{3,2,1,0:T(8,128)}, u32[]{:S(2)}) copy-start(f32[2,3,512,128]{3,2,1,0:T(8,128)} %get-tuple-element.12) | copy-start | bytes 4718596
  91.1 3.0 %copy-start.10 = (f32[2,3,512,128]{3,2,1,0:T(8,128)S(1)}, f32[2,3,512,128]{3,2,1,0:T(8,128)}, u32[]{:S(2)}) copy-start(f32[2,3,512,128]{3,2,1,0:T(8,128)} %get-tuple-element.13) | copy-start | bytes 4718596
  91.1 3.0 %copy-start.11 = (f32[2,3,512,128]{3,2,1,0:T(8,128)S(1)}, f32[2,3,512,128]{3,2,1,0:T(8,128)}, u32[]{:S(2)}) copy-start(f32[2,3,512,128]{3,2,1,0:T(8,128)} %get-tuple-element.14) | copy-start | bytes 4718596
  95.3 1.8 %copy-start.3 = (f32[2,384,864]{2,1,0:T(8,128)S(1)}, f32[2,384,864]{2,1,0:T(8,128)}, u32[]{:S(2)}) copy-start(f32[2,384,864]{2,1,0:T(8,128)} %reshape.523) | copy-start | bytes 7962628
  101.0 1.2 copy-start.4
  102.2 1.1 copy-start.7
  102.4 1.5 copy-start.6
  104.5 43.6 %copy-start.1 = (f32[6,3,3,15]{3,2,1,0:T(4,128)S(1)}, f32[6,3,3,15]{3,2,1,0:T(4,128)}, u32[]{:S(2)}) copy-start(f32[6,3,3,15]{3,2,1,0:T(4,128)} %param.10) | copy-start | bytes 9724
  107.5 38.8 %copy-start.5 = (f32[8,16,512]{2,1,0:T(8,128)S(1)}, f32[8,16,512]{2,1,0:T(8,128)}, u32[]{:S(2)}) copy-start(f32[8,16,512]{2,1,0:T(8,128)} %param.6) | copy-start | bytes 786436
Sparse Core Ops, SparseCore 0:
  26.3 60.6 all-gather.2
  110.3 35.9 reduce-scatter.1

commit v16 on v13

--- a/solution.py
+++ b/solution.py
@@ -30,7 +30,7 @@
 
 
 def dot_rounded_data(spec, data, taps, data_first):
-    data_high = data.astype(jnp.bfloat16)
+    data_high = lax.reduce_precision(data, exponent_bits=8, mantissa_bits=7).astype(jnp.bfloat16)
     taps_high, taps_low = split_bf16(taps)
     if data_first:
         terms = [(data_high, taps_high), (data_high, taps_low)]
@@ -112,7 +112,7 @@
     tz = depth_band(az, depth, 128)
 
     cells = block_x * tile_rows
-    part = jnp.einsum("tmk,tkz->tmz", kxy, windows, precision=MATMUL_PRECISION)
+    part = dot_rounded_data("tmk,tkz->tmz", windows, kxy, False)
     part = part.reshape(tile_count, rank_terms, cells, depth)
     blurred = dot_rounded_data("tqmz,tqzn->tmn", part, tz, True)
 

time: 151 us -> 153 us (1.013)
  waiting for transfers between devices: 72.7 us -> 64.4 us
  local copies, waits for them, and re-layouts: 16 us -> 22.8 us
  matrix products: 15.9 us -> 19.4 us
    dot_general x4 -> x6, matrix products: 3.57 us -> 13.9 us  [dot_rounded_data(): jnp.einsum(spec, a, b, preferred_element_type=jnp.float32)]
    all_gather x1, waiting for transfers between devices: 37.2 us -> 29.2 us  [on_device(): gathered = lax.all_gather(rimmed, 'tile', axis=1, tiled=True)]
    mul x0 -> x1, local copies, waits for them, and re-layouts: none -> 7.96 us  [kron_band(): return ea[..., :, None, :] * eb[..., None, :, :]]
    dot_general x1 -> x0, matrix products: 6.69 us -> none  [on_device(): part = jnp.einsum('tmk,tkz->tmz', kxy, windows, precision=MATMUL_PRECISION)]
  transfers between devices with their start and end apart: 4 -> 4, of which waited for: 4 -> 4; matrix products, arithmetic and copies ran while one was open for 13% -> 18% of each run, Pallas kernels for 0% -> 0%
where the time goes in v16:
time: 153 us
  waiting for transfers between devices  64.4 us (42%)
  local copies, waits for them, and re-layouts  22.8 us (15%)
  matrix products  19.4 us (13%)
  between operations  17.7 us (12%)
  other arithmetic  13.2 us (9%)
  blocking collectives  9.26 us (6%)
  starting transfers between devices  6.19 us (4%)
    all_gather x1, waiting for transfers between devices, on_device(): gathered = lax.all_gather(rimmed, 'tile', axis=1, tiled=True)  29.2 us
    reduce_scatter x1, waiting for transfers between devices, on_device(): lax.psum_scatter(numerator, 'tile', scatter_dimension=0, tiled=True)  24.8 us
    dot_general x6, matrix products, dot_rounded_data(): jnp.einsum(spec, a, b, preferred_element_type=jnp.float32)  13.9 us
    all_gather x1, blocking collectives, on_device(): all_info = lax.all_gather(tile_info, 'tile', tiled=True)  9.26 us
    mul x1, local copies, waits for them, and re-layouts, kron_band(): return ea[..., :, None, :] * eb[..., None, :, :]  7.96 us
    ppermute x1, waiting for transfers between devices, with_halo(): lax.ppermute(head, axis, [((i + 1) % count, i) for i in range(ends)])  6.86 us
    ppermute x1, starting transfers between devices, with_halo(): lax.ppermute(tail, axis, [(i, (i + 1) % count) for i in range(ends)])  4.86 us
    mul x1, other arithmetic, kron_band(): return ea[..., :, None, :] * eb[..., None, :, :]  3.74 us
  transfers between devices with their start and end apart: 4, of which 4 were waited for; matrix products, arithmetic and copies ran while one was open for 18% of the time, Pallas kernels for 0%

profile of v16, /device:TPU:0, one launch (start us, length us, event | category | flops | bytes accessed | tf_op | source)
XLA Modules:
  0.0 152.9 jit_solution(3515758257873410787)
XLA Ops:
  6.5 1.1 fusion.108
  7.7 4.9 %collective-permute-start = (f32[7,16,512]{2,1,0:T(8,128)S(1)}, f32[7,16,512]{2,1,0:T(8,128)S(1)}, u32[]{:S(2)}, u32[]{:S(2)}) collective-permute-start(f32[7,16,512]{2,1,0:T(8,128)S(1)} %get-tuple-element.13), channel_id=1, source_target_pairs={{0,8},{8,16},{16,24},{1,9},{9,17},{17,25},{2,10},{10,18},{18,26},{... | collective-permute-start | bytes 688136 | tf_op jit(solution)/shard_map/ppermute | solution.py:18
  12.5 1.3 collective-permute-start.1
  13.8 3.5 %collective-permute-done = f32[7,16,512]{2,1,0:T(8,128)S(1)} collective-permute-done((f32[7,16,512]{2,1,0:T(8,128)S(1)}, f32[7,16,512]{2,1,0:T(8,128)S(1)}, u32[]{:S(2)}, u32[]{:S(2)}) %collective-permute-start) | collective-permute-done | bytes 229408 | tf_op jit(solution)/shard_map/ppermute | solution.py:18
  17.4 6.9 %collective-permute-done.1 = f32[7,16,512]{2,1,0:T(8,128)S(1)} collective-permute-done((f32[7,16,512]{2,1,0:T(8,128)S(1)}, f32[7,16,512]{2,1,0:T(8,128)S(1)}, u32[]{:S(2)}, u32[]{:S(2)}) %collective-permute-start.1) | collective-permute-done | bytes 229408 | tf_op jit(solution)/shard_map/ppermute | solution.py:20
  24.2 1.9 %pad_maximum_fusion.4 = f32[22,16,512]{2,1,0:T(8,128)} fusion(f32[7,16,512]{2,1,0:T(8,128)S(1)} %collective-permute-done.1, f32[8,16,512]{2,1,0:T(8,128)} %param.6, f32[7,16,512]{2,1,0:T(8,128)S(1)} %collective-permute-done), kind=kLoop, calls=%fused_computation.54 | loop fusion | flops 360448 | bytes 1441792 | tf_op jit(solution)/shard_map/concatenate | solution.py:16
  26.2 0.6 fusion.114
  29.5 0.6 gather_fusion.1
  30.1 0.1 fusion.112
  30.2 0.1 copy.230
  30.4 0.1 copy.232
  30.7 0.1 copy.235
  30.8 0.1 copy.236
  30.9 0.1 copy.222
  31.0 0.1 copy.223
  31.1 0.1 copy.224
  31.2 0.1 copy.225
  31.7 0.1 fusion.113
  31.8 0.1 copy.238
  33.4 0.4 select_select_fusion.2
  33.8 0.7 subtract_compare_fusion.14
  34.5 1.4 select_select_fusion.1
  35.9 3.7 %broadcast_multiply_fusion = f32[2,3,8,32,1056]{4,3,2,1,0:T(8,128)} fusion(f32[2,3,32,1056]{3,2,1,0:T(8,128)S(1)} %select_select_fusion.1, f32[2,3,8,1056]{3,2,1,0:T(8,128)S(1)} %select_select_fusion.2), kind=kLoop, calls=%fused_computation.11 | loop fusion | flops 1622016 | bytes 7501824 | tf_op jit(solution)/shard_map/mul | solution.py:56
  39.7 8.0 %copy.254 = f32[2,768,1056]{1,2,0:T(8,128)} copy(f32[2,768,1056]{2,1,0:T(8,128)} %bitcast.116) | data formatting | bytes 12976128 | tf_op jit(solution)/shard_map/mul | solution.py:56
  47.6 0.1 fusion.111
  47.7 0.1 copy.257
  49.2 1.1 copy.253
  50.3 0.6 gather_fusion
  52.3 0.2 select_select_fusion.4
  52.6 0.4 select_select_fusion.3
  53.0 0.6 fusion.44
  53.5 0.1 broadcast_multiply_fusion.1
  53.7 1.5 select_select_fusion
  55.2 2.5 %pad_slice_fusion.3 = (f32[2,3,512,128]{3,2,1,0:T(8,128)S(1)}, f32[2,3,512,128]{3,2,1,0:T(8,128)}, f32[2,3,512,128]{3,2,1,0:T(8,128)}, f32[2,3,512,128]{3,2,1,0:T(8,128)}) fusion(f32[2,3,384,128]{3,2,1,0:T(8,128)S(1)} %select_select_fusion), kind=kLoop, calls=%fused_computation.20 | loop fusion | bytes 7471104 | tf_op jit(solution)/shard_map/slice | solution.py:73
  57.6 0.2 fusion.9
  57.9 29.2 %all-gather.3.cloned.1.call-done = f32[22,128,512]{2,1,0:T(8,128)} async-done(((f32[22,16,512]{2,1,0:T(8,128)}), f32[22,128,512]{2,1,0:T(8,128)}) %all-gather.3.cloned.1.call-update) | async-done | bytes 5767184 | tf_op jit(solution)/shard_map/all_gather | solution.py:95
  87.0 3.2 %constant_dynamic-slice_fusion.1 = (f32[22,48,512]{2,1,0:T(8,128)S(1)}, f32[22,48,512]{2,1,0:T(8,128)S(1)}) fusion(f32[22,128,512]{2,1,0:T(8,128)} %all-gather.3.cloned.1.call-done, s32[]{:T(128)S(6)} %select_n.661, s32[]{:T(128)S(6)} %select_n.662), kind=kLoop, calls=%fused_computation.159 | loop fusion | bytes 8650760 | tf_op jit(solution)/shard_map/dynamic_slice | solution.py:106
  90.2 5.2 %fusion.3 = f32[2,768,512]{2,1,0:T(8,128)S(1)} fusion(f32[2,768,1056]{1,2,0:T(8,128)} %copy.254, f32[1,1056,512]{2,1,0:T(8,128)S(1)} %bitcast.121, f32[1,1056,512]{2,1,0:T(8,128)S(1)} %bitcast.119), kind=kOutput, calls=%fused_computation.12 | convolution fusion | flops 1669054464 | bytes 13959168 | tf_op jit(solution)/shard_map/tmk,tkz->tmz/dot_general | solution.py:39
  95.5 3.5 %reduce-precision_convert_fusion.4 = bf16[2,768,512]{2,1,0:T(8,128)(2,1)} fusion(f32[2,768,512]{2,1,0:T(8,128)S(1)} %fusion.3, f32[2,768,1056]{1,2,0:T(8,128)S(1)} %bitcast.118, f32[1,1056,512]{2,1,0:T(8,128)S(1)} %bitcast.122, f32[1,1056,512]{2,1,0:T(8,128)S(1)} %bitcast.120), kind=kOutput, calls=%fused_computation.16 | convolution fusion | flops 1669791744 | bytes 15532032 | tf_op jit(solution)/shard_map/tmk,tkz->tmz/dot_general | solution.py:39
  99.0 2.6 %fusion.10 = f32[2,256,512]{2,1,0:T(8,128)S(1)} fusion(bf16[2,3,256,512]{3,2,1,0:T(8,128)(2,1)} %bitcast.124, f32[2,3,512,128]{3,2,1,0:T(8,128)S(1)} %copy-done.3, f32[2,3,512,128]{3,2,1,0:T(8,128)S(1)} %copy-done.4, f32[2,3,512,128]{3,2,1,0:T(8,128)S(1)} %copy-done.5, f32[2,3,512,128]{3,2,1,0:T(8,128)S(1)} %get-tuple-element.9), kind=kOutput, calls=%fused_computation.41 | convolution fusion | flops 813170688 | bytes 8912896 | tf_op jit(solution)/shard_map/tqmz,tqzn->tmn/dot_general | solution.py:39
  101.6 1.5 fusion.25
  103.1 0.6 fusion.115
  103.7 0.6 convolution_add_fusion
  104.2 2.9 %fusion.15 = f32[2,32,8,512]{3,2,1,0:T(8,128)S(1)} fusion(f32[2,3,256,512]{3,2,1,0:T(8,128)S(1)} %bitcast.123, f32[2,3,512,128]{3,2,1,0:T(8,128)S(1)} %copy-done.3, f32[2,3,512,128]{3,2,1,0:T(8,128)S(1)} %copy-done.4, f32[2,3,512,128]{3,2,1,0:T(8,128)S(1)} %copy-done.5, f32[2,3,512,128]{3,2,1,0:T(8,128)S(1)} %get-tuple-element.9, f32[2]{0:T(128)S(1)} %gather_fusion), kind=kOutput, calls=%fused_computation.45 | convolution fusion | flops 2420899840 | bytes 10485768 | tf_op jit(solution)/shard_map/tqmz,tqnz->tmn/dot_general | solution.py:136
  107.1 2.6 %convolution_bitcast_fusion = f32[128,8,512]{2,0,1:T(8,128)} fusion(f32[2,32,8,512]{3,2,1,0:T(8,128)S(1)} %fusion.15, s32[2]{0:T(128)S(1)} %copy-done.9), kind=kOutput, calls=%fused_computation.39 | convolution fusion | flops 201342976 | bytes 3145736 | tf_op jit(solution)/shard_map/jYy,jyxz->Yxz/dot_general | solution.py:141
  109.9 9.3 %all-gather = f32[8,2,2]{2,1,0:T(2,128)S(1)} all-gather(f32[1,2,2]{2,1,0:T(2,128)S(1)} %bitcast.207), channel_id=1, replica_groups=mesh['region'=4,'tile'=8] {'tile'}, dimensions={0}, use_global_device_ids=true | all-gather | bytes 144 | tf_op jit(solution)/shard_map/all_gather | solution.py:90
  119.5 24.8 %reduce-scatter.2.cloned.1.call-done = f32[16,8,512]{2,0,1:T(8,128)} async-done(((f32[128,8,512]{2,0,1:T(8,128)}), f32[16,8,512]{2,0,1:T(8,128)}) %reduce-scatter.2.cloned.1.call-update) | async-done | bytes 262160 | tf_op jit(solution)/shard_map/reduce_scatter | solution.py:142
  144.3 1.8 %fusion.29 = f32[8,16,512]{2,1,0:T(8,128)} fusion(f32[8,16,512]{2,1,0:T(8,128)S(1)} %copy-done.2, f32[16,8,512]{2,0,1:T(8,128)} %reduce-scatter.2.cloned.1.call-done, f32[16]{0:T(128)S(1)} %broadcast_add_fusion.2), kind=kLoop, calls=%fused_computation.56 | loop fusion | flops 196608 | bytes 786496 | tf_op jit(solution)/shard_map/div | solution.py:148
  (95 shorter events, 4.3 us)
Async XLA Ops:
  6.5 22.9 %copy-start = (f32[6,3,3,15]{3,2,1,0:T(4,128)S(1)}, f32[6,3,3,15]{3,2,1,0:T(4,128)}, u32[]{:S(2)}) copy-start(f32[6,3,3,15]{3,2,1,0:T(4,128)} %param.10) | copy-start | bytes 9724
  6.5 19.7 %copy-start.9 = (s32[2]{0:T(128)S(1)}, s32[2]{0:T(128)}, u32[]{:S(2)}) copy-start(s32[2]{0:T(128)} %param.8) | copy-start | bytes 28
  6.5 19.7 %copy-start.10 = (s32[2]{0:T(128)S(1)}, s32[2]{0:T(128)}, u32[]{:S(2)}) copy-start(s32[2]{0:T(128)} %param.9) | copy-start | bytes 28
  6.5 80.5 %all-gather.3.cloned.1.call-start = ((), (), s32[]{:S(2)}) async-start(), calls=%async_computation.1 | async-start | bytes 6488064 | tf_op jit(solution)/shard_map/all_gather | solution.py:95
  7.7 9.7 %collective-permute-start = (f32[7,16,512]{2,1,0:T(8,128)S(1)}, f32[7,16,512]{2,1,0:T(8,128)S(1)}, u32[]{:S(2)}, u32[]{:S(2)}) collective-permute-start(f32[7,16,512]{2,1,0:T(8,128)S(1)} %get-tuple-element.13), channel_id=1, source_target_pairs={{0,8},{8,16},{16,24},{1,9},{9,17},{17,25},{2,10},{10,18},{18,26},{... | collective-permute-start | bytes 688136 | tf_op jit(solution)/shard_map/ppermute | solution.py:18
  12.5 11.7 %collective-permute-start.1 = (f32[7,16,512]{2,1,0:T(8,128)S(1)}, f32[7,16,512]{2,1,0:T(8,128)S(1)}, u32[]{:S(2)}, u32[]{:S(2)}) collective-permute-start(f32[7,16,512]{2,1,0:T(8,128)S(1)} %get-tuple-element.14), channel_id=1, source_target_pairs={{8,0},{16,8},{24,16},{9,1},{17,9},{25,17},{10,2},{18,10},{26,18},{... | collective-permute-start | bytes 688136 | tf_op jit(solution)/shard_map/ppermute | solution.py:20
  26.2 118.1 %reduce-scatter.2.cloned.1.call-start = ((), (), s32[]{:S(2)}) async-start(), calls=%async_computation.2 | async-start | bytes 2359296 | tf_op jit(solution)/shard_map/reduce_scatter | solution.py:142
  39.7 9.6 %copy-start.7 = (f32[8,2,32,512]{3,2,1,0:T(8,128)S(1)}, f32[8,2,32,512]{3,2,1,0:T(8,128)}, u32[]{:S(2)}) copy-start(f32[8,2,32,512]{3,2,1,0:T(8,128)} %param.7) | copy-start | bytes 3145732
  47.6 2.7 %copy-start.1 = (f32[6]{0:T(128)S(1)}, f32[6]{0:T(128)}, u32[]{:S(2)}) copy-start(f32[6]{0:T(128)} %param.11) | copy-start | bytes 76
  87.0 8.4 %slice-start = ((s8[6488064]{0:T(1024)(128)(4,1)}), s8[4194304]{0:T(1024)(128)(4,1)S(1)}, s32[]{:S(2)}) async-start(s8[6488064]{0:T(1024)(128)(4,1)} %bitcast.117), calls=%async_computation.3 | async-start | bytes 8388608
  90.2 5.3 %slice-start.1 = ((s8[6488064]{0:T(1024)(128)(4,1)}), s8[2293760]{0:T(1024)(128)(4,1)S(1)}, s32[]{:S(2)}) async-start(s8[6488064]{0:T(1024)(128)(4,1)} %bitcast.117), calls=%async_computation.4 | async-start | bytes 4587520
  95.5 3.5 %copy-start.3 = (f32[2,3,512,128]{3,2,1,0:T(8,128)S(1)}, f32[2,3,512,128]{3,2,1,0:T(8,128)}, u32[]{:S(2)}) copy-start(f32[2,3,512,128]{3,2,1,0:T(8,128)} %get-tuple-element.10) | copy-start | bytes 4718596
  95.5 3.5 %copy-start.4 = (f32[2,3,512,128]{3,2,1,0:T(8,128)S(1)}, f32[2,3,512,128]{3,2,1,0:T(8,128)}, u32[]{:S(2)}) copy-start(f32[2,3,512,128]{3,2,1,0:T(8,128)} %get-tuple-element.11) | copy-start | bytes 4718596
  95.5 3.5 %copy-start.5 = (f32[2,3,512,128]{3,2,1,0:T(8,128)S(1)}, f32[2,3,512,128]{3,2,1,0:T(8,128)}, u32[]{:S(2)}) copy-start(f32[2,3,512,128]{3,2,1,0:T(8,128)} %get-tuple-element.12) | copy-start | bytes 4718596
  99.0 2.6 %copy-start.6 = (bf16[2,768,512]{2,1,0:T(8,128)(2,1)S(1)}, bf16[2,768,512]{2,1,0:T(8,128)(2,1)}, u32[]{:S(2)}) copy-start(bf16[2,768,512]{2,1,0:T(8,128)(2,1)} %reduce-precision_convert_fusion.4) | copy-start | bytes 4718596
  99.0 2.6 %copy-start.8 = (f32[2,8,32,512]{3,2,1,0:T(8,128)S(1)}, f32[2,8,32,512]{3,2,1,0:T(8,128)}, u32[]{:S(2)}) copy-start(f32[2,8,32,512]{3,2,1,0:T(8,128)} %copy.253) | copy-start | bytes 3145732
  107.1 37.2 %copy-start.2 = (f32[8,16,512]{2,1,0:T(8,128)S(1)}, f32[8,16,512]{2,1,0:T(8,128)}, u32[]{:S(2)}) copy-start(f32[8,16,512]{2,1,0:T(8,128)} %param.6) | copy-start | bytes 786436
Sparse Core Ops, SparseCore 0:
  26.3 60.6 all-gather.2
  109.9 34.3 reduce-scatter.1

commit v17 on v13

--- a/solution.py
+++ b/solution.py
@@ -138,7 +138,11 @@
     rows_all = lax.broadcasted_iota(jnp.int32, (tile_count, region_rows, tile_rows), 1)
     rows_tile = lax.broadcasted_iota(jnp.int32, (tile_count, region_rows, tile_rows), 2)
     place = (rows_all - rows_tile == tile_offset[:, None, None]).astype(jnp.float32)
-    numerator = jnp.einsum("jYy,jyxz->Yxz", place, weighted, precision=MATMUL_PRECISION)
+    data_hi, data_lo = split_bf16(weighted)
+    place = place.astype(jnp.bfloat16)
+    numerator = sum(
+        jnp.einsum("jYy,jyxz->Yxz", place, d, preferred_element_type=jnp.float32) for d in (data_hi, data_lo)
+    )
     own_numerator = lax.psum_scatter(numerator, "tile", scatter_dimension=0, tiled=True).transpose(1, 0, 2)
 
     me = lax.axis_index("tile")

time: 151 us -> 152 us (level)
    dot_general x1 -> x2, matrix products: 2.61 us -> 3.11 us  [on_device(): jnp.einsum('jYy,jyxz->Yxz', place, d, preferred_element_type=jnp.float32)]
where the time goes in v17:
time: 152 us; the launch traced here: 151 us
  waiting for transfers between devices  72.6 us (48%)
  between operations  17.6 us (12%)
  matrix products  16.4 us (11%)
  local copies, waits for them, and re-layouts  16.1 us (11%)
  other arithmetic  13.2 us (9%)
  blocking collectives  9.09 us (6%)
  starting transfers between devices  6.32 us (4%)
    all_gather x1, waiting for transfers between devices, on_device(): gathered = lax.all_gather(rimmed, 'tile', axis=1, tiled=True)  37.2 us
    reduce_scatter x1, waiting for transfers between devices, on_device(): lax.psum_scatter(numerator, 'tile', scatter_dimension=0, tiled=True)  25 us
    all_gather x1, blocking collectives, on_device(): all_info = lax.all_gather(tile_info, 'tile', tiled=True)  9.09 us
    ppermute x1, waiting for transfers between devices, with_halo(): lax.ppermute(head, axis, [((i + 1) % count, i) for i in range(ends)])  6.86 us
    dot_general x1, matrix products, on_device(): part = jnp.einsum('tmk,tkz->tmz', kxy, windows, precision=MATMUL_PRECISION)  6.69 us
    ppermute x1, starting transfers between devices, with_halo(): lax.ppermute(tail, axis, [(i, (i + 1) % count) for i in range(ends)])  4.99 us
    mul x1, other arithmetic, kron_band(): return ea[..., :, None, :] * eb[..., None, :, :]  3.73 us
    dot_general x4, matrix products, dot_rounded_data(): jnp.einsum(spec, a, b, preferred_element_type=jnp.float32)  3.56 us
  transfers between devices with their start and end apart: 4, of which 4 were waited for; matrix products, arithmetic and copies ran while one was open for 13% of the time, Pallas kernels for 0%

profile of v17, /device:TPU:0, one launch (start us, length us, event | category | flops | bytes accessed | tf_op | source)
XLA Modules:
  0.0 151.3 jit_solution(6272760728899966971)
XLA Ops:
  6.5 1.1 fusion.108
  7.7 5.0 %collective-permute-start = (f32[7,16,512]{2,1,0:T(8,128)S(1)}, f32[7,16,512]{2,1,0:T(8,128)S(1)}, u32[]{:S(2)}, u32[]{:S(2)}) collective-permute-start(f32[7,16,512]{2,1,0:T(8,128)S(1)} %get-tuple-element.13), channel_id=1, source_target_pairs={{0,8},{8,16},{16,24},{1,9},{9,17},{17,25},{2,10},{10,18},{18,26},{... | collective-permute-start | bytes 688136 | tf_op jit(solution)/shard_map/ppermute | solution.py:18
  12.7 1.3 collective-permute-start.1
  14.0 3.5 %collective-permute-done = f32[7,16,512]{2,1,0:T(8,128)S(1)} collective-permute-done((f32[7,16,512]{2,1,0:T(8,128)S(1)}, f32[7,16,512]{2,1,0:T(8,128)S(1)}, u32[]{:S(2)}, u32[]{:S(2)}) %collective-permute-start) | collective-permute-done | bytes 229408 | tf_op jit(solution)/shard_map/ppermute | solution.py:18
  17.5 6.9 %collective-permute-done.1 = f32[7,16,512]{2,1,0:T(8,128)S(1)} collective-permute-done((f32[7,16,512]{2,1,0:T(8,128)S(1)}, f32[7,16,512]{2,1,0:T(8,128)S(1)}, u32[]{:S(2)}, u32[]{:S(2)}) %collective-permute-start.1) | collective-permute-done | bytes 229408 | tf_op jit(solution)/shard_map/ppermute | solution.py:20
  24.4 1.9 %pad_maximum_fusion.4 = f32[22,16,512]{2,1,0:T(8,128)} fusion(f32[7,16,512]{2,1,0:T(8,128)S(1)} %collective-permute-done.1, f32[8,16,512]{2,1,0:T(8,128)} %param.6, f32[7,16,512]{2,1,0:T(8,128)S(1)} %collective-permute-done), kind=kLoop, calls=%fused_computation.52 | loop fusion | flops 360448 | bytes 1441792 | tf_op jit(solution)/shard_map/concatenate | solution.py:16
  26.4 0.6 fusion.114
  29.6 0.6 gather_fusion.1
  30.2 0.1 fusion.112
  30.3 0.1 copy.177
  30.4 0.1 copy.178
  31.0 0.1 copy.169
  31.3 0.1 copy.172
  31.4 0.1 copy.173
  31.5 0.1 copy.174
  31.6 0.1 copy.175
  31.8 0.1 fusion.113
  31.9 0.1 copy.185
  32.0 0.1 copy.186
  33.4 0.1 fusion.111
  33.5 0.1 copy.203
  35.0 1.1 copy.200
  36.1 0.6 gather_fusion
  38.2 0.2 select_select_fusion.4
  38.4 0.4 select_select_fusion.3
  38.8 0.6 fusion.45
  39.4 0.1 broadcast_multiply_fusion.1
  39.5 1.5 select_select_fusion
  41.0 2.4 %pad_slice_fusion.3 = (f32[2,3,512,128]{3,2,1,0:T(8,128)S(1)}, f32[2,3,512,128]{3,2,1,0:T(8,128)}, f32[2,3,512,128]{3,2,1,0:T(8,128)}, f32[2,3,512,128]{3,2,1,0:T(8,128)}) fusion(f32[2,3,384,128]{3,2,1,0:T(8,128)S(1)} %select_select_fusion), kind=kLoop, calls=%fused_computation.16 | loop fusion | bytes 7471104 | tf_op jit(solution)/shard_map/slice | solution.py:73
  43.4 0.2 fusion.11
  43.8 0.4 select_select_fusion.2
  44.1 0.7 subtract_compare_fusion.14
  44.8 1.4 select_select_fusion.1
  46.3 3.7 %broadcast_multiply_fusion = f32[2,3,8,32,1056]{4,3,2,1,0:T(8,128)} fusion(f32[2,3,32,1056]{3,2,1,0:T(8,128)S(1)} %select_select_fusion.1, f32[2,3,8,1056]{3,2,1,0:T(8,128)S(1)} %select_select_fusion.2), kind=kLoop, calls=%fused_computation.10 | loop fusion | flops 1622016 | bytes 7501824 | tf_op jit(solution)/shard_map/mul | solution.py:56
  50.0 37.2 %all-gather.3.cloned.1.call-done = f32[22,128,512]{2,1,0:T(8,128)} async-done(((f32[22,16,512]{2,1,0:T(8,128)}), f32[22,128,512]{2,1,0:T(8,128)}) %all-gather.3.cloned.1.call-update) | async-done | bytes 5767184 | tf_op jit(solution)/shard_map/all_gather | solution.py:95
  87.2 3.5 %constant_dynamic-slice_fusion.1 = (f32[22,48,512]{2,1,0:T(8,128)S(1)}, f32[22,48,512]{2,1,0:T(8,128)S(1)}) fusion(f32[22,128,512]{2,1,0:T(8,128)} %all-gather.3.cloned.1.call-done, s32[]{:T(128)S(6)} %select_n.661, s32[]{:T(128)S(6)} %select_n.662), kind=kLoop, calls=%fused_computation.160 | loop fusion | bytes 8650760 | tf_op jit(solution)/shard_map/dynamic_slice | solution.py:106
  90.6 1.0 copy-done.2
  91.7 6.7 %fusion.8 = bf16[2,768,512]{2,1,0:T(8,128)(2,1)S(1)} fusion(f32[2,768,1056]{2,1,0:T(8,128)S(1)} %bitcast.119, f32[1,1056,512]{2,1,0:T(8,128)S(1)} %bitcast.121, f32[1,1056,512]{2,1,0:T(8,128)S(1)} %bitcast.120), kind=kOutput, calls=%fused_computation.36 | convolution fusion | flops 4984700928 | bytes 12386304 | tf_op jit(solution)/shard_map/tmk,tkz->tmz/dot_general | solution.py:115
  98.4 1.2 fusion.12
  99.6 1.2 fusion.24
  100.9 0.6 fusion.115
  101.4 0.6 convolution_add_fusion
  102.0 3.0 %fusion.17 = f32[2,32,8,512]{3,2,1,0:T(8,128)S(1)} fusion(f32[2,3,256,512]{3,2,1,0:T(8,128)S(1)} %bitcast.122, f32[2,3,512,128]{3,2,1,0:T(8,128)S(1)} %copy-done.4, f32[2,3,512,128]{3,2,1,0:T(8,128)S(1)} %copy-done.5, f32[2,3,512,128]{3,2,1,0:T(8,128)S(1)} %copy-done.6, f32[2,3,512,128]{3,2,1,0:T(8,128)S(1)} %get-tuple-element.9, f32[2]{0:T(128)S(1)} %gather_fusion), kind=kOutput, calls=%fused_computation.44 | convolution fusion | flops 2420899840 | bytes 10485768 | tf_op jit(solution)/shard_map/tqmz,tqnz->tmn/dot_general | solution.py:136
  105.0 0.8 fusion.29
  105.9 2.3 %bitcast_add_fusion = f32[128,8,512]{2,0,1:T(8,128)} fusion(f32[128,8,512,1]{2,0,3,1:T(8,128)S(1)} %fusion.29, f32[2,32,8,512]{3,2,1,0:T(8,128)S(1)} %fusion.17, s32[2]{0:T(128)S(1)} %copy-done.9), kind=kOutput, calls=%fused_computation.34 | convolution fusion | flops 68452352 | bytes 5242888 | tf_op jit(solution)/shard_map/jYy,jyxz->Yxz/dot_general | solution.py:144
  108.3 9.1 %all-gather = f32[8,2,2]{2,1,0:T(2,128)S(1)} all-gather(f32[1,2,2]{2,1,0:T(2,128)S(1)} %bitcast.206), channel_id=1, replica_groups=mesh['region'=4,'tile'=8] {'tile'}, dimensions={0}, use_global_device_ids=true | all-gather | bytes 144 | tf_op jit(solution)/shard_map/all_gather | solution.py:90
  117.7 25.0 %reduce-scatter.2.cloned.1.call-done = f32[16,8,512]{2,0,1:T(8,128)} async-done(((f32[128,8,512]{2,0,1:T(8,128)}), f32[16,8,512]{2,0,1:T(8,128)}) %reduce-scatter.2.cloned.1.call-update) | async-done | bytes 262160 | tf_op jit(solution)/shard_map/reduce_scatter | solution.py:146
  142.7 1.8 %fusion.30 = f32[8,16,512]{2,1,0:T(8,128)} fusion(f32[8,16,512]{2,1,0:T(8,128)S(1)} %copy-done.3, f32[16,8,512]{2,0,1:T(8,128)} %reduce-scatter.2.cloned.1.call-done, f32[16]{0:T(128)S(1)} %broadcast_add_fusion.2), kind=kLoop, calls=%fused_computation.55 | loop fusion | flops 196608 | bytes 786496 | tf_op jit(solution)/shard_map/div | solution.py:152
  (89 shorter events, 4.3 us)
Async XLA Ops:
  6.5 23.1 %copy-start = (f32[6,3,3,15]{3,2,1,0:T(4,128)S(1)}, f32[6,3,3,15]{3,2,1,0:T(4,128)}, u32[]{:S(2)}) copy-start(f32[6,3,3,15]{3,2,1,0:T(4,128)} %param.10) | copy-start | bytes 9724
  6.5 19.8 %copy-start.9 = (s32[2]{0:T(128)S(1)}, s32[2]{0:T(128)}, u32[]{:S(2)}) copy-start(s32[2]{0:T(128)} %param.8) | copy-start | bytes 28
  6.5 19.8 %copy-start.10 = (s32[2]{0:T(128)S(1)}, s32[2]{0:T(128)}, u32[]{:S(2)}) copy-start(s32[2]{0:T(128)} %param.9) | copy-start | bytes 28
  6.5 80.6 %all-gather.3.cloned.1.call-start = ((), (), s32[]{:S(2)}) async-start(), calls=%async_computation.1 | async-start | bytes 6488064 | tf_op jit(solution)/shard_map/all_gather | solution.py:95
  7.7 27.3 %copy-start.7 = (f32[8,2,32,512]{3,2,1,0:T(8,128)S(1)}, f32[8,2,32,512]{3,2,1,0:T(8,128)}, u32[]{:S(2)}) copy-start(f32[8,2,32,512]{3,2,1,0:T(8,128)} %param.7) | copy-start | bytes 3145732
  7.7 9.8 %collective-permute-start = (f32[7,16,512]{2,1,0:T(8,128)S(1)}, f32[7,16,512]{2,1,0:T(8,128)S(1)}, u32[]{:S(2)}, u32[]{:S(2)}) collective-permute-start(f32[7,16,512]{2,1,0:T(8,128)S(1)} %get-tuple-element.13), channel_id=1, source_target_pairs={{0,8},{8,16},{16,24},{1,9},{9,17},{17,25},{2,10},{10,18},{18,26},{... | collective-permute-start | bytes 688136 | tf_op jit(solution)/shard_map/ppermute | solution.py:18
  12.7 11.7 %collective-permute-start.1 = (f32[7,16,512]{2,1,0:T(8,128)S(1)}, f32[7,16,512]{2,1,0:T(8,128)S(1)}, u32[]{:S(2)}, u32[]{:S(2)}) collective-permute-start(f32[7,16,512]{2,1,0:T(8,128)S(1)} %get-tuple-element.14), channel_id=1, source_target_pairs={{8,0},{16,8},{24,16},{9,1},{17,9},{25,17},{10,2},{18,10},{26,18},{... | collective-permute-start | bytes 688136 | tf_op jit(solution)/shard_map/ppermute | solution.py:20
  26.3 9.8 %copy-start.1 = (f32[6]{0:T(128)S(1)}, f32[6]{0:T(128)}, u32[]{:S(2)}) copy-start(f32[6]{0:T(128)} %param.11) | copy-start | bytes 76
  26.3 116.4 %reduce-scatter.2.cloned.1.call-start = ((), (), s32[]{:S(2)}) async-start(), calls=%async_computation.2 | async-start | bytes 2359296 | tf_op jit(solution)/shard_map/reduce_scatter | solution.py:146
  87.2 4.5 %copy-start.2 = (f32[2,3,8,32,1056]{4,3,2,1,0:T(8,128)S(1)}, f32[2,3,8,32,1056]{4,3,2,1,0:T(8,128)}, u32[]{:S(2)}) copy-start(f32[2,3,8,32,1056]{4,3,2,1,0:T(8,128)} %broadcast_multiply_fusion) | copy-start | bytes 19464196
  91.7 6.7 %copy-start.4 = (f32[2,3,512,128]{3,2,1,0:T(8,128)S(1)}, f32[2,3,512,128]{3,2,1,0:T(8,128)}, u32[]{:S(2)}) copy-start(f32[2,3,512,128]{3,2,1,0:T(8,128)} %get-tuple-element.10) | copy-start | bytes 4718596
  91.7 6.7 %copy-start.5 = (f32[2,3,512,128]{3,2,1,0:T(8,128)S(1)}, f32[2,3,512,128]{3,2,1,0:T(8,128)}, u32[]{:S(2)}) copy-start(f32[2,3,512,128]{3,2,1,0:T(8,128)} %get-tuple-element.11) | copy-start | bytes 4718596
  91.7 6.7 %copy-start.6 = (f32[2,3,512,128]{3,2,1,0:T(8,128)S(1)}, f32[2,3,512,128]{3,2,1,0:T(8,128)}, u32[]{:S(2)}) copy-start(f32[2,3,512,128]{3,2,1,0:T(8,128)} %get-tuple-element.12) | copy-start | bytes 4718596
  98.4 1.2 copy-start.8
  108.2 34.6 %copy-start.3 = (f32[8,16,512]{2,1,0:T(8,128)S(1)}, f32[8,16,512]{2,1,0:T(8,128)}, u32[]{:S(2)}) copy-start(f32[8,16,512]{2,1,0:T(8,128)} %param.6) | copy-start | bytes 786436
Sparse Core Ops, SparseCore 0:
  26.4 60.6 all-gather.2
  108.3 34.3 reduce-scatter.1
